TPU v7x, 32 devices: a whole 2x2x4 slice. The times are simulated.
32 devices in a mesh: blk: 8 (over z, y), harvest: 4 (over x, core).
Axes of the slice: x: 2, y: 2, z: 4, core: 2. Of those that a mesh axis runs over, the one named last changes fastest.
Arguments:
- grad_rows: bfloat16 [8192, 8192], P(('blk', 'harvest')), may hold values from -1500 to 1500
- row_weights: float32 [8192], P(('blk', 'harvest')), may hold values from 0.25 to 4
- destinations: int32 [8192, 1], P(('blk', 'harvest')), may hold values from 0 to 7; in each aligned block of 256 rows (0 to 255, 256 to 511, ...) at most 48 rows name the same one
- queries: bfloat16 [128, 8192], P(('blk', 'harvest')), may hold values from -6 to 6
- tile_pattern: int32 [8, 8], replicated, may hold values from 0 to 1, as said below
Outputs:
- scores: bfloat16 [12288, 128], P(('blk', 'harvest'))
Inputs may be any that keep to these rules, and one draw needn't show every extreme that they name: `destinations`: in the rows of one device no owner is named more than 48 times, a bound that some block reaches. tile_pattern[a, b] is 1 where the tile of query block a and owner b is scored.
All inputs are finite; a program needn't handle non-finite values.
Results may differ from a plain program's by a relative error of at most 0.0095.
Values may be sent and summed in bfloat16 or wider, within the bound.
No kernel may reach another device: no remote copies, remote signals or barrier semaphores. Data moves between devices by JAX's collectives and lax.ppermute only.
A program may use at most 128 MiB of HBM per device.

v0:
```python
import math

import jax
import jax.numpy as jnp
from jax import lax
from jax.sharding import PartitionSpec as P


def make_tile(left_rows, weight_scale, shard_rows, tile_mask):
    product = jnp.einsum("sk,pk->sp", left_rows, shard_rows, preferred_element_type=jnp.float32)
    return product * weight_scale[:, None] * tile_mask


def circulate(prepared, folding, initial):
    block_queries = lax.all_gather(prepared, "harvest", axis=0, tiled=True)
    return folding(initial, lax.all_gather(block_queries, "blk", axis=0, tiled=True), jnp.int32(0))


def local(grad_rows, row_weights, destinations, queries, tile_pattern):
    blk_count = lax.axis_size("blk")
    harv_count = lax.axis_size("harvest")
    row_count = grad_rows.shape[0]
    width = grad_rows.shape[1]
    capacity = max(3 * row_count // (2 * blk_count), 2)
    block_size = queries.shape[0] * harv_count
    query_count = block_size * blk_count
    inv_root = 1.0 / math.sqrt(width)
    squares = jnp.sum(row_weights[:, None] * jnp.square(grad_rows.astype(jnp.float32)), axis=0)
    total_sq, total_weight = lax.psum((squares, jnp.sum(row_weights)), ("blk", "harvest"))
    scaling = lax.rsqrt(total_sq / total_weight + 1e-06)
    prepared = (queries.astype(jnp.float32) * scaling).astype(jnp.bfloat16)
    owner_ids = destinations[:, 0]
    one_hot = (owner_ids[:, None] == jnp.arange(blk_count, dtype=jnp.int32)[None, :]).astype(
        jnp.int32
    )
    before = jnp.cumsum(one_hot, axis=0) - one_hot
    slot_rank = jnp.sum(before * one_hot, axis=1)
    slot_index = owner_ids * capacity + slot_rank
    weight_scale = row_weights * inv_root
    slot_total = blk_count * capacity
    bucket_rows = jnp.zeros((slot_total, width), jnp.bfloat16).at[slot_index].set(grad_rows)
    bucket_weights = jnp.zeros((slot_total,), jnp.float32).at[slot_index].set(weight_scale)
    slot_rows, slot_weights = (
        lax.all_to_all(
            bucket_rows.reshape(blk_count, capacity, width),
            "blk",
            split_axis=0,
            concat_axis=0,
            tiled=True,
        ),
        lax.all_to_all(
            bucket_weights.reshape(blk_count, capacity).astype(jnp.bfloat16),
            "blk",
            split_axis=0,
            concat_axis=0,
            tiled=True,
        ).astype(jnp.float32),
    )
    slot_rows = slot_rows.reshape(slot_total, width)
    slot_weights = slot_weights.reshape(slot_total)
    owner_index = lax.axis_index("blk")
    pattern_column = lax.dynamic_slice(tile_pattern, (0, owner_index), (blk_count, 1))[:, 0]
    query_mask = jnp.repeat(pattern_column.astype(jnp.float32), block_size)

    def fold_owner(running, shard_rows, offset):
        tile_mask = query_mask[None, :]
        tile_values = make_tile(slot_rows, slot_weights, shard_rows, tile_mask)
        return lax.dynamic_update_slice_in_dim(running, tile_values, offset, 1)

    initial = jnp.zeros((slot_total, query_count), jnp.float32)
    return circulate(prepared, fold_owner, initial).astype(jnp.bfloat16)


def solution(mesh):
    in_specs = (
        P(("blk", "harvest"), None),
        P(("blk", "harvest")),
        P(("blk", "harvest"), None),
        P(("blk", "harvest"), None),
        P(),
    )
    out_specs = P(("blk", "harvest"), None)
    return jax.shard_map(local, mesh=mesh, in_specs=in_specs, out_specs=out_specs, check_vma=False)
```

profile of v0, /device:TPU:0, one launch (start us, length us, event | category | flops | bytes accessed | tf_op | source)
XLA Modules:
  0.0 264.9 jit_solution(10223305340122949333)
XLA Ops:
  6.5 0.7 fusion.7
  7.2 0.6 reduce-window.6
  7.8 0.2 slice_reduce_fusion
  8.0 0.8 fusion.6
  8.8 0.7 compare_select_fusion
  9.5 1.3 broadcast_multiply_fusion
  10.8 1.4 scatter_custom_fusion.1
  12.2 0.7 convert_element_type.61
  12.9 7.3 %all-to-all-start.1 = ((bf16[8,1,48]{2,1,0:T(2,128)(2,1)}), bf16[8,1,48]{2,1,0:T(2,128)(2,1)S(1)}, u32[]{:S(2)}, u32[]{:S(2)}) async-start(bf16[8,1,48]{2,1,0:T(2,128)(2,1)} %convert_element_type.61), calls=%async_computation.1 | async-start | bytes 8192 | tf_op jit(solution)/shard_map/all_to_all | solution.py:51
  20.2 11.3 %scatter_custom_fusion = bf16[384,8192]{1,0:T(8,128)(2,1)} fusion(s32[256]{0:T(256)S(1)} %bitcast.23, bf16[256,8192]{1,0:T(8,128)(2,1)} %param.5, bf16[]{:T(256)} %constant.10.clone.1), kind=kCustom, calls=%fused_computation.3 | custom fusion | bytes 6291968 | tf_op jit(solution)/shard_map/scatter | solution.py:41
  31.5 6.1 %all-to-all-start = ((bf16[8,48,8192]{2,1,0:T(8,128)(2,1)}), bf16[8,48,8192]{2,1,0:T(8,128)(2,1)}, u32[]{:S(2)}, u32[]{:S(2)}) async-start(bf16[8,48,8192]{2,1,0:T(8,128)(2,1)} %bitcast.18), calls=%async_computation | async-start | bytes 12582912 | tf_op jit(solution)/shard_map/all_to_all | solution.py:44
  37.6 0.0 all-gather.3.cloned.1.call-start
  37.7 3.3 %multiply_reduce_fusion = f32[8192]{0:T(1024)S(1)} fusion(bf16[256,8192]{1,0:T(8,128)(2,1)} %param.5, f32[256]{0:T(256)S(1)} %copy-done.1), kind=kLoop, calls=%fused_computation.2 | loop fusion | flops 8380416 | bytes 4228096 | tf_op jit(solution)/shard_map/reduce_sum | solution.py:28
  41.0 154.6 %all-reduce = (f32[8192]{0:T(1024)S(1)}, f32[]{:T(128)}) all-reduce(f32[8192]{0:T(1024)S(1)} %multiply_reduce_fusion, f32[]{:T(128)} %get-tuple-element.8), channel_id=1, replica_groups=mesh['blk'=8,'harvest'=4] {'blk','harvest'}, use_global_device_ids=true, to_apply=%region_5.6 | all-reduce | flops 8193 | bytes 65544 | tf_op jit(solution)/shard_map/psum | solution.py:29
  195.6 0.7 add_rsqrt_fusion
  196.3 6.5 %all-gather = bf16[4,4,8192]{2,1,0:T(4,128)(2,1)S(1)} all-gather(bf16[1,4,8192]{2,1,0:T(4,128)(2,1)S(1)} %fusion.4), channel_id=1, replica_groups=mesh['blk'=8,'harvest'=4] {'harvest'}, dimensions={0}, use_global_device_ids=true | all-gather | bytes 327680 | tf_op jit(solution)/shard_map/all_gather | solution.py:15
  202.9 0.8 reshape.69
  203.6 0.0 all-gather.3.cloned.1.call-update
  203.7 0.2 convert_reduce_fusion.1
  203.9 0.1 broadcast_in_dim.16
  203.9 0.1 mul.61
  204.1 0.1 reshape.51
  204.1 48.1 %all-gather.3.cloned.1.call-done = bf16[128,8192]{1,0:T(8,128)(2,1)} async-done(((bf16[16,8192]{1,0:T(8,128)(2,1)}), bf16[128,8192]{1,0:T(8,128)(2,1)}) %all-gather.3.cloned.1.call-update) | async-done | bytes 2097168 | tf_op jit(solution)/shard_map/all_gather | solution.py:16
  252.2 5.8 %fusion.3 = bf16[384,128]{1,0:T(8,128)(2,1)} fusion(bf16[384,8192]{1,0:T(8,128)(2,1)} %bitcast.7, bf16[128,8192]{1,0:T(8,128)(2,1)} %all-gather.3.cloned.1.call-done, f32[128]{0:T(128)S(1)} %mul.61, f32[384]{0:T(512)S(1)} %reshape.51), kind=kOutput, calls=%fused_computation.7 | convolution fusion | flops 805453824 | bytes 8488960 | tf_op jit(solution)/shard_map/sk,pk->sp/dot_general | solution.py:10
  (13 shorter events, 0.1 us)
Async XLA Ops:
  12.9 18.5 %all-to-all-start.1 = ((bf16[8,1,48]{2,1,0:T(2,128)(2,1)}), bf16[8,1,48]{2,1,0:T(2,128)(2,1)S(1)}, u32[]{:S(2)}, u32[]{:S(2)}) async-start(bf16[8,1,48]{2,1,0:T(2,128)(2,1)} %convert_element_type.61), calls=%async_computation.1 | async-start | bytes 8192 | tf_op jit(solution)/shard_map/all_to_all | solution.py:51
  31.5 6.2 %copy-start.1 = (f32[256]{0:T(256)S(1)}, f32[256]{0:T(256)}, u32[]{:S(2)}) copy-start(f32[256]{0:T(256)} %param.6) | copy-start | bytes 3076
  31.5 164.8 %copy-start = (bf16[4,8192]{1,0:T(4,128)(2,1)S(1)}, bf16[4,8192]{1,0:T(4,128)(2,1)}, u32[]{:S(2)}) copy-start(bf16[4,8192]{1,0:T(4,128)(2,1)} %param.8) | copy-start | bytes 196612
  31.5 172.2 %copy-start.2 = (s32[8,8]{1,0:T(8,128)S(1)}, s32[8,8]{1,0:T(8,128)}, u32[]{:S(2)}) copy-start(s32[8,8]{1,0:T(8,128)} %param.9) | copy-start | bytes 772
  31.5 220.7 %all-to-all-start = ((bf16[8,48,8192]{2,1,0:T(8,128)(2,1)}), bf16[8,48,8192]{2,1,0:T(8,128)(2,1)}, u32[]{:S(2)}, u32[]{:S(2)}) async-start(bf16[8,48,8192]{2,1,0:T(8,128)(2,1)} %bitcast.18), calls=%async_computation | async-start | bytes 12582912 | tf_op jit(solution)/shard_map/all_to_all | solution.py:44
  37.6 214.6 %all-gather.3.cloned.1.call-start = ((), (), s32[]{:S(2)}) async-start(), calls=%async_computation.2 | async-start | bytes 2359296 | tf_op jit(solution)/shard_map/all_gather | solution.py:16
Sparse Core Ops, SparseCore 0:
  203.8 48.3 all-gather.2
where the time goes:
time: 265 us
  blocking collectives  161 us (61%)
  waiting for transfers between devices  48.1 us (18%)
  local copies, waits for them, and re-layouts  14.6 us (6%)
  starting transfers between devices  13.5 us (5%)
  between operations  13.5 us (5%)
  other arithmetic  8.31 us (3%)
  matrix products  5.85 us (2%)
    psum x1, blocking collectives, local(): lax.psum((squares, jnp.sum(row_weights)), ('blk', 'harvest'))  155 us
    all_gather x1, waiting for transfers between devices, circulate(): lax.all_gather(block_queries, 'blk', axis=0, tiled=True)  48.1 us
    scatter x1, local copies, waits for them, and re-layouts, local(): jnp.zeros((slot_total, width), jnp.bfloat16).at[slot_index].set(grad_rows)  11.3 us
    all_to_all x1, starting transfers between devices, local(): lax.all_to_all(bucket_weights.reshape(blk_count, capacity).astype(jnp.bfl...  7.28 us
    all_gather x1, blocking collectives, circulate(): block_queries = lax.all_gather(prepared, 'harvest', axis=0, tiled=True)  6.53 us
    all_to_all x1, starting transfers between devices, local(): lax.all_to_all(bucket_rows.reshape(blk_count, capacity, width), 'blk', sp...  6.14 us
    dot_general x1, matrix products, make_tile(): jnp.einsum('sk,pk->sp', left_rows, shard_rows, preferred_element_type=jnp...  5.85 us
  transfers between devices with their start and end apart: 3, of which 1 were waited for; matrix products, arithmetic and copies ran while one was open for 6% of the time, Pallas kernels for 0%

commit v1 on v0

v1 whole, which is shorter than its diff:
```python
import math

import jax
import jax.numpy as jnp
from jax import lax
from jax.sharding import PartitionSpec as P


def local(grad_rows, row_weights, destinations, queries, tile_pattern):
    blk_count = lax.axis_size("blk")
    harv_count = lax.axis_size("harvest")
    row_count = grad_rows.shape[0]
    width = grad_rows.shape[1]
    capacity = max(3 * row_count // (2 * blk_count), 2)
    block_size = queries.shape[0] * harv_count
    slot_total = blk_count * capacity
    inv_root = 1.0 / math.sqrt(width)

    all_queries = lax.all_gather(queries, ("blk", "harvest"), axis=0, tiled=True)
    query_count = all_queries.shape[0]

    squares = jnp.sum(row_weights[:, None] * jnp.square(grad_rows.astype(jnp.float32)), axis=0)
    total_sq, total_weight = lax.psum((squares, jnp.sum(row_weights)), ("blk", "harvest"))
    scaling = lax.rsqrt(total_sq / total_weight + 1e-06)
    prepared = (all_queries.astype(jnp.float32) * scaling).astype(jnp.bfloat16)

    raw = jnp.einsum("rk,qk->rq", grad_rows, prepared, preferred_element_type=jnp.float32)
    owner_ids = destinations[:, 0]
    pattern_rows = jnp.take(tile_pattern.T, owner_ids, axis=0).astype(jnp.float32)
    full_mask = jnp.repeat(pattern_rows, block_size, axis=1)
    weight_scale = row_weights * inv_root
    value = (raw * weight_scale[:, None] * full_mask).astype(jnp.bfloat16)

    one_hot = (owner_ids[:, None] == jnp.arange(blk_count, dtype=jnp.int32)[None, :]).astype(jnp.int32)
    before = jnp.cumsum(one_hot, axis=0) - one_hot
    slot_rank = jnp.sum(before * one_hot, axis=1)
    slot_index = owner_ids * capacity + slot_rank
    placement = (jnp.arange(slot_total, dtype=jnp.int32)[:, None] == slot_index[None, :]).astype(jnp.bfloat16)
    bucket = jnp.dot(placement, value, preferred_element_type=jnp.float32).astype(jnp.bfloat16)

    received = lax.all_to_all(
        bucket.reshape(blk_count, capacity, query_count), "blk", split_axis=0, concat_axis=0, tiled=True
    )
    return received.reshape(slot_total, query_count)


def solution(mesh):
    in_specs = (
        P(("blk", "harvest"), None),
        P(("blk", "harvest")),
        P(("blk", "harvest"), None),
        P(("blk", "harvest"), None),
        P(),
    )
    out_specs = P(("blk", "harvest"), None)
    return jax.shard_map(local, mesh=mesh, in_specs=in_specs, out_specs=out_specs, check_vma=False)
```

time: 265 us -> 98.1 us (0.37)
  blocking collectives: 161 us -> 54.2 us
  waiting for transfers between devices: 48.1 us -> 10.8 us
  starting transfers between devices: 13.5 us -> 0.01 us
  local copies, waits for them, and re-layouts: 14.6 us -> 6.64 us
    psum x1, blocking collectives: 155 us -> 42.9 us  [local(): lax.psum((squares, jnp.sum(row_weights)), ('blk', 'harvest'))]
    all_gather x1, waiting for transfers between devices: 48.1 us -> 10.1 us  [local(): lax.all_gather(queries, ('blk', 'harvest'), axis=0, tiled=True)]
    all_to_all x2 -> x0, starting transfers between devices: 13.4 us -> none  [the longest x1 7.28 us: local(): lax.all_to_all(bucket_weights.reshape(blk_count, capacity).astype(jnp.bfl...]
    scatter x2 -> x0, local copies, waits for them, and re-layouts: 12.7 us -> none  [the longest x1 11.3 us: local(): jnp.zeros((slot_total, width), jnp.bfloat16).at[slot_index].set(grad_rows)]
    all_to_all x0 -> x1, blocking collectives: none -> 11.3 us  [local(): lax.all_to_all(bucket.reshape(blk_count, capacity, query_count), 'blk', s...]
    all_gather x1 -> x0, blocking collectives: 6.53 us -> none  [circulate(): block_queries = lax.all_gather(prepared, 'harvest', axis=0, tiled=True)]
    convert_element_type x2 -> x1, local copies, waits for them, and re-layouts: 0.76 us -> 4.23 us  [local(): prepared = (all_queries.astype(jnp.float32) * scaling).astype(jnp.bfloat16)]
  transfers between devices with their start and end apart: 3 -> 1, of which waited for: 1 -> 1; matrix products, arithmetic and copies ran while one was open for 6% -> 9% of each run, Pallas kernels for 0% -> 0%
where the time goes in v1:
time: 98.1 us; the launch traced here: 97.7 us
  blocking collectives  54.2 us (55%)
  between operations  13.4 us (14%)
  waiting for transfers between devices  10.8 us (11%)
  other arithmetic  7.41 us (8%)
  local copies, waits for them, and re-layouts  6.64 us (7%)
  matrix products  5.25 us (5%)
    psum x1, blocking collectives, local(): lax.psum((squares, jnp.sum(row_weights)), ('blk', 'harvest'))  42.9 us
    all_to_all x1, blocking collectives, local(): lax.all_to_all(bucket.reshape(blk_count, capacity, query_count), 'blk', s...  11.3 us
    all_gather x1, waiting for transfers between devices, local(): lax.all_gather(queries, ('blk', 'harvest'), axis=0, tiled=True)  10.1 us
    dot_general x1, matrix products, local(): jnp.dot(placement, value, preferred_element_type=jnp.float32)  5.25 us
    convert_element_type x1, local copies, waits for them, and re-layouts, local(): prepared = (all_queries.astype(jnp.float32) * scaling).astype(jnp.bfloat16)  4.23 us
    reduce_sum x1, other arithmetic, local(): jnp.sum(row_weights[:, None] * jnp.square(grad_rows.astype(jnp.float32)),...  3.35 us
  transfers between devices with their start and end apart: 1, of which 1 were waited for; matrix products, arithmetic and copies ran while one was open for 9% of the time, Pallas kernels for 0%

profile of v1, /device:TPU:0, one launch (start us, length us, event | category | flops | bytes accessed | tf_op | source)
XLA Modules:
  0.0 97.7 jit_solution(304757554591589561)
XLA Ops:
  6.5 0.0 copy-start
  6.5 0.0 all-gather.3.cloned.1.call-start
  6.5 0.7 all-gather.3.cloned.1.call-update
  7.3 0.8 copy.12
  8.0 0.7 and_reduce_fusion
  8.7 0.7 gather_fusion
  9.5 0.1 copy.13
  9.5 0.7 fusion.10
  10.2 0.6 reduce-window.6
  10.8 0.2 slice_reduce_fusion
  11.0 1.3 %broadcast_multiply_fusion = (f32[256]{0:T(256)S(1)}, f32[]{:T(128)}) fusion(f32[256]{0:T(256)} %param.6), kind=kLoop, calls=%fused_computation.26 | loop fusion | flops 511 | bytes 2052 | tf_op jit(solution)/shard_map/mul | solution.py:31
  12.3 3.3 %multiply_reduce_fusion = f32[8192]{0:T(1024)S(1)} fusion(bf16[256,8192]{1,0:T(8,128)(2,1)} %param.5, f32[256]{0:T(256)} %param.6), kind=kLoop, calls=%fused_computation.1 | loop fusion | flops 8380416 | bytes 4228096 | tf_op jit(solution)/shard_map/reduce_sum | solution.py:22
  15.7 42.9 %all-reduce = (f32[8192]{0:T(1024)S(1)}, f32[]{:T(128)}) all-reduce(f32[8192]{0:T(1024)S(1)} %multiply_reduce_fusion, f32[]{:T(128)} %get-tuple-element.10), channel_id=1, replica_groups=mesh['blk'=8,'harvest'=4] {'blk','harvest'}, use_global_device_ids=true, to_apply=%region_4.5 | all-reduce | flops 8193 | bytes 65544 | tf_op jit(solution)/shard_map/psum | solution.py:23
  58.6 0.0 copy-done
  58.6 0.1 fusion.9
  58.7 0.7 add_rsqrt_fusion
  59.3 10.1 %all-gather.3.cloned.1.call-done = bf16[32,4,8192]{2,1,0:T(4,128)(2,1)} async-done(((bf16[1,4,8192]{2,1,0:T(4,128)(2,1)}), bf16[32,4,8192]{2,1,0:T(4,128)(2,1)}) %all-gather.3.cloned.1.call-update) | async-done | bytes 2097168 | tf_op jit(solution)/shard_map/all_gather | solution.py:19
  69.4 4.2 %reshape.54 = f32[128,8192]{1,0:T(8,128)} reshape(bf16[32,4,8192]{2,1,0:T(4,128)(2,1)} %all-gather.3.cloned.1.call-done) | data formatting | bytes 6291456 | tf_op jit(solution)/shard_map/convert_element_type | solution.py:25
  73.7 5.3 %convolution_convert_fusion = bf16[384,128]{1,0:T(8,128)(2,1)S(1)} fusion(f32[256,128]{0,1:T(8,128)S(1)} %bitcast.26, bf16[256,8192]{1,0:T(8,128)(2,1)} %param.5, f32[128,8192]{1,0:T(8,128)} %reshape.54, f32[8192]{0:T(1024)S(1)} %add_rsqrt_fusion, s32[256]{0:T(256)S(1)} %multiply_add_fusion, f32[256]{0:T(256)S(1)} %get-tuple-element.9), kind=kOutput, calls=%fused_computation.5 | convolution fusion | flops 564379648 | bytes 8652800 | tf_op jit(solution)/shard_map/dot_general | solution.py:39
  78.9 11.3 %all_to_all.5 = bf16[8,48,128]{2,1,0:T(8,128)(2,1)S(1)} all-to-all(bf16[8,48,128]{2,1,0:T(8,128)(2,1)S(1)} %bitcast.27), channel_id=1, replica_groups=mesh['blk'=8,'harvest'=4] {'blk'}, dimensions={0} | all-to-all | bytes 196608 | tf_op jit(solution)/shard_map/all_to_all | solution.py:41
  90.2 0.6 copy.15
  (6 shorter events, 0.1 us)
Async XLA Ops:
  6.5 52.0 %copy-start = (s32[256,1]{0,1:T(1,128)S(1)}, s32[256,1]{0,1:T(1,128)}, u32[]{:S(2)}) copy-start(s32[256,1]{0,1:T(1,128)} %param.7) | copy-start | bytes 3076
  6.5 62.9 %all-gather.3.cloned.1.call-start = ((), (), s32[]{:S(2)}) async-start(), calls=%async_computation.1 | async-start | bytes 2162688 | tf_op jit(solution)/shard_map/all_gather | solution.py:19
Sparse Core Ops, SparseCore 0:
  10.2 59.1 all-gather.2

commit v2 on v1

--- a/solution.py
+++ b/solution.py
@@ -5,10 +5,98 @@
 from jax import lax
 from jax.sharding import PartitionSpec as P
 
+AXES = ("blk", "harvest")
+
+
+def axis_factors(blk_count, harv_count):
+    def split(n, lead):
+        sizes = []
+        if lead and n % 4 == 0:
+            sizes.append(4)
+            n //= 4
+        while n % 2 == 0 and n > 1:
+            sizes.append(2)
+            n //= 2
+        if n > 1:
+            sizes.append(n)
+        return sizes
+
+    factors = []
+    stride = blk_count * harv_count
+    for size in split(blk_count, True) + split(harv_count, False):
+        stride //= size
+        factors.append((size, stride))
+    return factors
+
+
+def coordinate(index, factor):
+    size, stride = factor
+    return (index // stride) % size
+
+
+def shifted(factor, shift, device_count):
+    size, stride = factor
+    return [(i, i + ((coordinate(i, factor) + shift) % size - coordinate(i, factor)) * stride) for i in range(device_count)]
+
+
+def gather_factor(piece, factor, device_count):
+    size, _ = factor
+    own = coordinate(lax.axis_index(AXES), factor)
+    stacked = jnp.zeros((size,) + piece.shape, piece.dtype)
+    stacked = lax.dynamic_update_index_in_dim(stacked, piece, own, 0)
+    for shift in range(1, size):
+        received = lax.ppermute(piece, AXES, shifted(factor, shift, device_count))
+        stacked = lax.dynamic_update_index_in_dim(stacked, received, (own - shift) % size, 0)
+    return stacked
+
+
+def gather_in_order(piece, order, factors, device_count):
+    for position in order:
+        piece = gather_factor(piece, factors[position], device_count)
+    held = list(reversed(order))
+    rank = len(factors)
+    axes = [held.index(position) for position in range(rank)] + list(range(rank, piece.ndim))
+    return jnp.transpose(piece, axes)
+
+
+def gather_queries(queries, factors, device_count):
+    rank = len(factors)
+    first, middle, last = [0], list(range(1, rank - 1)), [rank - 1]
+    if rank < 3 or queries.shape[0] % 2:
+        return gather_in_order(queries, list(range(rank)), factors, device_count).reshape(-1, queries.shape[1])
+    first_part = gather_factor(queries, factors[first[0]], device_count)
+    half = queries.shape[0] // 2
+    halves = []
+    for part, order in ((first_part[:, :half], middle), (first_part[:, half:], middle[::-1])):
+        gathered = part
+        for position in order:
+            gathered = gather_factor(gathered, factors[position], device_count)
+        held = list(reversed(order))
+        axes = [held.index(position) for position in middle] + list(range(len(middle), gathered.ndim))
+        halves.append(jnp.transpose(gathered, axes))
+    joined = jnp.concatenate(halves, axis=-2)
+    joined = jnp.moveaxis(joined, len(middle), 0)
+    joined = gather_factor(joined, factors[last[0]], device_count)
+    joined = jnp.moveaxis(joined, 0, rank - 1)
+    return joined.reshape(-1, queries.shape[1])
+
+
+def butterfly_sum(values, factors, device_count):
+    for factor in factors:
+        size, stride = factor
+        bit = 1
+        while bit < size:
+            pairs = [(i, i + ((coordinate(i, factor) ^ bit) - coordinate(i, factor)) * stride) for i in range(device_count)]
+            values = values + lax.ppermute(values, AXES, pairs)
+            bit *= 2
+    return values
+
 
 def local(grad_rows, row_weights, destinations, queries, tile_pattern):
     blk_count = lax.axis_size("blk")
     harv_count = lax.axis_size("harvest")
+    device_count = blk_count * harv_count
+    factors = axis_factors(blk_count, harv_count)
     row_count = grad_rows.shape[0]
     width = grad_rows.shape[1]
     capacity = max(3 * row_count // (2 * blk_count), 2)
@@ -16,11 +104,13 @@
     slot_total = blk_count * capacity
     inv_root = 1.0 / math.sqrt(width)
 
-    all_queries = lax.all_gather(queries, ("blk", "harvest"), axis=0, tiled=True)
+    all_queries = gather_queries(queries, factors, device_count)
     query_count = all_queries.shape[0]
 
     squares = jnp.sum(row_weights[:, None] * jnp.square(grad_rows.astype(jnp.float32)), axis=0)
-    total_sq, total_weight = lax.psum((squares, jnp.sum(row_weights)), ("blk", "harvest"))
+    packed = jnp.concatenate([squares, jnp.zeros((128,), jnp.float32).at[0].set(jnp.sum(row_weights))])
+    packed = butterfly_sum(packed, factors, device_count)
+    total_sq, total_weight = packed[:width], packed[width]
     scaling = lax.rsqrt(total_sq / total_weight + 1e-06)
     prepared = (all_queries.astype(jnp.float32) * scaling).astype(jnp.bfloat16)
 
@@ -46,11 +136,11 @@
 
 def solution(mesh):
     in_specs = (
-        P(("blk", "harvest"), None),
-        P(("blk", "harvest")),
-        P(("blk", "harvest"), None),
-        P(("blk", "harvest"), None),
+        P(AXES, None),
+        P(AXES),
+        P(AXES, None),
+        P(AXES, None),
         P(),
     )
-    out_specs = P(("blk", "harvest"), None)
+    out_specs = P(AXES, None)
     return jax.shard_map(local, mesh=mesh, in_specs=in_specs, out_specs=out_specs, check_vma=False)

time: 98.1 us -> 71.4 us (0.73)
  blocking collectives: 54.2 us -> 9.72 us
  starting transfers between devices: 0.01 us -> 16.3 us
  between operations: 13.4 us -> 0.44 us
  local copies, waits for them, and re-layouts: 6.64 us -> 11.8 us
  waiting for transfers between devices: 10.8 us -> 15.6 us
  other arithmetic: 7.41 us -> 12 us
    psum x1 -> x0, blocking collectives: 42.9 us -> none  [local(): lax.psum((squares, jnp.sum(row_weights)), ('blk', 'harvest'))]
    ppermute x0 -> x13, starting transfers between devices: none -> 16.3 us  [the longest x8 12.3 us: gather_factor(): received = lax.ppermute(piece, AXES, shifted(factor, shift, device_count))]
    ppermute x0 -> x13, waiting for transfers between devices: none -> 15.6 us  [the longest x5 9.29 us: butterfly_sum(): values = values + lax.ppermute(values, AXES, pairs)]
    all_gather x1 -> x0, waiting for transfers between devices: 10.1 us -> none  [local(): lax.all_gather(queries, ('blk', 'harvest'), axis=0, tiled=True)]
    convert_element_type x0 -> x1, other arithmetic: none -> 2.41 us  [local(): prepared = (all_queries.astype(jnp.float32) * scaling).astype(jnp.bfloat16)]
    dynamic_update_slice x0 -> x13, local copies, waits for them, and re-layouts: none -> 1.99 us  [the longest x8 1.26 us: gather_factor(): lax.dynamic_update_index_in_dim(stacked, received, (own - shift) % size, 0)]
    all_to_all x1, blocking collectives: 11.3 us -> 9.72 us  [local(): lax.all_to_all(bucket.reshape(blk_count, capacity, query_count), 'blk', s...]
    another operation x1 -> x6, local copies, waits for them, and re-layouts: 0.01 us -> 1.29 us
  transfers between devices with their start and end apart: 1 -> 13, of which waited for: 1 -> 8; matrix products, arithmetic and copies ran while one was open for 9% -> 19% of each run, Pallas kernels for 0% -> 0%
where the time goes in v2:
time: 71.4 us; the launch traced here: 71.1 us
  starting transfers between devices  16.3 us (23%)
  waiting for transfers between devices  15.6 us (22%)
  other arithmetic  12 us (17%)
  local copies, waits for them, and re-layouts  11.8 us (17%)
  blocking collectives  9.72 us (14%)
  matrix products  5.25 us (7%)
    ppermute x8, starting transfers between devices, gather_factor(): received = lax.ppermute(piece, AXES, shifted(factor, shift, device_count))  12.3 us
    all_to_all x1, blocking collectives, local(): lax.all_to_all(bucket.reshape(blk_count, capacity, query_count), 'blk', s...  9.72 us
    ppermute x5, waiting for transfers between devices, butterfly_sum(): values = values + lax.ppermute(values, AXES, pairs)  9.29 us
    ppermute x8, waiting for transfers between devices, gather_factor(): received = lax.ppermute(piece, AXES, shifted(factor, shift, device_count))  6.3 us
    convert_element_type x1, local copies, waits for them, and re-layouts, local(): prepared = (all_queries.astype(jnp.float32) * scaling).astype(jnp.bfloat16)  5.28 us
    dot_general x1, matrix products, local(): jnp.dot(placement, value, preferred_element_type=jnp.float32)  5.25 us
    ppermute x5, starting transfers between devices, butterfly_sum(): values = values + lax.ppermute(values, AXES, pairs)  4.01 us
    reduce_sum x1, other arithmetic, local(): jnp.sum(row_weights[:, None] * jnp.square(grad_rows.astype(jnp.float32)),...  3.35 us
  transfers between devices with their start and end apart: 13, of which 8 were waited for; matrix products, arithmetic and copies ran while one was open for 19% of the time, Pallas kernels for 0%

profile of v2, /device:TPU:0, one launch (start us, length us, event | category | flops | bytes accessed | tf_op | source)
XLA Modules:
  0.0 71.1 jit_solution(391475966248889744)
XLA Ops:
  0.0 3.1 %collective-permute-start = (bf16[4,8192]{1,0:T(4,128)(2,1)}, bf16[4,8192]{1,0:T(4,128)(2,1)S(1)}, u32[]{:S(2)}, u32[]{:S(2)}) collective-permute-start(bf16[4,8192]{1,0:T(4,128)(2,1)} %param.10), channel_id=1, source_target_pairs={{0,8},{1,9},{2,10},{3,11},{4,12},{5,13},{6,14},{7,15},{8,16},{9,17... | collective-permute-start | bytes 196616 | tf_op jit(solution)/shard_map/ppermute | solution.py:48
  3.1 2.6 %collective-permute-start.1 = (bf16[4,8192]{1,0:T(4,128)(2,1)}, bf16[4,8192]{1,0:T(4,128)(2,1)S(1)}, u32[]{:S(2)}, u32[]{:S(2)}) collective-permute-start(bf16[4,8192]{1,0:T(4,128)(2,1)} %param.10), channel_id=1, source_target_pairs={{0,16},{1,17},{2,18},{3,19},{4,20},{5,21},{6,22},{7,23},{8,24},{9,... | collective-permute-start | bytes 196616 | tf_op jit(solution)/shard_map/ppermute | solution.py:48
  5.7 1.3 %collective-permute-start.2 = (bf16[4,8192]{1,0:T(4,128)(2,1)}, bf16[4,8192]{1,0:T(4,128)(2,1)S(1)}, u32[]{:S(2)}, u32[]{:S(2)}) collective-permute-start(bf16[4,8192]{1,0:T(4,128)(2,1)} %param.10), channel_id=1, source_target_pairs={{0,24},{1,25},{2,26},{3,27},{4,28},{5,29},{6,30},{7,31},{8,0},{9,1... | collective-permute-start | bytes 196616 | tf_op jit(solution)/shard_map/ppermute | solution.py:48
  7.0 1.3 %broadcast_multiply_fusion = (f32[256]{0:T(256)S(1)}, f32[]{:T(128)}) fusion(f32[256]{0:T(256)} %param.8), kind=kLoop, calls=%fused_computation.47 | loop fusion | flops 511 | bytes 2052 | tf_op jit(solution)/shard_map/mul | solution.py:121
  8.3 3.3 %multiply_reduce_fusion = f32[8192]{0:T(1024)S(1)} fusion(bf16[256,8192]{1,0:T(8,128)(2,1)} %param.7, f32[256]{0:T(256)} %param.8), kind=kLoop, calls=%fused_computation.1 | loop fusion | flops 8380416 | bytes 4228096 | tf_op jit(solution)/shard_map/reduce_sum | solution.py:110
  12.3 0.7 %collective-permute-start.8 = (f32[8320]{0:T(1024)S(1)}, f32[8320]{0:T(1024)S(1)}, u32[]{:S(2)}, u32[]{:S(2)}) collective-permute-start(f32[8320]{0:T(1024)S(1)} %select_maximum_fusion), channel_id=1, source_target_pairs={{0,8},{1,9},{2,10},{3,11},{4,12},{5,13},{6,14},{7,15},{8,0},{9,1},... | collective-permute-start | bytes 99848 | tf_op jit(solution)/shard_map/ppermute | solution.py:90
  15.3 1.1 %collective-permute-done.8 = f32[8320]{0:T(1024)S(1)} collective-permute-done((f32[8320]{0:T(1024)S(1)}, f32[8320]{0:T(1024)S(1)}, u32[]{:S(2)}, u32[]{:S(2)}) %collective-permute-start.8) | collective-permute-done | bytes 33312 | tf_op jit(solution)/shard_map/ppermute | solution.py:90
  17.4 4.9 %collective-permute-done.9 = f32[8320]{0:T(1024)S(1)} collective-permute-done((f32[8320]{0:T(1024)S(1)}, f32[8320]{0:T(1024)S(1)}, u32[]{:S(2)}, u32[]{:S(2)}) %collective-permute-start.9) | collective-permute-done | bytes 33312 | tf_op jit(solution)/shard_map/ppermute | solution.py:90
  22.3 1.5 %collective-permute-start.10 = (f32[8320]{0:T(1024)S(1)}, f32[8320]{0:T(1024)S(1)}, u32[]{:S(2)}, u32[]{:S(2)}) collective-permute-start(f32[8320]{0:T(1024)S(1)} %add.156), channel_id=1, source_target_pairs={{0,4},{1,5},{2,6},{3,7},{4,0},{5,1},{6,2},{7,3},{8,12},{9,13},{10,... | collective-permute-start | bytes 99848 | tf_op jit(solution)/shard_map/ppermute | solution.py:90
  24.6 1.5 %collective-permute-start.5 = (bf16[4,2,8192]{2,1,0:T(2,128)(2,1)S(1)}, bf16[4,2,8192]{2,1,0:T(2,128)(2,1)S(1)}, u32[]{:S(2)}, u32[]{:S(2)}) collective-permute-start(bf16[4,2,8192]{2,1,0:T(2,128)(2,1)S(1)} %get-tuple-element.20), channel_id=1, source_target_pairs={{0,2},{1,3},{2,0},{3,1},{4,6},{5,7},{6,4},{7,5},{8,10},{9,11},{10,... | collective-permute-start | bytes 393224 | tf_op jit(solution)/shard_map/ppermute | solution.py:48
  26.3 1.5 %collective-permute-start.11 = (f32[8320]{0:T(1024)S(1)}, f32[8320]{0:T(1024)S(1)}, u32[]{:S(2)}, u32[]{:S(2)}) collective-permute-start(f32[8320]{0:T(1024)S(1)} %add.157), channel_id=1, source_target_pairs={{0,2},{1,3},{2,0},{3,1},{4,6},{5,7},{6,4},{7,5},{8,10},{9,11},{10,... | collective-permute-start | bytes 99848 | tf_op jit(solution)/shard_map/ppermute | solution.py:90
  28.0 2.2 %collective-permute-done.11 = f32[8320]{0:T(1024)S(1)} collective-permute-done((f32[8320]{0:T(1024)S(1)}, f32[8320]{0:T(1024)S(1)}, u32[]{:S(2)}, u32[]{:S(2)}) %collective-permute-start.11) | collective-permute-done | bytes 33312 | tf_op jit(solution)/shard_map/ppermute | solution.py:90
  30.6 0.9 %collective-permute-done.12 = f32[8320]{0:T(1024)S(1)} collective-permute-done((f32[8320]{0:T(1024)S(1)}, f32[8320]{0:T(1024)S(1)}, u32[]{:S(2)}, u32[]{:S(2)}) %collective-permute-start.12) | collective-permute-done | bytes 33312 | tf_op jit(solution)/shard_map/ppermute | solution.py:90
  32.8 1.6 %collective-permute-start.4 = (bf16[2,4,2,8192]{3,2,0,1:T(2,128)(2,1)S(1)}, bf16[2,4,2,8192]{3,2,0,1:T(2,128)(2,1)S(1)}, u32[]{:S(2)}, u32[]{:S(2)}) collective-permute-start(bf16[2,4,2,8192]{3,2,0,1:T(2,128)(2,1)S(1)} %bitcast_dynamic-update-slice_fusion.7), channel_id=1, source_target_pairs={{0,2},{1,3},{2,0},{3,1},{4,6},{5,7},{6,4},{7,5},{8,10},{9,11},{10,... | collective-permute-start | bytes 786440 | tf_op jit(solution)/shard_map/ppermute | solution.py:48
  35.1 1.6 %collective-permute-start.6 = (bf16[2,4,2,8192]{3,2,0,1:T(2,128)(2,1)S(1)}, bf16[2,4,2,8192]{3,2,0,1:T(2,128)(2,1)S(1)}, u32[]{:S(2)}, u32[]{:S(2)}) collective-permute-start(bf16[2,4,2,8192]{3,2,0,1:T(2,128)(2,1)S(1)} %bitcast_dynamic-update-slice_fusion.9), channel_id=1, source_target_pairs={{0,4},{1,5},{2,6},{3,7},{4,0},{5,1},{6,2},{7,3},{8,12},{9,13},{10,... | collective-permute-start | bytes 786440 | tf_op jit(solution)/shard_map/ppermute | solution.py:48
  37.3 3.9 %collective-permute-done.4 = bf16[2,4,2,8192]{3,2,0,1:T(2,128)(2,1)S(1)} collective-permute-done((bf16[2,4,2,8192]{3,2,0,1:T(2,128)(2,1)S(1)}, bf16[2,4,2,8192]{3,2,0,1:T(2,128)(2,1)S(1)}, u32[]{:S(2)}, u32[]{:S(2)}) %collective-permute-start.4) | collective-permute-done | bytes 262176 | tf_op jit(solution)/shard_map/ppermute | solution.py:48
  41.4 1.8 %collective-permute-done.6 = bf16[2,4,2,8192]{3,2,0,1:T(2,128)(2,1)S(1)} collective-permute-done((bf16[2,4,2,8192]{3,2,0,1:T(2,128)(2,1)S(1)}, bf16[2,4,2,8192]{3,2,0,1:T(2,128)(2,1)S(1)}, u32[]{:S(2)}, u32[]{:S(2)}) %collective-permute-start.6) | collective-permute-done | bytes 262176 | tf_op jit(solution)/shard_map/ppermute | solution.py:48
  43.5 1.1 %fusion.6 = bf16[4,2,2,4,8192]{4,3,2,1,0:T(4,128)(2,1)S(1)} fusion(bf16[2,2,4,2,8192]{4,3,1,0,2:T(2,128)(2,1)S(1)} %bitcast_dynamic-update-slice_fusion.5, bf16[2,2,4,2,8192]{4,3,1,0,2:T(2,128)(2,1)S(1)} %bitcast_dynamic-update-slice_fusion.3), kind=kLoop, calls=%fused_computation.15 | loop fusion | flops 2097152 | bytes 2097152 | tf_op jit(solution)/shard_map/transpose | solution.py:78
  44.6 0.9 %broadcast_in_dim.72 = bf16[2,4,2,2,4,8192]{5,4,0,3,2,1:T(4,128)(2,1)S(1)} broadcast(bf16[]{:T(256)} %constant.198.clone.1), dimensions={} | broadcast | bytes 2097154 | tf_op jit(solution)/shard_map/broadcast_in_dim | solution.py:45
  45.6 1.2 %bitcast_dynamic-update-slice_fusion = bf16[2,4,2,2,4,8192]{5,4,0,3,2,1:T(4,128)(2,1)S(1)} fusion(bf16[2,4,2,2,4,8192]{5,4,0,3,2,1:T(4,128)(2,1)S(1)} %broadcast_in_dim.72, s32[]{:T(128)S(6)} %select_n.133, bf16[2,2,4,2,8192]{4,3,1,0,2:T(2,128)(2,1)S(1)} %bitcast_dynamic-update-slice_fusion.5, ...), kind=kLoop, calls=%fused_computation.12 | loop fusion | flops 2097152 | bytes 2097156 | tf_op jit(solution)/shard_map/jit(dynamic_update_index_in_dim)/dynamic_update_slice | solution.py:46
  47.8 2.4 %convert_bitcast_fusion = f32[4,2,2,2,4,8192]{5,4,3,2,1,0:T(4,128)} fusion(bf16[2,4,2,2,4,8192]{5,4,0,3,2,1:T(4,128)(2,1)S(1)} %bitcast_dynamic-update-slice_fusion.1), kind=kLoop, calls=%fused_computation.2 | loop fusion | flops 1048576 | bytes 6291456 | tf_op jit(solution)/shard_map/convert_element_type | solution.py:115
  50.2 5.3 %reshape.74 = f32[128,8192]{1,0:T(8,128)} reshape(f32[4,2,2,2,4,8192]{5,4,3,2,1,0:T(4,128)} %convert_bitcast_fusion) | data formatting | bytes 8388608 | tf_op jit(solution)/shard_map/convert_element_type | solution.py:115
  55.5 5.3 %convolution_convert_fusion = bf16[384,128]{1,0:T(8,128)(2,1)S(1)} fusion(f32[256,128]{0,1:T(8,128)S(1)} %bitcast.81, bf16[256,8192]{1,0:T(8,128)(2,1)} %param.7, f32[128,8192]{1,0:T(8,128)} %reshape.74, f32[8192]{0:T(1024)S(1)} %fusion.10, s32[256]{0:T(256)S(1)} %multiply_add_fusion, f32[256]{0:T(256)S(1)} %get-tuple-element.21), kind=kOutput, calls=%fused_computation.6 | convolution fusion | flops 564379648 | bytes 8652800 | tf_op jit(solution)/shard_map/dot_general | solution.py:129
  60.8 9.7 %all_to_all.5 = bf16[8,48,128]{2,1,0:T(8,128)(2,1)S(1)} all-to-all(bf16[8,48,128]{2,1,0:T(8,128)(2,1)S(1)} %bitcast.82), channel_id=1, replica_groups=mesh['blk'=8,'harvest'=4] {'blk'}, dimensions={0} | all-to-all | bytes 196608 | tf_op jit(solution)/shard_map/all_to_all | solution.py:131
  (59 shorter events, 10.0 us)
Async XLA Ops:
  0.0 14.9 %copy-start = (bf16[4,8192]{1,0:T(4,128)(2,1)S(1)}, bf16[4,8192]{1,0:T(4,128)(2,1)}, u32[]{:S(2)}) copy-start(bf16[4,8192]{1,0:T(4,128)(2,1)} %param.10) | copy-start | bytes 196612
  0.0 13.1 %copy-start.1 = (s32[256,1]{0,1:T(1,128)S(1)}, s32[256,1]{0,1:T(1,128)}, u32[]{:S(2)}) copy-start(s32[256,1]{0,1:T(1,128)} %param.9) | copy-start | bytes 3076
  0.0 13.9 %copy-start.2 = (s32[8,8]{1,0:T(8,128)S(1)}, s32[8,8]{1,0:T(8,128)}, u32[]{:S(2)}) copy-start(s32[8,8]{1,0:T(8,128)} %param.11) | copy-start | bytes 772
  0.0 17.3 %collective-permute-start = (bf16[4,8192]{1,0:T(4,128)(2,1)}, bf16[4,8192]{1,0:T(4,128)(2,1)S(1)}, u32[]{:S(2)}, u32[]{:S(2)}) collective-permute-start(bf16[4,8192]{1,0:T(4,128)(2,1)} %param.10), channel_id=1, source_target_pairs={{0,8},{1,9},{2,10},{3,11},{4,12},{5,13},{6,14},{7,15},{8,16},{9,17... | collective-permute-start | bytes 196616 | tf_op jit(solution)/shard_map/ppermute | solution.py:48
  3.1 14.2 %collective-permute-start.1 = (bf16[4,8192]{1,0:T(4,128)(2,1)}, bf16[4,8192]{1,0:T(4,128)(2,1)S(1)}, u32[]{:S(2)}, u32[]{:S(2)}) collective-permute-start(bf16[4,8192]{1,0:T(4,128)(2,1)} %param.10), channel_id=1, source_target_pairs={{0,16},{1,17},{2,18},{3,19},{4,20},{5,21},{6,22},{7,23},{8,24},{9,... | collective-permute-start | bytes 196616 | tf_op jit(solution)/shard_map/ppermute | solution.py:48
  5.7 11.7 %collective-permute-start.2 = (bf16[4,8192]{1,0:T(4,128)(2,1)}, bf16[4,8192]{1,0:T(4,128)(2,1)S(1)}, u32[]{:S(2)}, u32[]{:S(2)}) collective-permute-start(bf16[4,8192]{1,0:T(4,128)(2,1)} %param.10), channel_id=1, source_target_pairs={{0,24},{1,25},{2,26},{3,27},{4,28},{5,29},{6,30},{7,31},{8,0},{9,1... | collective-permute-start | bytes 196616 | tf_op jit(solution)/shard_map/ppermute | solution.py:48
  12.3 4.0 %collective-permute-start.8 = (f32[8320]{0:T(1024)S(1)}, f32[8320]{0:T(1024)S(1)}, u32[]{:S(2)}, u32[]{:S(2)}) collective-permute-start(f32[8320]{0:T(1024)S(1)} %select_maximum_fusion), channel_id=1, source_target_pairs={{0,8},{1,9},{2,10},{3,11},{4,12},{5,13},{6,14},{7,15},{8,0},{9,1},... | collective-permute-start | bytes 99848 | tf_op jit(solution)/shard_map/ppermute | solution.py:90
  17.0 5.3 %collective-permute-start.9 = (f32[8320]{0:T(1024)S(1)}, f32[8320]{0:T(1024)S(1)}, u32[]{:S(2)}, u32[]{:S(2)}) collective-permute-start(f32[8320]{0:T(1024)S(1)} %fusion.14), channel_id=1, source_target_pairs={{0,16},{1,17},{2,18},{3,19},{4,20},{5,21},{6,22},{7,23},{8,24},{9,... | collective-permute-start | bytes 99848 | tf_op jit(solution)/shard_map/ppermute | solution.py:90
  22.3 4.0 %collective-permute-start.10 = (f32[8320]{0:T(1024)S(1)}, f32[8320]{0:T(1024)S(1)}, u32[]{:S(2)}, u32[]{:S(2)}) collective-permute-start(f32[8320]{0:T(1024)S(1)} %add.156), channel_id=1, source_target_pairs={{0,4},{1,5},{2,6},{3,7},{4,0},{5,1},{6,2},{7,3},{8,12},{9,13},{10,... | collective-permute-start | bytes 99848 | tf_op jit(solution)/shard_map/ppermute | solution.py:90
  24.0 8.6 %collective-permute-start.3 = (bf16[4,2,8192]{2,1,0:T(2,128)(2,1)S(1)}, bf16[4,2,8192]{2,1,0:T(2,128)(2,1)S(1)}, u32[]{:S(2)}, u32[]{:S(2)}) collective-permute-start(bf16[4,2,8192]{2,1,0:T(2,128)(2,1)S(1)} %get-tuple-element.19), channel_id=1, source_target_pairs={{0,4},{1,5},{2,6},{3,7},{4,0},{5,1},{6,2},{7,3},{8,12},{9,13},{10,... | collective-permute-start | bytes 393224 | tf_op jit(solution)/shard_map/ppermute | solution.py:48
  24.6 10.4 %collective-permute-start.5 = (bf16[4,2,8192]{2,1,0:T(2,128)(2,1)S(1)}, bf16[4,2,8192]{2,1,0:T(2,128)(2,1)S(1)}, u32[]{:S(2)}, u32[]{:S(2)}) collective-permute-start(bf16[4,2,8192]{2,1,0:T(2,128)(2,1)S(1)} %get-tuple-element.20), channel_id=1, source_target_pairs={{0,2},{1,3},{2,0},{3,1},{4,6},{5,7},{6,4},{7,5},{8,10},{9,11},{10,... | collective-permute-start | bytes 393224 | tf_op jit(solution)/shard_map/ppermute | solution.py:48
  26.3 4.0 %collective-permute-start.11 = (f32[8320]{0:T(1024)S(1)}, f32[8320]{0:T(1024)S(1)}, u32[]{:S(2)}, u32[]{:S(2)}) collective-permute-start(f32[8320]{0:T(1024)S(1)} %add.157), channel_id=1, source_target_pairs={{0,2},{1,3},{2,0},{3,1},{4,6},{5,7},{6,4},{7,5},{8,10},{9,11},{10,... | collective-permute-start | bytes 99848 | tf_op jit(solution)/shard_map/ppermute | solution.py:90
  30.3 1.2 %collective-permute-start.12 = (f32[8320]{0:T(1024)S(1)}, f32[8320]{0:T(1024)S(1)}, u32[]{:S(2)}, u32[]{:S(2)}) collective-permute-start(f32[8320]{0:T(1024)S(1)} %add.158), channel_id=1, source_target_pairs={{0,1},{1,0},{2,3},{3,2},{4,5},{5,4},{6,7},{7,6},{8,9},{9,8},{10,11... | collective-permute-start | bytes 99848 | tf_op jit(solution)/shard_map/ppermute | solution.py:90
  32.8 8.4 %collective-permute-start.4 = (bf16[2,4,2,8192]{3,2,0,1:T(2,128)(2,1)S(1)}, bf16[2,4,2,8192]{3,2,0,1:T(2,128)(2,1)S(1)}, u32[]{:S(2)}, u32[]{:S(2)}) collective-permute-start(bf16[2,4,2,8192]{3,2,0,1:T(2,128)(2,1)S(1)} %bitcast_dynamic-update-slice_fusion.7), channel_id=1, source_target_pairs={{0,2},{1,3},{2,0},{3,1},{4,6},{5,7},{6,4},{7,5},{8,10},{9,11},{10,... | collective-permute-start | bytes 786440 | tf_op jit(solution)/shard_map/ppermute | solution.py:48
  35.1 8.2 %collective-permute-start.6 = (bf16[2,4,2,8192]{3,2,0,1:T(2,128)(2,1)S(1)}, bf16[2,4,2,8192]{3,2,0,1:T(2,128)(2,1)S(1)}, u32[]{:S(2)}, u32[]{:S(2)}) collective-permute-start(bf16[2,4,2,8192]{3,2,0,1:T(2,128)(2,1)S(1)} %bitcast_dynamic-update-slice_fusion.9), channel_id=1, source_target_pairs={{0,4},{1,5},{2,6},{3,7},{4,0},{5,1},{6,2},{7,3},{8,12},{9,13},{10,... | collective-permute-start | bytes 786440 | tf_op jit(solution)/shard_map/ppermute | solution.py:48
  44.6 2.7 %collective-permute-start.7 = (bf16[4,2,2,4,8192]{4,3,2,1,0:T(4,128)(2,1)S(1)}, bf16[4,2,2,4,8192]{4,3,2,1,0:T(4,128)(2,1)S(1)}, u32[]{:S(2)}, u32[]{:S(2)}) collective-permute-start(bf16[4,2,2,4,8192]{4,3,2,1,0:T(4,128)(2,1)S(1)} %fusion.6), channel_id=1, source_target_pairs={{0,1},{1,0},{2,3},{3,2},{4,5},{5,4},{6,7},{7,6},{8,9},{9,8},{10,11... | collective-permute-start | bytes 3145736 | tf_op jit(solution)/shard_map/ppermute | solution.py:48

commit v3 on v2

--- a/solution.py
+++ b/solution.py
@@ -50,35 +50,44 @@
     return stacked
 
 
-def gather_in_order(piece, order, factors, device_count):
-    for position in order:
-        piece = gather_factor(piece, factors[position], device_count)
-    held = list(reversed(order))
-    rank = len(factors)
-    axes = [held.index(position) for position in range(rank)] + list(range(rank, piece.ndim))
-    return jnp.transpose(piece, axes)
+def gather_rows(piece, factor, device_count):
+    rows = piece.shape[0]
+    return gather_factor(piece, factor, device_count).reshape((factor[0] * rows,) + piece.shape[1:])
 
 
-def gather_queries(queries, factors, device_count):
+def column_splits(width, parts):
+    blocks = width // 128
+    sizes = [(blocks // parts + (1 if j < blocks % parts else 0)) * 128 for j in range(parts)]
+    starts = [sum(sizes[:j]) for j in range(parts)]
+    return list(zip(starts, sizes))
+
+
+def streamed_scores(grad_rows, queries, scaling, factors, device_count):
     rank = len(factors)
-    first, middle, last = [0], list(range(1, rank - 1)), [rank - 1]
-    if rank < 3 or queries.shape[0] % 2:
-        return gather_in_order(queries, list(range(rank)), factors, device_count).reshape(-1, queries.shape[1])
-    first_part = gather_factor(queries, factors[first[0]], device_count)
-    half = queries.shape[0] // 2
-    halves = []
-    for part, order in ((first_part[:, :half], middle), (first_part[:, half:], middle[::-1])):
-        gathered = part
+    rows = queries.shape[0]
+    first = gather_rows(queries, factors[0], device_count)
+    rest = list(range(1, rank))
+    streams = max(len(rest), 1)
+    raw = None
+    for j, (start, size) in enumerate(column_splits(queries.shape[1], streams)):
+        order = rest[j:] + rest[:j]
+        part = first[:, start:start + size]
         for position in order:
-            gathered = gather_factor(gathered, factors[position], device_count)
+            part = gather_factor(part, factors[position], device_count)
         held = list(reversed(order))
-        axes = [held.index(position) for position in middle] + list(range(len(middle), gathered.ndim))
-        halves.append(jnp.transpose(gathered, axes))
-    joined = jnp.concatenate(halves, axis=-2)
-    joined = jnp.moveaxis(joined, len(middle), 0)
-    joined = gather_factor(joined, factors[last[0]], device_count)
-    joined = jnp.moveaxis(joined, 0, rank - 1)
-    return joined.reshape(-1, queries.shape[1])
+        stacked_rows = part.reshape(-1, size)
+        prepared = (stacked_rows.astype(jnp.float32) * scaling[start:start + size]).astype(jnp.bfloat16)
+        partial = jnp.einsum(
+            "rk,qk->rq", grad_rows[:, start:start + size], prepared, preferred_element_type=jnp.float32
+        )
+        shape = [factors[p][0] for p in held] + [factors[0][0], rows]
+        partial = partial.reshape((grad_rows.shape[0],) + tuple(shape))
+        canonical = [held.index(p) + 1 for p in rest]
+        lead = len(held) + 1
+        partial = jnp.transpose(partial, [0, lead] + canonical + [lead + 1])
+        partial = partial.reshape(grad_rows.shape[0], -1)
+        raw = partial if raw is None else raw + partial
+    return raw
 
 
 def butterfly_sum(values, factors, device_count):
@@ -104,17 +113,14 @@
     slot_total = blk_count * capacity
     inv_root = 1.0 / math.sqrt(width)
 
-    all_queries = gather_queries(queries, factors, device_count)
-    query_count = all_queries.shape[0]
+    query_count = queries.shape[0] * device_count
 
     squares = jnp.sum(row_weights[:, None] * jnp.square(grad_rows.astype(jnp.float32)), axis=0)
     packed = jnp.concatenate([squares, jnp.zeros((128,), jnp.float32).at[0].set(jnp.sum(row_weights))])
     packed = butterfly_sum(packed, factors, device_count)
     total_sq, total_weight = packed[:width], packed[width]
     scaling = lax.rsqrt(total_sq / total_weight + 1e-06)
-    prepared = (all_queries.astype(jnp.float32) * scaling).astype(jnp.bfloat16)
-
-    raw = jnp.einsum("rk,qk->rq", grad_rows, prepared, preferred_element_type=jnp.float32)
+    raw = streamed_scores(grad_rows, queries, scaling, factors, device_count)
     owner_ids = destinations[:, 0]
     pattern_rows = jnp.take(tile_pattern.T, owner_ids, axis=0).astype(jnp.float32)
     full_mask = jnp.repeat(pattern_rows, block_size, axis=1)

time: 71.4 us -> 65.4 us (0.916)
  local copies, waits for them, and re-layouts: 11.8 us -> 3.46 us
  starting transfers between devices: 16.3 us -> 20.9 us
  other arithmetic: 12 us -> 7.49 us
  waiting for transfers between devices: 15.6 us -> 16.9 us
  matrix products: 5.25 us -> 6.03 us
    dot_general x0 -> x3, matrix products: none -> 5.82 us  [streamed_scores(): jnp.einsum('rk,qk->rq', grad_rows[:, start:start + size], prepared, prefe...]
    convert_element_type x1 -> x0, local copies, waits for them, and re-layouts: 5.28 us -> none  [local(): prepared = (all_queries.astype(jnp.float32) * scaling).astype(jnp.bfloat16)]
    dot_general x1, matrix products: 5.25 us -> 0.21 us  [local(): jnp.dot(placement, value, preferred_element_type=jnp.float32)]
    ppermute x8 -> x12, starting transfers between devices: 12.3 us -> 16.9 us  [gather_factor(): received = lax.ppermute(piece, AXES, shifted(factor, shift, device_count))]
    ppermute x8 -> x12, waiting for transfers between devices: 6.3 us -> 9.49 us  [gather_factor(): received = lax.ppermute(piece, AXES, shifted(factor, shift, device_count))]
    convert_element_type x1, other arithmetic: 2.41 us -> 0.02 us  [local(): value = (raw * weight_scale[:, None] * full_mask).astype(jnp.bfloat16)]
    ppermute x5, waiting for transfers between devices: 9.29 us -> 7.4 us  [butterfly_sum(): values = values + lax.ppermute(values, AXES, pairs)]
    dynamic_update_slice x1 -> x0, other arithmetic: 1.15 us -> none  [gather_factor(): stacked = lax.dynamic_update_index_in_dim(stacked, piece, own, 0)]
  transfers between devices with their start and end apart: 13 -> 17, of which waited for: 8 -> 7; matrix products, arithmetic and copies ran while one was open for 19% -> 21% of each run, Pallas kernels for 0% -> 0%
where the time goes in v3:
time: 65.4 us; the launch traced here: 65.1 us
  starting transfers between devices  20.9 us (32%)
  waiting for transfers between devices  16.9 us (26%)
  blocking collectives  9.72 us (15%)
  other arithmetic  7.49 us (11%)
  matrix products  6.03 us (9%)
  local copies, waits for them, and re-layouts  3.46 us (5%)
    ppermute x12, starting transfers between devices, gather_factor(): received = lax.ppermute(piece, AXES, shifted(factor, shift, device_count))  16.9 us
    all_to_all x1, blocking collectives, local(): lax.all_to_all(bucket.reshape(blk_count, capacity, query_count), 'blk', s...  9.72 us
    ppermute x12, waiting for transfers between devices, gather_factor(): received = lax.ppermute(piece, AXES, shifted(factor, shift, device_count))  9.49 us
    ppermute x5, waiting for transfers between devices, butterfly_sum(): values = values + lax.ppermute(values, AXES, pairs)  7.4 us
    dot_general x3, matrix products, streamed_scores(): jnp.einsum('rk,qk->rq', grad_rows[:, start:start + size], prepared, prefe...  5.82 us
    ppermute x5, starting transfers between devices, butterfly_sum(): values = values + lax.ppermute(values, AXES, pairs)  3.94 us
    reduce_sum x1, other arithmetic, local(): jnp.sum(row_weights[:, None] * jnp.square(grad_rows.astype(jnp.float32)),...  3.38 us
  transfers between devices with their start and end apart: 17, of which 7 were waited for; matrix products, arithmetic and copies ran while one was open for 21% of the time, Pallas kernels for 0%

profile of v3, /device:TPU:0, one launch (start us, length us, event | category | flops | bytes accessed | tf_op | source)
XLA Modules:
  0.0 65.1 jit_solution(14812567134932323876)
XLA Ops:
  0.0 3.0 %collective-permute-start = (bf16[4,8192]{1,0:T(4,128)(2,1)}, bf16[4,8192]{1,0:T(4,128)(2,1)S(1)}, u32[]{:S(2)}, u32[]{:S(2)}) collective-permute-start(bf16[4,8192]{1,0:T(4,128)(2,1)} %param.10), channel_id=1, source_target_pairs={{0,8},{1,9},{2,10},{3,11},{4,12},{5,13},{6,14},{7,15},{8,16},{9,17... | collective-permute-start | bytes 196616 | tf_op jit(solution)/shard_map/ppermute | solution.py:48
  3.0 2.6 %collective-permute-start.1 = (bf16[4,8192]{1,0:T(4,128)(2,1)}, bf16[4,8192]{1,0:T(4,128)(2,1)S(1)}, u32[]{:S(2)}, u32[]{:S(2)}) collective-permute-start(bf16[4,8192]{1,0:T(4,128)(2,1)} %param.10), channel_id=1, source_target_pairs={{0,16},{1,17},{2,18},{3,19},{4,20},{5,21},{6,22},{7,23},{8,24},{9,... | collective-permute-start | bytes 196616 | tf_op jit(solution)/shard_map/ppermute | solution.py:48
  5.6 1.3 %collective-permute-start.2 = (bf16[4,8192]{1,0:T(4,128)(2,1)}, bf16[4,8192]{1,0:T(4,128)(2,1)S(1)}, u32[]{:S(2)}, u32[]{:S(2)}) collective-permute-start(bf16[4,8192]{1,0:T(4,128)(2,1)} %param.10), channel_id=1, source_target_pairs={{0,24},{1,25},{2,26},{3,27},{4,28},{5,29},{6,30},{7,31},{8,0},{9,1... | collective-permute-start | bytes 196616 | tf_op jit(solution)/shard_map/ppermute | solution.py:48
  7.0 1.3 %broadcast_multiply_fusion = (f32[256]{0:T(256)S(1)}, f32[]{:T(128)}) fusion(f32[256]{0:T(256)} %param.8), kind=kLoop, calls=%fused_computation.66 | loop fusion | flops 511 | bytes 2052 | tf_op jit(solution)/shard_map/mul | solution.py:127
  8.3 3.4 %multiply_reduce_fusion = f32[8192]{0:T(1024)S(1)} fusion(bf16[256,8192]{1,0:T(8,128)(2,1)} %param.7, f32[256]{0:T(256)} %param.8), kind=kLoop, calls=%fused_computation.1 | loop fusion | flops 8380416 | bytes 4228096 | tf_op jit(solution)/shard_map/reduce_sum | solution.py:118
  15.3 1.1 %collective-permute-done.6 = f32[8320]{0:T(1024)S(1)} collective-permute-done((f32[8320]{0:T(1024)S(1)}, f32[8320]{0:T(1024)S(1)}, u32[]{:S(2)}, u32[]{:S(2)}) %collective-permute-start.6) | collective-permute-done | bytes 33312 | tf_op jit(solution)/shard_map/ppermute | solution.py:99
  17.5 1.8 %collective-permute-start.11 = (bf16[16,2688]{1,0:T(8,128)(2,1)S(1)}, bf16[16,2688]{1,0:T(8,128)(2,1)S(1)}, u32[]{:S(2)}, u32[]{:S(2)}) collective-permute-start(bf16[16,2688]{1,0:T(8,128)(2,1)S(1)} %get-tuple-element.19), channel_id=1, source_target_pairs={{0,2},{1,3},{2,0},{3,1},{4,6},{5,7},{6,4},{7,5},{8,10},{9,11},{10,... | collective-permute-start | bytes 258056 | tf_op jit(solution)/shard_map/ppermute | solution.py:48
  19.3 1.5 %collective-permute-start.3 = (bf16[16,2816]{1,0:T(8,128)(2,1)S(1)}, bf16[16,2816]{1,0:T(8,128)(2,1)S(1)}, u32[]{:S(2)}, u32[]{:S(2)}) collective-permute-start(bf16[16,2816]{1,0:T(8,128)(2,1)S(1)} %slice.64), channel_id=1, source_target_pairs={{0,4},{1,5},{2,6},{3,7},{4,0},{5,1},{6,2},{7,3},{8,12},{9,13},{10,... | collective-permute-start | bytes 270344 | tf_op jit(solution)/shard_map/ppermute | solution.py:48
  20.9 1.5 %collective-permute-done.7 = f32[8320]{0:T(1024)S(1)} collective-permute-done((f32[8320]{0:T(1024)S(1)}, f32[8320]{0:T(1024)S(1)}, u32[]{:S(2)}, u32[]{:S(2)}) %collective-permute-start.7) | collective-permute-done | bytes 33312 | tf_op jit(solution)/shard_map/ppermute | solution.py:99
  22.3 1.5 %collective-permute-start.8 = (f32[8320]{0:T(1024)S(1)}, f32[8320]{0:T(1024)S(1)}, u32[]{:S(2)}, u32[]{:S(2)}) collective-permute-start(f32[8320]{0:T(1024)S(1)} %add.189), channel_id=1, source_target_pairs={{0,4},{1,5},{2,6},{3,7},{4,0},{5,1},{6,2},{7,3},{8,12},{9,13},{10,... | collective-permute-start | bytes 99848 | tf_op jit(solution)/shard_map/ppermute | solution.py:99
  23.9 2.4 %collective-permute-done.8 = f32[8320]{0:T(1024)S(1)} collective-permute-done((f32[8320]{0:T(1024)S(1)}, f32[8320]{0:T(1024)S(1)}, u32[]{:S(2)}, u32[]{:S(2)}) %collective-permute-start.8) | collective-permute-done | bytes 33312 | tf_op jit(solution)/shard_map/ppermute | solution.py:99
  26.3 1.5 %collective-permute-start.9 = (f32[8320]{0:T(1024)S(1)}, f32[8320]{0:T(1024)S(1)}, u32[]{:S(2)}, u32[]{:S(2)}) collective-permute-start(f32[8320]{0:T(1024)S(1)} %add.190), channel_id=1, source_target_pairs={{0,2},{1,3},{2,0},{3,1},{4,6},{5,7},{6,4},{7,5},{8,10},{9,11},{10,... | collective-permute-start | bytes 99848 | tf_op jit(solution)/shard_map/ppermute | solution.py:99
  27.8 2.4 %collective-permute-done.9 = f32[8320]{0:T(1024)S(1)} collective-permute-done((f32[8320]{0:T(1024)S(1)}, f32[8320]{0:T(1024)S(1)}, u32[]{:S(2)}, u32[]{:S(2)}) %collective-permute-start.9) | collective-permute-done | bytes 33312 | tf_op jit(solution)/shard_map/ppermute | solution.py:99
  30.3 1.6 %collective-permute-start.15 = (bf16[2,16,2688]{2,1,0:T(8,128)(2,1)S(1)}, bf16[2,16,2688]{2,1,0:T(8,128)(2,1)S(1)}, u32[]{:S(2)}, u32[]{:S(2)}) collective-permute-start(bf16[2,16,2688]{2,1,0:T(8,128)(2,1)S(1)} %bitcast_dynamic-update-slice_fusion.14), channel_id=1, source_target_pairs={{0,4},{1,5},{2,6},{3,7},{4,0},{5,1},{6,2},{7,3},{8,12},{9,13},{10,... | collective-permute-start | bytes 516104 | tf_op jit(solution)/shard_map/ppermute | solution.py:48
  32.4 1.6 %collective-permute-start.4 = (bf16[2,16,2816]{2,1,0:T(8,128)(2,1)S(1)}, bf16[2,16,2816]{2,1,0:T(8,128)(2,1)S(1)}, u32[]{:S(2)}, u32[]{:S(2)}) collective-permute-start(bf16[2,16,2816]{2,1,0:T(8,128)(2,1)S(1)} %bitcast_dynamic-update-slice_fusion.12), channel_id=1, source_target_pairs={{0,2},{1,3},{2,0},{3,1},{4,6},{5,7},{6,4},{7,5},{8,10},{9,11},{10,... | collective-permute-start | bytes 540680 | tf_op jit(solution)/shard_map/ppermute | solution.py:48
  35.2 1.9 %collective-permute-done.15 = bf16[2,16,2688]{2,1,0:T(8,128)(2,1)S(1)} collective-permute-done((bf16[2,16,2688]{2,1,0:T(8,128)(2,1)S(1)}, bf16[2,16,2688]{2,1,0:T(8,128)(2,1)S(1)}, u32[]{:S(2)}, u32[]{:S(2)}) %collective-permute-start.15) | collective-permute-done | bytes 172064 | tf_op jit(solution)/shard_map/ppermute | solution.py:48
  37.2 1.6 %collective-permute-start.16 = (bf16[2,2,16,2688]{3,2,1,0:T(8,128)(2,1)S(1)}, bf16[2,2,16,2688]{3,2,1,0:T(8,128)(2,1)S(1)}, u32[]{:S(2)}, u32[]{:S(2)}) collective-permute-start(bf16[2,2,16,2688]{3,2,1,0:T(8,128)(2,1)S(1)} %bitcast_dynamic-update-slice_fusion.8), channel_id=1, source_target_pairs={{0,2},{1,3},{2,0},{3,1},{4,6},{5,7},{6,4},{7,5},{8,10},{9,11},{10,... | collective-permute-start | bytes 1032200 | tf_op jit(solution)/shard_map/ppermute | solution.py:48
  38.9 1.6 %collective-permute-start.13 = (bf16[2,2,16,2688]{3,2,1,0:T(8,128)(2,1)S(1)}, bf16[2,2,16,2688]{3,2,1,0:T(8,128)(2,1)S(1)}, u32[]{:S(2)}, u32[]{:S(2)}) collective-permute-start(bf16[2,2,16,2688]{3,2,1,0:T(8,128)(2,1)S(1)} %bitcast_dynamic-update-slice_fusion.10), channel_id=1, source_target_pairs={{0,4},{1,5},{2,6},{3,7},{4,0},{5,1},{6,2},{7,3},{8,12},{9,13},{10,... | collective-permute-start | bytes 1032200 | tf_op jit(solution)/shard_map/ppermute | solution.py:48
  40.8 6.1 %collective-permute-done.16 = bf16[2,2,16,2688]{3,2,1,0:T(8,128)(2,1)S(1)} collective-permute-done((bf16[2,2,16,2688]{3,2,1,0:T(8,128)(2,1)S(1)}, bf16[2,2,16,2688]{3,2,1,0:T(8,128)(2,1)S(1)}, u32[]{:S(2)}, u32[]{:S(2)}) %collective-permute-start.16) | collective-permute-done | bytes 344096 | tf_op jit(solution)/shard_map/ppermute | solution.py:48
  46.9 1.4 %collective-permute-done.13 = bf16[2,2,16,2688]{3,2,1,0:T(8,128)(2,1)S(1)} collective-permute-done((bf16[2,2,16,2688]{3,2,1,0:T(8,128)(2,1)S(1)}, bf16[2,2,16,2688]{3,2,1,0:T(8,128)(2,1)S(1)}, u32[]{:S(2)}, u32[]{:S(2)}) %collective-permute-start.13) | collective-permute-done | bytes 344096 | tf_op jit(solution)/shard_map/ppermute | solution.py:48
  48.3 1.9 %fusion.12 = f32[256,128]{0,1:T(8,128)S(1)} fusion(bf16[256,8192]{1,0:T(8,128)(2,1)} %param.7, bf16[128,2688]{1,0:T(8,128)(2,1)S(1)} %bitcast.95, f32[2688]{0:T(1024)S(1)} %get-tuple-element.22), kind=kOutput, calls=%fused_computation.16 | convolution fusion | flops 177192960 | bytes 2206208 | tf_op jit(solution)/shard_map/rk,qk->rq/dot_general | solution.py:80
  50.3 1.9 %fusion.9 = f32[256,128]{0,1:T(8,128)S(1)} fusion(bf16[256,8192]{1,0:T(8,128)(2,1)} %param.7, bf16[128,2688]{1,0:T(8,128)(2,1)S(1)} %bitcast.96, f32[2688]{0:T(1024)S(1)} %get-tuple-element.21), kind=kOutput, calls=%fused_computation.15 | convolution fusion | flops 177192960 | bytes 2206208 | tf_op jit(solution)/shard_map/rk,qk->rq/dot_general | solution.py:80
  52.4 2.0 %fusion.15 = f32[256,128]{0,1:T(8,128)S(1)} fusion(bf16[256,8192]{1,0:T(8,128)(2,1)} %param.7, bf16[128,2816]{1,0:T(8,128)(2,1)S(1)} %bitcast.94, f32[2816]{0:T(1024)S(1)} %slice-done), kind=kOutput, calls=%fused_computation.17 | convolution fusion | flops 185630720 | bytes 2305024 | tf_op jit(solution)/shard_map/rk,qk->rq/dot_general | solution.py:80
  54.7 9.7 %all_to_all.5 = bf16[8,48,128]{2,1,0:T(8,128)(2,1)S(1)} all-to-all(bf16[8,48,128]{2,1,0:T(8,128)(2,1)S(1)} %bitcast.98), channel_id=1, replica_groups=mesh['blk'=8,'harvest'=4] {'blk'}, dimensions={0} | all-to-all | bytes 196608 | tf_op jit(solution)/shard_map/all_to_all | solution.py:137
  (91 shorter events, 7.9 us)
Async XLA Ops:
  0.0 17.2 %collective-permute-start = (bf16[4,8192]{1,0:T(4,128)(2,1)}, bf16[4,8192]{1,0:T(4,128)(2,1)S(1)}, u32[]{:S(2)}, u32[]{:S(2)}) collective-permute-start(bf16[4,8192]{1,0:T(4,128)(2,1)} %param.10), channel_id=1, source_target_pairs={{0,8},{1,9},{2,10},{3,11},{4,12},{5,13},{6,14},{7,15},{8,16},{9,17... | collective-permute-start | bytes 196616 | tf_op jit(solution)/shard_map/ppermute | solution.py:48
  3.0 14.2 %collective-permute-start.1 = (bf16[4,8192]{1,0:T(4,128)(2,1)}, bf16[4,8192]{1,0:T(4,128)(2,1)S(1)}, u32[]{:S(2)}, u32[]{:S(2)}) collective-permute-start(bf16[4,8192]{1,0:T(4,128)(2,1)} %param.10), channel_id=1, source_target_pairs={{0,16},{1,17},{2,18},{3,19},{4,20},{5,21},{6,22},{7,23},{8,24},{9,... | collective-permute-start | bytes 196616 | tf_op jit(solution)/shard_map/ppermute | solution.py:48
  5.6 11.7 %collective-permute-start.2 = (bf16[4,8192]{1,0:T(4,128)(2,1)}, bf16[4,8192]{1,0:T(4,128)(2,1)S(1)}, u32[]{:S(2)}, u32[]{:S(2)}) collective-permute-start(bf16[4,8192]{1,0:T(4,128)(2,1)} %param.10), channel_id=1, source_target_pairs={{0,24},{1,25},{2,26},{3,27},{4,28},{5,29},{6,30},{7,31},{8,0},{9,1... | collective-permute-start | bytes 196616 | tf_op jit(solution)/shard_map/ppermute | solution.py:48
  8.2 4.8 %copy-start.3 = (s32[8,8]{1,0:T(8,128)S(1)}, s32[8,8]{1,0:T(8,128)}, u32[]{:S(2)}) copy-start(s32[8,8]{1,0:T(8,128)} %param.11) | copy-start | bytes 772
  8.2 4.9 %copy-start.2 = (s32[256,1]{0,1:T(1,128)S(1)}, s32[256,1]{0,1:T(1,128)}, u32[]{:S(2)}) copy-start(s32[256,1]{0,1:T(1,128)} %param.9) | copy-start | bytes 3076
  11.6 3.3 %copy-start.1 = (bf16[4,8192]{1,0:T(4,128)(2,1)S(1)}, bf16[4,8192]{1,0:T(4,128)(2,1)}, u32[]{:S(2)}) copy-start(bf16[4,8192]{1,0:T(4,128)(2,1)} %param.10) | copy-start | bytes 196612
  12.3 4.0 %collective-permute-start.6 = (f32[8320]{0:T(1024)S(1)}, f32[8320]{0:T(1024)S(1)}, u32[]{:S(2)}, u32[]{:S(2)}) collective-permute-start(f32[8320]{0:T(1024)S(1)} %select_maximum_fusion), channel_id=1, source_target_pairs={{0,8},{1,9},{2,10},{3,11},{4,12},{5,13},{6,14},{7,15},{8,0},{9,1},... | collective-permute-start | bytes 99848 | tf_op jit(solution)/shard_map/ppermute | solution.py:99
  17.0 5.3 %collective-permute-start.7 = (f32[8320]{0:T(1024)S(1)}, f32[8320]{0:T(1024)S(1)}, u32[]{:S(2)}, u32[]{:S(2)}) collective-permute-start(f32[8320]{0:T(1024)S(1)} %fusion.31), channel_id=1, source_target_pairs={{0,16},{1,17},{2,18},{3,19},{4,20},{5,21},{6,22},{7,23},{8,24},{9,... | collective-permute-start | bytes 99848 | tf_op jit(solution)/shard_map/ppermute | solution.py:99
  17.5 12.8 %collective-permute-start.14 = (bf16[16,2688]{1,0:T(8,128)(2,1)S(1)}, bf16[16,2688]{1,0:T(8,128)(2,1)S(1)}, u32[]{:S(2)}, u32[]{:S(2)}) collective-permute-start(bf16[16,2688]{1,0:T(8,128)(2,1)S(1)} %get-tuple-element.20), channel_id=1, source_target_pairs={{0,1},{1,0},{2,3},{3,2},{4,5},{5,4},{6,7},{7,6},{8,9},{9,8},{10,11... | collective-permute-start | bytes 258056 | tf_op jit(solution)/shard_map/ppermute | solution.py:48
  17.5 14.4 %collective-permute-start.11 = (bf16[16,2688]{1,0:T(8,128)(2,1)S(1)}, bf16[16,2688]{1,0:T(8,128)(2,1)S(1)}, u32[]{:S(2)}, u32[]{:S(2)}) collective-permute-start(bf16[16,2688]{1,0:T(8,128)(2,1)S(1)} %get-tuple-element.19), channel_id=1, source_target_pairs={{0,2},{1,3},{2,0},{3,1},{4,6},{5,7},{6,4},{7,5},{8,10},{9,11},{10,... | collective-permute-start | bytes 258056 | tf_op jit(solution)/shard_map/ppermute | solution.py:48
  19.3 13.0 %collective-permute-start.3 = (bf16[16,2816]{1,0:T(8,128)(2,1)S(1)}, bf16[16,2816]{1,0:T(8,128)(2,1)S(1)}, u32[]{:S(2)}, u32[]{:S(2)}) collective-permute-start(bf16[16,2816]{1,0:T(8,128)(2,1)S(1)} %slice.64), channel_id=1, source_target_pairs={{0,4},{1,5},{2,6},{3,7},{4,0},{5,1},{6,2},{7,3},{8,12},{9,13},{10,... | collective-permute-start | bytes 270344 | tf_op jit(solution)/shard_map/ppermute | solution.py:48
  22.3 4.0 %collective-permute-start.8 = (f32[8320]{0:T(1024)S(1)}, f32[8320]{0:T(1024)S(1)}, u32[]{:S(2)}, u32[]{:S(2)}) collective-permute-start(f32[8320]{0:T(1024)S(1)} %add.189), channel_id=1, source_target_pairs={{0,4},{1,5},{2,6},{3,7},{4,0},{5,1},{6,2},{7,3},{8,12},{9,13},{10,... | collective-permute-start | bytes 99848 | tf_op jit(solution)/shard_map/ppermute | solution.py:99
  26.3 4.0 %collective-permute-start.9 = (f32[8320]{0:T(1024)S(1)}, f32[8320]{0:T(1024)S(1)}, u32[]{:S(2)}, u32[]{:S(2)}) collective-permute-start(f32[8320]{0:T(1024)S(1)} %add.190), channel_id=1, source_target_pairs={{0,2},{1,3},{2,0},{3,1},{4,6},{5,7},{6,4},{7,5},{8,10},{9,11},{10,... | collective-permute-start | bytes 99848 | tf_op jit(solution)/shard_map/ppermute | solution.py:99
  30.3 3.7 %collective-permute-start.10 = (f32[8320]{0:T(1024)S(1)}, f32[8320]{0:T(1024)S(1)}, u32[]{:S(2)}, u32[]{:S(2)}) collective-permute-start(f32[8320]{0:T(1024)S(1)} %add.191), channel_id=1, source_target_pairs={{0,1},{1,0},{2,3},{3,2},{4,5},{5,4},{6,7},{7,6},{8,9},{9,8},{10,11... | collective-permute-start | bytes 99848 | tf_op jit(solution)/shard_map/ppermute | solution.py:99
  30.3 6.8 %collective-permute-start.15 = (bf16[2,16,2688]{2,1,0:T(8,128)(2,1)S(1)}, bf16[2,16,2688]{2,1,0:T(8,128)(2,1)S(1)}, u32[]{:S(2)}, u32[]{:S(2)}) collective-permute-start(bf16[2,16,2688]{2,1,0:T(8,128)(2,1)S(1)} %bitcast_dynamic-update-slice_fusion.14), channel_id=1, source_target_pairs={{0,4},{1,5},{2,6},{3,7},{4,0},{5,1},{6,2},{7,3},{8,12},{9,13},{10,... | collective-permute-start | bytes 516104 | tf_op jit(solution)/shard_map/ppermute | solution.py:48
  32.0 6.8 %collective-permute-start.12 = (bf16[2,16,2688]{2,1,0:T(8,128)(2,1)S(1)}, bf16[2,16,2688]{2,1,0:T(8,128)(2,1)S(1)}, u32[]{:S(2)}, u32[]{:S(2)}) collective-permute-start(bf16[2,16,2688]{2,1,0:T(8,128)(2,1)S(1)} %bitcast_dynamic-update-slice_fusion.16), channel_id=1, source_target_pairs={{0,1},{1,0},{2,3},{3,2},{4,5},{5,4},{6,7},{7,6},{8,9},{9,8},{10,11... | collective-permute-start | bytes 516104 | tf_op jit(solution)/shard_map/ppermute | solution.py:48
  32.4 8.2 %collective-permute-start.4 = (bf16[2,16,2816]{2,1,0:T(8,128)(2,1)S(1)}, bf16[2,16,2816]{2,1,0:T(8,128)(2,1)S(1)}, u32[]{:S(2)}, u32[]{:S(2)}) collective-permute-start(bf16[2,16,2816]{2,1,0:T(8,128)(2,1)S(1)} %bitcast_dynamic-update-slice_fusion.12), channel_id=1, source_target_pairs={{0,2},{1,3},{2,0},{3,1},{4,6},{5,7},{6,4},{7,5},{8,10},{9,11},{10,... | collective-permute-start | bytes 540680 | tf_op jit(solution)/shard_map/ppermute | solution.py:48
  35.2 5.4 %copy-start = (f32[8192]{0:T(1024)}, f32[8192]{0:T(1024)S(1)}, u32[]{:S(2)}) copy-start(f32[8192]{0:T(1024)S(1)} %fusion.27) | copy-start | bytes 98308
  37.2 9.7 %collective-permute-start.16 = (bf16[2,2,16,2688]{3,2,1,0:T(8,128)(2,1)S(1)}, bf16[2,2,16,2688]{3,2,1,0:T(8,128)(2,1)S(1)}, u32[]{:S(2)}, u32[]{:S(2)}) collective-permute-start(bf16[2,2,16,2688]{3,2,1,0:T(8,128)(2,1)S(1)} %bitcast_dynamic-update-slice_fusion.8), channel_id=1, source_target_pairs={{0,2},{1,3},{2,0},{3,1},{4,6},{5,7},{6,4},{7,5},{8,10},{9,11},{10,... | collective-permute-start | bytes 1032200 | tf_op jit(solution)/shard_map/ppermute | solution.py:48
  38.9 9.5 %collective-permute-start.13 = (bf16[2,2,16,2688]{3,2,1,0:T(8,128)(2,1)S(1)}, bf16[2,2,16,2688]{3,2,1,0:T(8,128)(2,1)S(1)}, u32[]{:S(2)}, u32[]{:S(2)}) collective-permute-start(bf16[2,2,16,2688]{3,2,1,0:T(8,128)(2,1)S(1)} %bitcast_dynamic-update-slice_fusion.10), channel_id=1, source_target_pairs={{0,4},{1,5},{2,6},{3,7},{4,0},{5,1},{6,2},{7,3},{8,12},{9,13},{10,... | collective-permute-start | bytes 1032200 | tf_op jit(solution)/shard_map/ppermute | solution.py:48
  40.6 11.7 %collective-permute-start.5 = (bf16[2,2,16,2816]{3,2,1,0:T(8,128)(2,1)S(1)}, bf16[2,2,16,2816]{3,2,1,0:T(8,128)(2,1)S(1)}, u32[]{:S(2)}, u32[]{:S(2)}) collective-permute-start(bf16[2,2,16,2816]{3,2,1,0:T(8,128)(2,1)S(1)} %bitcast_dynamic-update-slice_fusion.6), channel_id=1, source_target_pairs={{0,1},{1,0},{2,3},{3,2},{4,5},{5,4},{6,7},{7,6},{8,9},{9,8},{10,11... | collective-permute-start | bytes 1081352 | tf_op jit(solution)/shard_map/ppermute | solution.py:48
  50.3 2.0 %slice-start = ((f32[8192]{0:T(1024)}), f32[2816]{0:T(1024)S(1)}, s32[]{:S(2)}) async-start(f32[8192]{0:T(1024)} %copy-done), calls=%async_computation.1 | async-start | bytes 24576 | tf_op jit(solution)/shard_map/slice | solution.py:79

commit v4 on v3

--- a/solution.py
+++ b/solution.py
@@ -65,29 +65,52 @@
 def streamed_scores(grad_rows, queries, scaling, factors, device_count):
     rank = len(factors)
     rows = queries.shape[0]
+    row_count = grad_rows.shape[0]
     first = gather_rows(queries, factors[0], device_count)
-    rest = list(range(1, rank))
-    streams = max(len(rest), 1)
-    raw = None
-    for j, (start, size) in enumerate(column_splits(queries.shape[1], streams)):
-        order = rest[j:] + rest[:j]
+    if rank == 1:
+        prepared = (first.astype(jnp.float32) * scaling).astype(jnp.bfloat16)
+        return jnp.einsum("rk,qk->rq", grad_rows, prepared, preferred_element_type=jnp.float32)
+    middle = list(range(1, rank - 1))
+    last = rank - 1
+    splits = column_splits(queries.shape[1], max(len(middle), 1))
+    parts, orders = [], []
+    for j, (start, size) in enumerate(splits):
+        order = middle[j:] + middle[:j]
         part = first[:, start:start + size]
         for position in order:
             part = gather_factor(part, factors[position], device_count)
-        held = list(reversed(order))
-        stacked_rows = part.reshape(-1, size)
-        prepared = (stacked_rows.astype(jnp.float32) * scaling[start:start + size]).astype(jnp.bfloat16)
-        partial = jnp.einsum(
-            "rk,qk->rq", grad_rows[:, start:start + size], prepared, preferred_element_type=jnp.float32
-        )
-        shape = [factors[p][0] for p in held] + [factors[0][0], rows]
-        partial = partial.reshape((grad_rows.shape[0],) + tuple(shape))
-        canonical = [held.index(p) + 1 for p in rest]
-        lead = len(held) + 1
-        partial = jnp.transpose(partial, [0, lead] + canonical + [lead + 1])
-        partial = partial.reshape(grad_rows.shape[0], -1)
-        raw = partial if raw is None else raw + partial
-    return raw
+        parts.append(part.reshape(-1, size))
+        orders.append(order)
+    joined = jnp.concatenate(parts, axis=1) if len(parts) > 1 else parts[0]
+
+    def partial_scores(block):
+        total = None
+        for (start, size), order in zip(splits, orders):
+            prepared = (block[:, start:start + size].astype(jnp.float32) * scaling[start:start + size]).astype(
+                jnp.bfloat16
+            )
+            partial = jnp.einsum(
+                "rk,qk->rq", grad_rows[:, start:start + size], prepared, preferred_element_type=jnp.float32
+            )
+            held = list(reversed(order))
+            shape = [factors[p][0] for p in held] + [factors[0][0], rows]
+            partial = partial.reshape((row_count,) + tuple(shape))
+            axes = [0, len(held) + 1] + [held.index(p) + 1 for p in middle] + [len(held) + 2]
+            partial = jnp.transpose(partial, axes)
+            total = partial if total is None else total + partial
+        return total
+
+    size_last = factors[last][0]
+    own = coordinate(lax.axis_index(AXES), factors[last])
+    own_scores = partial_scores(joined)
+    stacked = jnp.zeros((size_last,) + own_scores.shape, jnp.float32)
+    stacked = lax.dynamic_update_index_in_dim(stacked, own_scores, own, 0)
+    for shift in range(1, size_last):
+        received = lax.ppermute(joined, AXES, shifted(factors[last], shift, device_count))
+        stacked = lax.dynamic_update_index_in_dim(stacked, partial_scores(received), (own - shift) % size_last, 0)
+    dims = stacked.ndim
+    stacked = jnp.transpose(stacked, [1] + list(range(2, dims - 1)) + [0, dims - 1])
+    return stacked.reshape(row_count, -1)
 
 
 def butterfly_sum(values, factors, device_count):

time: 65.4 us -> 61.8 us (0.945)
  starting transfers between devices: 20.9 us -> 16.3 us
  matrix products: 6.03 us -> 8.03 us
    ppermute x12 -> x7, starting transfers between devices: 16.9 us -> 12.2 us  [gather_factor(): received = lax.ppermute(piece, AXES, shifted(factor, shift, device_count))]
    ppermute x12 -> x7, waiting for transfers between devices: 9.49 us -> 6.52 us  [gather_factor(): received = lax.ppermute(piece, AXES, shifted(factor, shift, device_count))]
    ppermute x5, waiting for transfers between devices: 7.4 us -> 9.86 us  [butterfly_sum(): values = values + lax.ppermute(values, AXES, pairs)]
    dot_general x3 -> x4, matrix products: 5.82 us -> 7.82 us  [partial_scores(): jnp.einsum('rk,qk->rq', grad_rows[:, start:start + size], prepared, prefe...]
  transfers between devices with their start and end apart: 17 -> 13, of which waited for: 7 -> 7; matrix products, arithmetic and copies ran while one was open for 21% -> 21% of each run, Pallas kernels for 0% -> 0%
where the time goes in v4:
time: 61.8 us; the launch traced here: 61.6 us
  waiting for transfers between devices  16.4 us (27%)
  starting transfers between devices  16.3 us (26%)
  blocking collectives  9.83 us (16%)
  matrix products  8.03 us (13%)
  other arithmetic  7.52 us (12%)
  local copies, waits for them, and re-layouts  3 us (5%)
    ppermute x7, starting transfers between devices, gather_factor(): received = lax.ppermute(piece, AXES, shifted(factor, shift, device_count))  12.2 us
    ppermute x5, waiting for transfers between devices, butterfly_sum(): values = values + lax.ppermute(values, AXES, pairs)  9.86 us
    all_to_all x1, blocking collectives, local(): lax.all_to_all(bucket.reshape(blk_count, capacity, query_count), 'blk', s...  9.83 us
    dot_general x4, matrix products, partial_scores(): jnp.einsum('rk,qk->rq', grad_rows[:, start:start + size], prepared, prefe...  7.82 us
    ppermute x7, waiting for transfers between devices, gather_factor(): received = lax.ppermute(piece, AXES, shifted(factor, shift, device_count))  6.52 us
    ppermute x5, starting transfers between devices, butterfly_sum(): values = values + lax.ppermute(values, AXES, pairs)  4.01 us
    reduce_sum x1, other arithmetic, local(): jnp.sum(row_weights[:, None] * jnp.square(grad_rows.astype(jnp.float32)),...  3.35 us
    mul x1, other arithmetic, local(): weight_scale = row_weights * inv_root  1.28 us
  transfers between devices with their start and end apart: 13, of which 7 were waited for; matrix products, arithmetic and copies ran while one was open for 21% of the time, Pallas kernels for 0%

profile of v4, /device:TPU:0, one launch (start us, length us, event | category | flops | bytes accessed | tf_op | source)
XLA Modules:
  0.0 61.6 jit_solution(430795705845323570)
XLA Ops:
  0.0 3.1 %collective-permute-start = (bf16[4,8192]{1,0:T(4,128)(2,1)}, bf16[4,8192]{1,0:T(4,128)(2,1)S(1)}, u32[]{:S(2)}, u32[]{:S(2)}) collective-permute-start(bf16[4,8192]{1,0:T(4,128)(2,1)} %param.10), channel_id=1, source_target_pairs={{0,8},{1,9},{2,10},{3,11},{4,12},{5,13},{6,14},{7,15},{8,16},{9,17... | collective-permute-start | bytes 196616 | tf_op jit(solution)/shard_map/ppermute | solution.py:48
  3.1 2.6 %collective-permute-start.1 = (bf16[4,8192]{1,0:T(4,128)(2,1)}, bf16[4,8192]{1,0:T(4,128)(2,1)S(1)}, u32[]{:S(2)}, u32[]{:S(2)}) collective-permute-start(bf16[4,8192]{1,0:T(4,128)(2,1)} %param.10), channel_id=1, source_target_pairs={{0,16},{1,17},{2,18},{3,19},{4,20},{5,21},{6,22},{7,23},{8,24},{9,... | collective-permute-start | bytes 196616 | tf_op jit(solution)/shard_map/ppermute | solution.py:48
  5.7 1.3 %collective-permute-start.2 = (bf16[4,8192]{1,0:T(4,128)(2,1)}, bf16[4,8192]{1,0:T(4,128)(2,1)S(1)}, u32[]{:S(2)}, u32[]{:S(2)}) collective-permute-start(bf16[4,8192]{1,0:T(4,128)(2,1)} %param.10), channel_id=1, source_target_pairs={{0,24},{1,25},{2,26},{3,27},{4,28},{5,29},{6,30},{7,31},{8,0},{9,1... | collective-permute-start | bytes 196616 | tf_op jit(solution)/shard_map/ppermute | solution.py:48
  7.0 1.3 %broadcast_multiply_fusion = (f32[256]{0:T(256)S(1)}, f32[]{:T(128)}) fusion(f32[256]{0:T(256)} %param.8), kind=kLoop, calls=%fused_computation.63 | loop fusion | flops 511 | bytes 2052 | tf_op jit(solution)/shard_map/mul | solution.py:150
  8.3 3.4 %multiply_reduce_fusion = f32[8192]{0:T(1024)S(1)} fusion(bf16[256,8192]{1,0:T(8,128)(2,1)} %param.7, f32[256]{0:T(256)} %param.8), kind=kLoop, calls=%fused_computation.1 | loop fusion | flops 8380416 | bytes 4228096 | tf_op jit(solution)/shard_map/reduce_sum | solution.py:141
  12.3 0.7 %collective-permute-start.5 = (f32[8320]{0:T(1024)S(1)}, f32[8320]{0:T(1024)S(1)}, u32[]{:S(2)}, u32[]{:S(2)}) collective-permute-start(f32[8320]{0:T(1024)S(1)} %select_maximum_fusion), channel_id=1, source_target_pairs={{0,8},{1,9},{2,10},{3,11},{4,12},{5,13},{6,14},{7,15},{8,0},{9,1},... | collective-permute-start | bytes 99848 | tf_op jit(solution)/shard_map/ppermute | solution.py:122
  13.2 0.7 %gather_fusion = s32[256,8]{1,0:T(8,128)S(1)} fusion(s32[8,8]{1,0:T(8,128)S(1)} %bitcast.82, s32[1024]{0:T(1024)S(1)} %pad_clamp_fusion), kind=kCustom, calls=%fused_computation | custom fusion | bytes 17408 | tf_op jit(solution)/shard_map/jit(_take)/gather | solution.py:148
  15.2 1.1 %collective-permute-done.5 = f32[8320]{0:T(1024)S(1)} collective-permute-done((f32[8320]{0:T(1024)S(1)}, f32[8320]{0:T(1024)S(1)}, u32[]{:S(2)}, u32[]{:S(2)}) %collective-permute-start.5) | collective-permute-done | bytes 33312 | tf_op jit(solution)/shard_map/ppermute | solution.py:122
  17.5 4.8 %collective-permute-done.6 = f32[8320]{0:T(1024)S(1)} collective-permute-done((f32[8320]{0:T(1024)S(1)}, f32[8320]{0:T(1024)S(1)}, u32[]{:S(2)}, u32[]{:S(2)}) %collective-permute-start.6) | collective-permute-done | bytes 33312 | tf_op jit(solution)/shard_map/ppermute | solution.py:122
  22.3 1.5 %collective-permute-start.7 = (f32[8320]{0:T(1024)S(1)}, f32[8320]{0:T(1024)S(1)}, u32[]{:S(2)}, u32[]{:S(2)}) collective-permute-start(f32[8320]{0:T(1024)S(1)} %add.158), channel_id=1, source_target_pairs={{0,4},{1,5},{2,6},{3,7},{4,0},{5,1},{6,2},{7,3},{8,12},{9,13},{10,... | collective-permute-start | bytes 99848 | tf_op jit(solution)/shard_map/ppermute | solution.py:122
  23.9 1.6 %collective-permute-start.10 = (bf16[16,4096]{1,0:T(8,128)(2,1)S(1)}, bf16[16,4096]{1,0:T(8,128)(2,1)S(1)}, u32[]{:S(2)}, u32[]{:S(2)}) collective-permute-start(bf16[16,4096]{1,0:T(8,128)(2,1)S(1)} %get-tuple-element.20), channel_id=1, source_target_pairs={{0,2},{1,3},{2,0},{3,1},{4,6},{5,7},{6,4},{7,5},{8,10},{9,11},{10,... | collective-permute-start | bytes 393224 | tf_op jit(solution)/shard_map/ppermute | solution.py:48
  26.3 1.5 %collective-permute-start.8 = (f32[8320]{0:T(1024)S(1)}, f32[8320]{0:T(1024)S(1)}, u32[]{:S(2)}, u32[]{:S(2)}) collective-permute-start(f32[8320]{0:T(1024)S(1)} %add.159), channel_id=1, source_target_pairs={{0,2},{1,3},{2,0},{3,1},{4,6},{5,7},{6,4},{7,5},{8,10},{9,11},{10,... | collective-permute-start | bytes 99848 | tf_op jit(solution)/shard_map/ppermute | solution.py:122
  27.8 2.4 %collective-permute-done.8 = f32[8320]{0:T(1024)S(1)} collective-permute-done((f32[8320]{0:T(1024)S(1)}, f32[8320]{0:T(1024)S(1)}, u32[]{:S(2)}, u32[]{:S(2)}) %collective-permute-start.8) | collective-permute-done | bytes 33312 | tf_op jit(solution)/shard_map/ppermute | solution.py:122
  30.3 1.2 %collective-permute-done.9 = f32[8320]{0:T(1024)S(1)} collective-permute-done((f32[8320]{0:T(1024)S(1)}, f32[8320]{0:T(1024)S(1)}, u32[]{:S(2)}, u32[]{:S(2)}) %collective-permute-start.9) | collective-permute-done | bytes 33312 | tf_op jit(solution)/shard_map/ppermute | solution.py:122
  32.0 1.6 %collective-permute-start.11 = (bf16[2,16,4096]{2,1,0:T(8,128)(2,1)S(1)}, bf16[2,16,4096]{2,1,0:T(8,128)(2,1)S(1)}, u32[]{:S(2)}, u32[]{:S(2)}) collective-permute-start(bf16[2,16,4096]{2,1,0:T(8,128)(2,1)S(1)} %bitcast_dynamic-update-slice_fusion.4), channel_id=1, source_target_pairs={{0,4},{1,5},{2,6},{3,7},{4,0},{5,1},{6,2},{7,3},{8,12},{9,13},{10,... | collective-permute-start | bytes 786440 | tf_op jit(solution)/shard_map/ppermute | solution.py:48
  33.7 1.6 %collective-permute-start.4 = (bf16[2,16,4096]{2,1,0:T(8,128)(2,1)S(1)}, bf16[2,16,4096]{2,1,0:T(8,128)(2,1)S(1)}, u32[]{:S(2)}, u32[]{:S(2)}) collective-permute-start(bf16[2,16,4096]{2,1,0:T(8,128)(2,1)S(1)} %bitcast_dynamic-update-slice_fusion.6), channel_id=1, source_target_pairs={{0,2},{1,3},{2,0},{3,1},{4,6},{5,7},{6,4},{7,5},{8,10},{9,11},{10,... | collective-permute-start | bytes 786440 | tf_op jit(solution)/shard_map/ppermute | solution.py:48
  35.3 5.1 %collective-permute-done.11 = bf16[2,16,4096]{2,1,0:T(8,128)(2,1)S(1)} collective-permute-done((bf16[2,16,4096]{2,1,0:T(8,128)(2,1)S(1)}, bf16[2,16,4096]{2,1,0:T(8,128)(2,1)S(1)}, u32[]{:S(2)}, u32[]{:S(2)}) %collective-permute-start.11) | collective-permute-done | bytes 262176 | tf_op jit(solution)/shard_map/ppermute | solution.py:48
  40.5 1.4 %collective-permute-done.4 = bf16[2,16,4096]{2,1,0:T(8,128)(2,1)S(1)} collective-permute-done((bf16[2,16,4096]{2,1,0:T(8,128)(2,1)S(1)}, bf16[2,16,4096]{2,1,0:T(8,128)(2,1)S(1)}, u32[]{:S(2)}, u32[]{:S(2)}) %collective-permute-start.4) | collective-permute-done | bytes 262176 | tf_op jit(solution)/shard_map/ppermute | solution.py:48
  42.0 0.7 %fusion.29 = f32[8192]{0:T(1024)S(1)} fusion(f32[8320]{0:T(1024)S(1)} %add.161, f32[]{:T(128)} %bitcast.14), kind=kLoop, calls=%fused_computation.50 | loop fusion | flops 16384 | bytes 65540 | tf_op jit(solution)/shard_map/rsqrt | solution.py:145
  42.7 0.8 %fusion.14 = f32[256,64]{0,1:T(8,128)S(1)} fusion(bf16[256,8192]{1,0:T(8,128)(2,1)S(1)} %copy-done, bf16[64,4096]{1,0:T(8,128)(2,1)S(1)} %bitcast.86, f32[4096]{0:T(1024)S(1)} %get-tuple-element.22), kind=kOutput, calls=%fused_computation.13 | convolution fusion | flops 135004160 | bytes 2703360 | tf_op jit(solution)/shard_map/rk,qk->rq/dot_general | solution.py:92
  43.5 2.4 %fusion.8 = f32[256,64]{0,1:T(8,128)S(1)} fusion(bf16[256,8192]{1,0:T(8,128)(2,1)} %param.7, bf16[64,4096]{1,0:T(8,128)(2,1)S(1)} %bitcast.84, f32[4096]{0:T(1024)S(1)} %get-tuple-element.21), kind=kOutput, calls=%fused_computation.11 | convolution fusion | flops 135004160 | bytes 2703360 | tf_op jit(solution)/shard_map/rk,qk->rq/dot_general | solution.py:92
  46.0 2.4 %fusion.17 = f32[256,64]{0,1:T(8,128)S(1)} fusion(bf16[256,8192]{1,0:T(8,128)(2,1)} %param.7, bf16[64,8192]{1,0:T(8,128)(2,1)S(1)} %collective-permute-done.12, f32[4096]{0:T(1024)S(1)} %get-tuple-element.22), kind=kOutput, calls=%fused_computation.14 | convolution fusion | flops 135004160 | bytes 2703360 | tf_op jit(solution)/shard_map/rk,qk->rq/dot_general | solution.py:92
  48.4 2.4 %fusion.11 = f32[256,64]{0,1:T(8,128)S(1)} fusion(bf16[256,8192]{1,0:T(8,128)(2,1)} %param.7, bf16[64,8192]{1,0:T(8,128)(2,1)S(1)} %collective-permute-done.12, f32[4096]{0:T(1024)S(1)} %get-tuple-element.21), kind=kOutput, calls=%fused_computation.12 | convolution fusion | flops 135004160 | bytes 2703360 | tf_op jit(solution)/shard_map/rk,qk->rq/dot_general | solution.py:92
  51.1 9.8 %all_to_all.5 = bf16[8,48,128]{2,1,0:T(8,128)(2,1)S(1)} all-to-all(bf16[8,48,128]{2,1,0:T(8,128)(2,1)S(1)} %bitcast.89), channel_id=1, replica_groups=mesh['blk'=8,'harvest'=4] {'blk'}, dimensions={0} | all-to-all | bytes 196608 | tf_op jit(solution)/shard_map/all_to_all | solution.py:160
  (70 shorter events, 5.9 us)
Async XLA Ops:
  0.0 14.9 %copy-start.1 = (bf16[4,8192]{1,0:T(4,128)(2,1)S(1)}, bf16[4,8192]{1,0:T(4,128)(2,1)}, u32[]{:S(2)}) copy-start(bf16[4,8192]{1,0:T(4,128)(2,1)} %param.10) | copy-start | bytes 196612
  0.0 13.1 %copy-start.3 = (s32[8,8]{1,0:T(8,128)S(1)}, s32[8,8]{1,0:T(8,128)}, u32[]{:S(2)}) copy-start(s32[8,8]{1,0:T(8,128)} %param.11) | copy-start | bytes 772
  0.0 13.1 %copy-start.2 = (s32[256,1]{0,1:T(1,128)S(1)}, s32[256,1]{0,1:T(1,128)}, u32[]{:S(2)}) copy-start(s32[256,1]{0,1:T(1,128)} %param.9) | copy-start | bytes 3076
  0.0 17.3 %collective-permute-start = (bf16[4,8192]{1,0:T(4,128)(2,1)}, bf16[4,8192]{1,0:T(4,128)(2,1)S(1)}, u32[]{:S(2)}, u32[]{:S(2)}) collective-permute-start(bf16[4,8192]{1,0:T(4,128)(2,1)} %param.10), channel_id=1, source_target_pairs={{0,8},{1,9},{2,10},{3,11},{4,12},{5,13},{6,14},{7,15},{8,16},{9,17... | collective-permute-start | bytes 196616 | tf_op jit(solution)/shard_map/ppermute | solution.py:48
  3.1 14.2 %collective-permute-start.1 = (bf16[4,8192]{1,0:T(4,128)(2,1)}, bf16[4,8192]{1,0:T(4,128)(2,1)S(1)}, u32[]{:S(2)}, u32[]{:S(2)}) collective-permute-start(bf16[4,8192]{1,0:T(4,128)(2,1)} %param.10), channel_id=1, source_target_pairs={{0,16},{1,17},{2,18},{3,19},{4,20},{5,21},{6,22},{7,23},{8,24},{9,... | collective-permute-start | bytes 196616 | tf_op jit(solution)/shard_map/ppermute | solution.py:48
  5.7 11.7 %collective-permute-start.2 = (bf16[4,8192]{1,0:T(4,128)(2,1)}, bf16[4,8192]{1,0:T(4,128)(2,1)S(1)}, u32[]{:S(2)}, u32[]{:S(2)}) collective-permute-start(bf16[4,8192]{1,0:T(4,128)(2,1)} %param.10), channel_id=1, source_target_pairs={{0,24},{1,25},{2,26},{3,27},{4,28},{5,29},{6,30},{7,31},{8,0},{9,1... | collective-permute-start | bytes 196616 | tf_op jit(solution)/shard_map/ppermute | solution.py:48
  12.3 4.0 %collective-permute-start.5 = (f32[8320]{0:T(1024)S(1)}, f32[8320]{0:T(1024)S(1)}, u32[]{:S(2)}, u32[]{:S(2)}) collective-permute-start(f32[8320]{0:T(1024)S(1)} %select_maximum_fusion), channel_id=1, source_target_pairs={{0,8},{1,9},{2,10},{3,11},{4,12},{5,13},{6,14},{7,15},{8,0},{9,1},... | collective-permute-start | bytes 99848 | tf_op jit(solution)/shard_map/ppermute | solution.py:122
  17.0 5.3 %collective-permute-start.6 = (f32[8320]{0:T(1024)S(1)}, f32[8320]{0:T(1024)S(1)}, u32[]{:S(2)}, u32[]{:S(2)}) collective-permute-start(f32[8320]{0:T(1024)S(1)} %fusion.33), channel_id=1, source_target_pairs={{0,16},{1,17},{2,18},{3,19},{4,20},{5,21},{6,22},{7,23},{8,24},{9,... | collective-permute-start | bytes 99848 | tf_op jit(solution)/shard_map/ppermute | solution.py:122
  17.5 25.3 %copy-start = (bf16[256,8192]{1,0:T(8,128)(2,1)S(1)}, bf16[256,8192]{1,0:T(8,128)(2,1)}, u32[]{:S(2)}) copy-start(bf16[256,8192]{1,0:T(8,128)(2,1)} %param.7) | copy-start | bytes 12582916
  22.3 4.0 %collective-permute-start.7 = (f32[8320]{0:T(1024)S(1)}, f32[8320]{0:T(1024)S(1)}, u32[]{:S(2)}, u32[]{:S(2)}) collective-permute-start(f32[8320]{0:T(1024)S(1)} %add.158), channel_id=1, source_target_pairs={{0,4},{1,5},{2,6},{3,7},{4,0},{5,1},{6,2},{7,3},{8,12},{9,13},{10,... | collective-permute-start | bytes 99848 | tf_op jit(solution)/shard_map/ppermute | solution.py:122
  23.9 8.1 %collective-permute-start.10 = (bf16[16,4096]{1,0:T(8,128)(2,1)S(1)}, bf16[16,4096]{1,0:T(8,128)(2,1)S(1)}, u32[]{:S(2)}, u32[]{:S(2)}) collective-permute-start(bf16[16,4096]{1,0:T(8,128)(2,1)S(1)} %get-tuple-element.20), channel_id=1, source_target_pairs={{0,2},{1,3},{2,0},{3,1},{4,6},{5,7},{6,4},{7,5},{8,10},{9,11},{10,... | collective-permute-start | bytes 393224 | tf_op jit(solution)/shard_map/ppermute | solution.py:48
  25.4 8.2 %collective-permute-start.3 = (bf16[16,4096]{1,0:T(8,128)(2,1)S(1)}, bf16[16,4096]{1,0:T(8,128)(2,1)S(1)}, u32[]{:S(2)}, u32[]{:S(2)}) collective-permute-start(bf16[16,4096]{1,0:T(8,128)(2,1)S(1)} %get-tuple-element.19), channel_id=1, source_target_pairs={{0,4},{1,5},{2,6},{3,7},{4,0},{5,1},{6,2},{7,3},{8,12},{9,13},{10,... | collective-permute-start | bytes 393224 | tf_op jit(solution)/shard_map/ppermute | solution.py:48
  26.3 4.0 %collective-permute-start.8 = (f32[8320]{0:T(1024)S(1)}, f32[8320]{0:T(1024)S(1)}, u32[]{:S(2)}, u32[]{:S(2)}) collective-permute-start(f32[8320]{0:T(1024)S(1)} %add.159), channel_id=1, source_target_pairs={{0,2},{1,3},{2,0},{3,1},{4,6},{5,7},{6,4},{7,5},{8,10},{9,11},{10,... | collective-permute-start | bytes 99848 | tf_op jit(solution)/shard_map/ppermute | solution.py:122
  30.3 1.2 %collective-permute-start.9 = (f32[8320]{0:T(1024)S(1)}, f32[8320]{0:T(1024)S(1)}, u32[]{:S(2)}, u32[]{:S(2)}) collective-permute-start(f32[8320]{0:T(1024)S(1)} %add.160), channel_id=1, source_target_pairs={{0,1},{1,0},{2,3},{3,2},{4,5},{5,4},{6,7},{7,6},{8,9},{9,8},{10,11... | collective-permute-start | bytes 99848 | tf_op jit(solution)/shard_map/ppermute | solution.py:122
  32.0 8.4 %collective-permute-start.11 = (bf16[2,16,4096]{2,1,0:T(8,128)(2,1)S(1)}, bf16[2,16,4096]{2,1,0:T(8,128)(2,1)S(1)}, u32[]{:S(2)}, u32[]{:S(2)}) collective-permute-start(bf16[2,16,4096]{2,1,0:T(8,128)(2,1)S(1)} %bitcast_dynamic-update-slice_fusion.4), channel_id=1, source_target_pairs={{0,4},{1,5},{2,6},{3,7},{4,0},{5,1},{6,2},{7,3},{8,12},{9,13},{10,... | collective-permute-start | bytes 786440 | tf_op jit(solution)/shard_map/ppermute | solution.py:48
  33.7 8.2 %collective-permute-start.4 = (bf16[2,16,4096]{2,1,0:T(8,128)(2,1)S(1)}, bf16[2,16,4096]{2,1,0:T(8,128)(2,1)S(1)}, u32[]{:S(2)}, u32[]{:S(2)}) collective-permute-start(bf16[2,16,4096]{2,1,0:T(8,128)(2,1)S(1)} %bitcast_dynamic-update-slice_fusion.6), channel_id=1, source_target_pairs={{0,2},{1,3},{2,0},{3,1},{4,6},{5,7},{6,4},{7,5},{8,10},{9,11},{10,... | collective-permute-start | bytes 786440 | tf_op jit(solution)/shard_map/ppermute | solution.py:48
  42.0 4.0 %collective-permute-start.12 = (bf16[64,8192]{1,0:T(8,128)(2,1)S(1)}, bf16[64,8192]{1,0:T(8,128)(2,1)S(1)}, u32[]{:S(2)}, u32[]{:S(2)}) collective-permute-start(bf16[64,8192]{1,0:T(8,128)(2,1)S(1)} %pad_maximum_fusion), channel_id=1, source_target_pairs={{0,1},{1,0},{2,3},{3,2},{4,5},{5,4},{6,7},{7,6},{8,9},{9,8},{10,11... | collective-permute-start | bytes 3145736 | tf_op jit(solution)/shard_map/ppermute | solution.py:109

commit v5 on v4

--- a/solution.py
+++ b/solution.py
@@ -62,11 +62,10 @@
     return list(zip(starts, sizes))
 
 
-def streamed_scores(grad_rows, queries, scaling, factors, device_count):
+def streamed_scores(grad_rows, queries, scaling, factors, device_count, first):
     rank = len(factors)
     rows = queries.shape[0]
     row_count = grad_rows.shape[0]
-    first = gather_rows(queries, factors[0], device_count)
     if rank == 1:
         prepared = (first.astype(jnp.float32) * scaling).astype(jnp.bfloat16)
         return jnp.einsum("rk,qk->rq", grad_rows, prepared, preferred_element_type=jnp.float32)
@@ -140,10 +139,12 @@
 
     squares = jnp.sum(row_weights[:, None] * jnp.square(grad_rows.astype(jnp.float32)), axis=0)
     packed = jnp.concatenate([squares, jnp.zeros((128,), jnp.float32).at[0].set(jnp.sum(row_weights))])
+    first = gather_rows(queries, factors[0], device_count)
+    first, packed = lax.optimization_barrier((first, packed))
     packed = butterfly_sum(packed, factors, device_count)
     total_sq, total_weight = packed[:width], packed[width]
     scaling = lax.rsqrt(total_sq / total_weight + 1e-06)
-    raw = streamed_scores(grad_rows, queries, scaling, factors, device_count)
+    raw = streamed_scores(grad_rows, queries, scaling, factors, device_count, first)
     owner_ids = destinations[:, 0]
     pattern_rows = jnp.take(tile_pattern.T, owner_ids, axis=0).astype(jnp.float32)
     full_mask = jnp.repeat(pattern_rows, block_size, axis=1)

time: 61.8 us -> 58 us (0.939)
  waiting for transfers between devices: 16.4 us -> 12.1 us
  starting transfers between devices: 16.3 us -> 17.4 us
  other arithmetic: 7.52 us -> 6.88 us
    ppermute x7, waiting for transfers between devices: 6.52 us -> 3.97 us  [gather_factor(): received = lax.ppermute(piece, AXES, shifted(factor, shift, device_count))]
    ppermute x5, waiting for transfers between devices: 9.86 us -> 8.1 us  [butterfly_sum(): values = values + lax.ppermute(values, AXES, pairs)]
    ppermute x5, starting transfers between devices: 4.01 us -> 5.18 us  [butterfly_sum(): values = values + lax.ppermute(values, AXES, pairs)]
    add x5, other arithmetic: 0.68 us -> 0.03 us  [butterfly_sum(): values = values + lax.ppermute(values, AXES, pairs)]
where the time goes in v5:
time: 58 us; the launch traced here: 57.7 us
  starting transfers between devices  17.4 us (30%)
  waiting for transfers between devices  12.1 us (21%)
  blocking collectives  9.83 us (17%)
  matrix products  8.03 us (14%)
  other arithmetic  6.88 us (12%)
  local copies, waits for them, and re-layouts  2.99 us (5%)
    ppermute x7, starting transfers between devices, gather_factor(): received = lax.ppermute(piece, AXES, shifted(factor, shift, device_count))  12.1 us
    all_to_all x1, blocking collectives, local(): lax.all_to_all(bucket.reshape(blk_count, capacity, query_count), 'blk', s...  9.83 us
    ppermute x5, waiting for transfers between devices, butterfly_sum(): values = values + lax.ppermute(values, AXES, pairs)  8.1 us
    dot_general x4, matrix products, partial_scores(): jnp.einsum('rk,qk->rq', grad_rows[:, start:start + size], prepared, prefe...  7.82 us
    ppermute x5, starting transfers between devices, butterfly_sum(): values = values + lax.ppermute(values, AXES, pairs)  5.18 us
    ppermute x7, waiting for transfers between devices, gather_factor(): received = lax.ppermute(piece, AXES, shifted(factor, shift, device_count))  3.97 us
    reduce_sum x1, other arithmetic, local(): jnp.sum(row_weights[:, None] * jnp.square(grad_rows.astype(jnp.float32)),...  3.35 us
    mul x1, other arithmetic, local(): weight_scale = row_weights * inv_root  1.28 us
  transfers between devices with their start and end apart: 13, of which 7 were waited for; matrix products, arithmetic and copies ran while one was open for 21% of the time, Pallas kernels for 0%

profile of v5, /device:TPU:0, one launch (start us, length us, event | category | flops | bytes accessed | tf_op | source)
XLA Modules:
  0.0 57.7 jit_solution(11483890489751247630)
XLA Ops:
  0.0 3.1 %collective-permute-start = (bf16[4,8192]{1,0:T(4,128)(2,1)}, bf16[4,8192]{1,0:T(4,128)(2,1)S(1)}, u32[]{:S(2)}, u32[]{:S(2)}) collective-permute-start(bf16[4,8192]{1,0:T(4,128)(2,1)} %param.10), channel_id=1, source_target_pairs={{0,8},{1,9},{2,10},{3,11},{4,12},{5,13},{6,14},{7,15},{8,16},{9,17... | collective-permute-start | bytes 196616 | tf_op jit(solution)/shard_map/ppermute | solution.py:48
  3.1 2.6 %collective-permute-start.1 = (bf16[4,8192]{1,0:T(4,128)(2,1)}, bf16[4,8192]{1,0:T(4,128)(2,1)S(1)}, u32[]{:S(2)}, u32[]{:S(2)}) collective-permute-start(bf16[4,8192]{1,0:T(4,128)(2,1)} %param.10), channel_id=1, source_target_pairs={{0,16},{1,17},{2,18},{3,19},{4,20},{5,21},{6,22},{7,23},{8,24},{9,... | collective-permute-start | bytes 196616 | tf_op jit(solution)/shard_map/ppermute | solution.py:48
  5.7 1.3 %collective-permute-start.2 = (bf16[4,8192]{1,0:T(4,128)(2,1)}, bf16[4,8192]{1,0:T(4,128)(2,1)S(1)}, u32[]{:S(2)}, u32[]{:S(2)}) collective-permute-start(bf16[4,8192]{1,0:T(4,128)(2,1)} %param.10), channel_id=1, source_target_pairs={{0,24},{1,25},{2,26},{3,27},{4,28},{5,29},{6,30},{7,31},{8,0},{9,1... | collective-permute-start | bytes 196616 | tf_op jit(solution)/shard_map/ppermute | solution.py:48
  7.0 1.3 %broadcast_multiply_fusion = (f32[256]{0:T(256)S(1)}, f32[]{:T(128)}) fusion(f32[256]{0:T(256)} %param.8), kind=kLoop, calls=%fused_computation.63 | loop fusion | flops 511 | bytes 2052 | tf_op jit(solution)/shard_map/mul | solution.py:151
  8.3 3.4 %multiply_reduce_fusion = f32[8192]{0:T(1024)S(1)} fusion(bf16[256,8192]{1,0:T(8,128)(2,1)} %param.7, f32[256]{0:T(256)} %param.8), kind=kLoop, calls=%fused_computation.1 | loop fusion | flops 8380416 | bytes 4228096 | tf_op jit(solution)/shard_map/reduce_sum | solution.py:140
  11.8 0.7 %gather_fusion = s32[256,8]{1,0:T(8,128)S(1)} fusion(s32[8,8]{1,0:T(8,128)S(1)} %bitcast.82, s32[1024]{0:T(1024)S(1)} %pad_clamp_fusion), kind=kCustom, calls=%fused_computation | custom fusion | bytes 17408 | tf_op jit(solution)/shard_map/jit(_take)/gather | solution.py:149
  13.6 0.7 %select_maximum_fusion = f32[8320]{0:T(1024)S(1)} fusion(f32[1]{0:T(128)} %bitcast.8, f32[8192]{0:T(1024)S(1)} %multiply_reduce_fusion), kind=kLoop, calls=%fused_computation.46 | loop fusion | flops 24960 | bytes 66052 | tf_op jit(solution)/shard_map/concatenate | solution.py:141
  14.8 0.7 %collective-permute-start.5 = (f32[8320]{0:T(1024)S(1)}, f32[8320]{0:T(1024)S(1)}, u32[]{:S(2)}, u32[]{:S(2)}) collective-permute-start(f32[8320]{0:T(1024)S(1)} %select_maximum_fusion), channel_id=1, source_target_pairs={{0,8},{1,9},{2,10},{3,11},{4,12},{5,13},{6,14},{7,15},{8,0},{9,1},... | collective-permute-start | bytes 99848 | tf_op jit(solution)/shard_map/ppermute | solution.py:121
  15.5 1.6 %collective-permute-start.10 = (bf16[16,4096]{1,0:T(8,128)(2,1)S(1)}, bf16[16,4096]{1,0:T(8,128)(2,1)S(1)}, u32[]{:S(2)}, u32[]{:S(2)}) collective-permute-start(bf16[16,4096]{1,0:T(8,128)(2,1)S(1)} %get-tuple-element.24), channel_id=1, source_target_pairs={{0,2},{1,3},{2,0},{3,1},{4,6},{5,7},{6,4},{7,5},{8,10},{9,11},{10,... | collective-permute-start | bytes 393224 | tf_op jit(solution)/shard_map/ppermute | solution.py:48
  17.1 1.5 %collective-permute-start.3 = (bf16[16,4096]{1,0:T(8,128)(2,1)S(1)}, bf16[16,4096]{1,0:T(8,128)(2,1)S(1)}, u32[]{:S(2)}, u32[]{:S(2)}) collective-permute-start(bf16[16,4096]{1,0:T(8,128)(2,1)S(1)} %get-tuple-element.23), channel_id=1, source_target_pairs={{0,4},{1,5},{2,6},{3,7},{4,0},{5,1},{6,2},{7,3},{8,12},{9,13},{10,... | collective-permute-start | bytes 393224 | tf_op jit(solution)/shard_map/ppermute | solution.py:48
  19.1 4.6 %collective-permute-done.6 = f32[8320]{0:T(1024)S(1)} collective-permute-done((f32[8320]{0:T(1024)S(1)}, f32[8320]{0:T(1024)S(1)}, u32[]{:S(2)}, u32[]{:S(2)}) %collective-permute-start.6) | collective-permute-done | bytes 33312 | tf_op jit(solution)/shard_map/ppermute | solution.py:121
  23.6 1.9 %collective-permute-start.7 = (f32[8320]{0:T(1024)S(1)}, f32[8320]{0:T(1024)S(1)}, u32[]{:S(2)}, u32[]{:S(2)}) collective-permute-start(f32[8320]{0:T(1024)S(1)} %add.158), channel_id=1, source_target_pairs={{0,4},{1,5},{2,6},{3,7},{4,0},{5,1},{6,2},{7,3},{8,12},{9,13},{10,... | collective-permute-start | bytes 99848 | tf_op jit(solution)/shard_map/ppermute | solution.py:121
  25.6 2.0 %collective-permute-done.7 = f32[8320]{0:T(1024)S(1)} collective-permute-done((f32[8320]{0:T(1024)S(1)}, f32[8320]{0:T(1024)S(1)}, u32[]{:S(2)}, u32[]{:S(2)}) %collective-permute-start.7) | collective-permute-done | bytes 33312 | tf_op jit(solution)/shard_map/ppermute | solution.py:121
  27.6 2.3 %collective-permute-start.8 = (f32[8320]{0:T(1024)S(1)}, f32[8320]{0:T(1024)S(1)}, u32[]{:S(2)}, u32[]{:S(2)}) collective-permute-start(f32[8320]{0:T(1024)S(1)} %add.159), channel_id=1, source_target_pairs={{0,2},{1,3},{2,0},{3,1},{4,6},{5,7},{6,4},{7,5},{8,10},{9,11},{10,... | collective-permute-start | bytes 99848 | tf_op jit(solution)/shard_map/ppermute | solution.py:121
  29.9 1.6 %collective-permute-start.11 = (bf16[2,16,4096]{2,1,0:T(8,128)(2,1)S(1)}, bf16[2,16,4096]{2,1,0:T(8,128)(2,1)S(1)}, u32[]{:S(2)}, u32[]{:S(2)}) collective-permute-start(bf16[2,16,4096]{2,1,0:T(8,128)(2,1)S(1)} %bitcast_dynamic-update-slice_fusion.4), channel_id=1, source_target_pairs={{0,4},{1,5},{2,6},{3,7},{4,0},{5,1},{6,2},{7,3},{8,12},{9,13},{10,... | collective-permute-start | bytes 786440 | tf_op jit(solution)/shard_map/ppermute | solution.py:48
  32.4 1.1 %collective-permute-done.9 = f32[8320]{0:T(1024)S(1)} collective-permute-done((f32[8320]{0:T(1024)S(1)}, f32[8320]{0:T(1024)S(1)}, u32[]{:S(2)}, u32[]{:S(2)}) %collective-permute-start.9) | collective-permute-done | bytes 33312 | tf_op jit(solution)/shard_map/ppermute | solution.py:121
  34.0 2.3 %collective-permute-done.11 = bf16[2,16,4096]{2,1,0:T(8,128)(2,1)S(1)} collective-permute-done((bf16[2,16,4096]{2,1,0:T(8,128)(2,1)S(1)}, bf16[2,16,4096]{2,1,0:T(8,128)(2,1)S(1)}, u32[]{:S(2)}, u32[]{:S(2)}) %collective-permute-start.11) | collective-permute-done | bytes 262176 | tf_op jit(solution)/shard_map/ppermute | solution.py:48
  36.4 1.6 %collective-permute-done.4 = bf16[2,16,4096]{2,1,0:T(8,128)(2,1)S(1)} collective-permute-done((bf16[2,16,4096]{2,1,0:T(8,128)(2,1)S(1)}, bf16[2,16,4096]{2,1,0:T(8,128)(2,1)S(1)}, u32[]{:S(2)}, u32[]{:S(2)}) %collective-permute-start.4) | collective-permute-done | bytes 262176 | tf_op jit(solution)/shard_map/ppermute | solution.py:48
  38.2 0.7 %fusion.29 = f32[8192]{0:T(1024)S(1)} fusion(f32[8320]{0:T(1024)S(1)} %add.161, f32[]{:T(128)} %bitcast.14), kind=kLoop, calls=%fused_computation.50 | loop fusion | flops 16384 | bytes 65540 | tf_op jit(solution)/shard_map/rsqrt | solution.py:146
  38.9 0.8 %fusion.14 = f32[256,64]{0,1:T(8,128)S(1)} fusion(bf16[256,8192]{1,0:T(8,128)(2,1)S(1)} %copy-done, bf16[64,4096]{1,0:T(8,128)(2,1)S(1)} %bitcast.86, f32[4096]{0:T(1024)S(1)} %get-tuple-element.26), kind=kOutput, calls=%fused_computation.13 | convolution fusion | flops 135004160 | bytes 2703360 | tf_op jit(solution)/shard_map/rk,qk->rq/dot_general | solution.py:91
  39.7 2.4 %fusion.8 = f32[256,64]{0,1:T(8,128)S(1)} fusion(bf16[256,8192]{1,0:T(8,128)(2,1)} %param.7, bf16[64,4096]{1,0:T(8,128)(2,1)S(1)} %bitcast.84, f32[4096]{0:T(1024)S(1)} %get-tuple-element.25), kind=kOutput, calls=%fused_computation.11 | convolution fusion | flops 135004160 | bytes 2703360 | tf_op jit(solution)/shard_map/rk,qk->rq/dot_general | solution.py:91
  42.1 2.4 %fusion.17 = f32[256,64]{0,1:T(8,128)S(1)} fusion(bf16[256,8192]{1,0:T(8,128)(2,1)} %param.7, bf16[64,8192]{1,0:T(8,128)(2,1)S(1)} %collective-permute-done.12, f32[4096]{0:T(1024)S(1)} %get-tuple-element.26), kind=kOutput, calls=%fused_computation.14 | convolution fusion | flops 135004160 | bytes 2703360 | tf_op jit(solution)/shard_map/rk,qk->rq/dot_general | solution.py:91
  44.5 2.4 %fusion.11 = f32[256,64]{0,1:T(8,128)S(1)} fusion(bf16[256,8192]{1,0:T(8,128)(2,1)} %param.7, bf16[64,8192]{1,0:T(8,128)(2,1)S(1)} %collective-permute-done.12, f32[4096]{0:T(1024)S(1)} %get-tuple-element.25), kind=kOutput, calls=%fused_computation.12 | convolution fusion | flops 135004160 | bytes 2703360 | tf_op jit(solution)/shard_map/rk,qk->rq/dot_general | solution.py:91
  47.2 9.8 %all_to_all.5 = bf16[8,48,128]{2,1,0:T(8,128)(2,1)S(1)} all-to-all(bf16[8,48,128]{2,1,0:T(8,128)(2,1)S(1)} %bitcast.89), channel_id=1, replica_groups=mesh['blk'=8,'harvest'=4] {'blk'}, dimensions={0} | all-to-all | bytes 196608 | tf_op jit(solution)/shard_map/all_to_all | solution.py:161
  (70 shorter events, 4.6 us)
Async XLA Ops:
  0.0 13.5 %copy-start.1 = (bf16[4,8192]{1,0:T(4,128)(2,1)S(1)}, bf16[4,8192]{1,0:T(4,128)(2,1)}, u32[]{:S(2)}) copy-start(bf16[4,8192]{1,0:T(4,128)(2,1)} %param.10) | copy-start | bytes 196612
  0.0 11.7 %copy-start.3 = (s32[8,8]{1,0:T(8,128)S(1)}, s32[8,8]{1,0:T(8,128)}, u32[]{:S(2)}) copy-start(s32[8,8]{1,0:T(8,128)} %param.11) | copy-start | bytes 772
  0.0 11.7 %copy-start.2 = (s32[256,1]{0,1:T(1,128)S(1)}, s32[256,1]{0,1:T(1,128)}, u32[]{:S(2)}) copy-start(s32[256,1]{0,1:T(1,128)} %param.9) | copy-start | bytes 3076
  0.0 14.5 %collective-permute-start = (bf16[4,8192]{1,0:T(4,128)(2,1)}, bf16[4,8192]{1,0:T(4,128)(2,1)S(1)}, u32[]{:S(2)}, u32[]{:S(2)}) collective-permute-start(bf16[4,8192]{1,0:T(4,128)(2,1)} %param.10), channel_id=1, source_target_pairs={{0,8},{1,9},{2,10},{3,11},{4,12},{5,13},{6,14},{7,15},{8,16},{9,17... | collective-permute-start | bytes 196616 | tf_op jit(solution)/shard_map/ppermute | solution.py:48
  3.1 11.5 %collective-permute-start.1 = (bf16[4,8192]{1,0:T(4,128)(2,1)}, bf16[4,8192]{1,0:T(4,128)(2,1)S(1)}, u32[]{:S(2)}, u32[]{:S(2)}) collective-permute-start(bf16[4,8192]{1,0:T(4,128)(2,1)} %param.10), channel_id=1, source_target_pairs={{0,16},{1,17},{2,18},{3,19},{4,20},{5,21},{6,22},{7,23},{8,24},{9,... | collective-permute-start | bytes 196616 | tf_op jit(solution)/shard_map/ppermute | solution.py:48
  5.7 8.9 %collective-permute-start.2 = (bf16[4,8192]{1,0:T(4,128)(2,1)}, bf16[4,8192]{1,0:T(4,128)(2,1)S(1)}, u32[]{:S(2)}, u32[]{:S(2)}) collective-permute-start(bf16[4,8192]{1,0:T(4,128)(2,1)} %param.10), channel_id=1, source_target_pairs={{0,24},{1,25},{2,26},{3,27},{4,28},{5,29},{6,30},{7,31},{8,0},{9,1... | collective-permute-start | bytes 196616 | tf_op jit(solution)/shard_map/ppermute | solution.py:48
  14.7 24.1 %copy-start = (bf16[256,8192]{1,0:T(8,128)(2,1)S(1)}, bf16[256,8192]{1,0:T(8,128)(2,1)}, u32[]{:S(2)}) copy-start(bf16[256,8192]{1,0:T(8,128)(2,1)} %param.7) | copy-start | bytes 12582916
  14.8 4.0 %collective-permute-start.5 = (f32[8320]{0:T(1024)S(1)}, f32[8320]{0:T(1024)S(1)}, u32[]{:S(2)}, u32[]{:S(2)}) collective-permute-start(f32[8320]{0:T(1024)S(1)} %select_maximum_fusion), channel_id=1, source_target_pairs={{0,8},{1,9},{2,10},{3,11},{4,12},{5,13},{6,14},{7,15},{8,0},{9,1},... | collective-permute-start | bytes 99848 | tf_op jit(solution)/shard_map/ppermute | solution.py:121
  15.5 14.4 %collective-permute-start.10 = (bf16[16,4096]{1,0:T(8,128)(2,1)S(1)}, bf16[16,4096]{1,0:T(8,128)(2,1)S(1)}, u32[]{:S(2)}, u32[]{:S(2)}) collective-permute-start(bf16[16,4096]{1,0:T(8,128)(2,1)S(1)} %get-tuple-element.24), channel_id=1, source_target_pairs={{0,2},{1,3},{2,0},{3,1},{4,6},{5,7},{6,4},{7,5},{8,10},{9,11},{10,... | collective-permute-start | bytes 393224 | tf_op jit(solution)/shard_map/ppermute | solution.py:48
  17.1 14.5 %collective-permute-start.3 = (bf16[16,4096]{1,0:T(8,128)(2,1)S(1)}, bf16[16,4096]{1,0:T(8,128)(2,1)S(1)}, u32[]{:S(2)}, u32[]{:S(2)}) collective-permute-start(bf16[16,4096]{1,0:T(8,128)(2,1)S(1)} %get-tuple-element.23), channel_id=1, source_target_pairs={{0,4},{1,5},{2,6},{3,7},{4,0},{5,1},{6,2},{7,3},{8,12},{9,13},{10,... | collective-permute-start | bytes 393224 | tf_op jit(solution)/shard_map/ppermute | solution.py:48
  18.8 4.9 %collective-permute-start.6 = (f32[8320]{0:T(1024)S(1)}, f32[8320]{0:T(1024)S(1)}, u32[]{:S(2)}, u32[]{:S(2)}) collective-permute-start(f32[8320]{0:T(1024)S(1)} %add.157), channel_id=1, source_target_pairs={{0,16},{1,17},{2,18},{3,19},{4,20},{5,21},{6,22},{7,23},{8,24},{9,... | collective-permute-start | bytes 99848 | tf_op jit(solution)/shard_map/ppermute | solution.py:121
  23.6 4.0 %collective-permute-start.7 = (f32[8320]{0:T(1024)S(1)}, f32[8320]{0:T(1024)S(1)}, u32[]{:S(2)}, u32[]{:S(2)}) collective-permute-start(f32[8320]{0:T(1024)S(1)} %add.158), channel_id=1, source_target_pairs={{0,4},{1,5},{2,6},{3,7},{4,0},{5,1},{6,2},{7,3},{8,12},{9,13},{10,... | collective-permute-start | bytes 99848 | tf_op jit(solution)/shard_map/ppermute | solution.py:121
  27.6 4.7 %collective-permute-start.8 = (f32[8320]{0:T(1024)S(1)}, f32[8320]{0:T(1024)S(1)}, u32[]{:S(2)}, u32[]{:S(2)}) collective-permute-start(f32[8320]{0:T(1024)S(1)} %add.159), channel_id=1, source_target_pairs={{0,2},{1,3},{2,0},{3,1},{4,6},{5,7},{6,4},{7,5},{8,10},{9,11},{10,... | collective-permute-start | bytes 99848 | tf_op jit(solution)/shard_map/ppermute | solution.py:121
  29.9 6.4 %collective-permute-start.11 = (bf16[2,16,4096]{2,1,0:T(8,128)(2,1)S(1)}, bf16[2,16,4096]{2,1,0:T(8,128)(2,1)S(1)}, u32[]{:S(2)}, u32[]{:S(2)}) collective-permute-start(bf16[2,16,4096]{2,1,0:T(8,128)(2,1)S(1)} %bitcast_dynamic-update-slice_fusion.4), channel_id=1, source_target_pairs={{0,4},{1,5},{2,6},{3,7},{4,0},{5,1},{6,2},{7,3},{8,12},{9,13},{10,... | collective-permute-start | bytes 786440 | tf_op jit(solution)/shard_map/ppermute | solution.py:48
  31.6 6.4 %collective-permute-start.4 = (bf16[2,16,4096]{2,1,0:T(8,128)(2,1)S(1)}, bf16[2,16,4096]{2,1,0:T(8,128)(2,1)S(1)}, u32[]{:S(2)}, u32[]{:S(2)}) collective-permute-start(bf16[2,16,4096]{2,1,0:T(8,128)(2,1)S(1)} %bitcast_dynamic-update-slice_fusion.6), channel_id=1, source_target_pairs={{0,2},{1,3},{2,0},{3,1},{4,6},{5,7},{6,4},{7,5},{8,10},{9,11},{10,... | collective-permute-start | bytes 786440 | tf_op jit(solution)/shard_map/ppermute | solution.py:48
  32.3 1.2 %collective-permute-start.9 = (f32[8320]{0:T(1024)S(1)}, f32[8320]{0:T(1024)S(1)}, u32[]{:S(2)}, u32[]{:S(2)}) collective-permute-start(f32[8320]{0:T(1024)S(1)} %add.160), channel_id=1, source_target_pairs={{0,1},{1,0},{2,3},{3,2},{4,5},{5,4},{6,7},{7,6},{8,9},{9,8},{10,11... | collective-permute-start | bytes 99848 | tf_op jit(solution)/shard_map/ppermute | solution.py:121
  38.1 4.0 %collective-permute-start.12 = (bf16[64,8192]{1,0:T(8,128)(2,1)S(1)}, bf16[64,8192]{1,0:T(8,128)(2,1)S(1)}, u32[]{:S(2)}, u32[]{:S(2)}) collective-permute-start(bf16[64,8192]{1,0:T(8,128)(2,1)S(1)} %pad_maximum_fusion), channel_id=1, source_target_pairs={{0,1},{1,0},{2,3},{3,2},{4,5},{5,4},{6,7},{7,6},{8,9},{9,8},{10,11... | collective-permute-start | bytes 3145736 | tf_op jit(solution)/shard_map/ppermute | solution.py:108

commit v6 on v5

--- a/solution.py
+++ b/solution.py
@@ -113,7 +113,7 @@
 
 
 def butterfly_sum(values, factors, device_count):
-    for factor in factors:
+    for factor in factors[-1:] + factors[:-1]:
         size, stride = factor
         bit = 1
         while bit < size:

time: 58 us -> 56.8 us (0.979)
  starting transfers between devices: 17.4 us -> 14.7 us
  waiting for transfers between devices: 12.1 us -> 13.6 us
    ppermute x5, waiting for transfers between devices: 8.1 us -> 13.6 us  [butterfly_sum(): values = values + lax.ppermute(values, AXES, pairs)]
    ppermute x7, waiting for transfers between devices: 3.97 us -> 0.02 us  [gather_factor(): received = lax.ppermute(piece, AXES, shifted(factor, shift, device_count))]
    ppermute x5, starting transfers between devices: 5.18 us -> 2.33 us  [butterfly_sum(): values = values + lax.ppermute(values, AXES, pairs)]
  transfers between devices with their start and end apart: 13 -> 13, of which waited for: 7 -> 4; matrix products, arithmetic and copies ran while one was open for 21% -> 21% of each run, Pallas kernels for 0% -> 0%
where the time goes in v6:
time: 56.8 us; the launch traced here: 56.5 us
  starting transfers between devices  14.7 us (26%)
  waiting for transfers between devices  13.6 us (24%)
  blocking collectives  9.83 us (17%)
  matrix products  8.03 us (14%)
  other arithmetic  6.88 us (12%)
  local copies, waits for them, and re-layouts  3 us (5%)
    ppermute x5, waiting for transfers between devices, butterfly_sum(): values = values + lax.ppermute(values, AXES, pairs)  13.6 us
    ppermute x7, starting transfers between devices, gather_factor(): received = lax.ppermute(piece, AXES, shifted(factor, shift, device_count))  12.3 us
    all_to_all x1, blocking collectives, local(): lax.all_to_all(bucket.reshape(blk_count, capacity, query_count), 'blk', s...  9.83 us
    dot_general x4, matrix products, partial_scores(): jnp.einsum('rk,qk->rq', grad_rows[:, start:start + size], prepared, prefe...  7.82 us
    reduce_sum x1, other arithmetic, local(): jnp.sum(row_weights[:, None] * jnp.square(grad_rows.astype(jnp.float32)),...  3.35 us
    ppermute x5, starting transfers between devices, butterfly_sum(): values = values + lax.ppermute(values, AXES, pairs)  2.33 us
    mul x1, other arithmetic, local(): weight_scale = row_weights * inv_root  1.28 us
  transfers between devices with their start and end apart: 13, of which 4 were waited for; matrix products, arithmetic and copies ran while one was open for 21% of the time, Pallas kernels for 0%

profile of v6, /device:TPU:0, one launch (start us, length us, event | category | flops | bytes accessed | tf_op | source)
XLA Modules:
  0.0 56.5 jit_solution(18435350541901508657)
XLA Ops:
  0.0 3.1 %collective-permute-start = (bf16[4,8192]{1,0:T(4,128)(2,1)}, bf16[4,8192]{1,0:T(4,128)(2,1)S(1)}, u32[]{:S(2)}, u32[]{:S(2)}) collective-permute-start(bf16[4,8192]{1,0:T(4,128)(2,1)} %param.10), channel_id=1, source_target_pairs={{0,8},{1,9},{2,10},{3,11},{4,12},{5,13},{6,14},{7,15},{8,16},{9,17... | collective-permute-start | bytes 196616 | tf_op jit(solution)/shard_map/ppermute | solution.py:48
  3.1 2.6 %collective-permute-start.1 = (bf16[4,8192]{1,0:T(4,128)(2,1)}, bf16[4,8192]{1,0:T(4,128)(2,1)S(1)}, u32[]{:S(2)}, u32[]{:S(2)}) collective-permute-start(bf16[4,8192]{1,0:T(4,128)(2,1)} %param.10), channel_id=1, source_target_pairs={{0,16},{1,17},{2,18},{3,19},{4,20},{5,21},{6,22},{7,23},{8,24},{9,... | collective-permute-start | bytes 196616 | tf_op jit(solution)/shard_map/ppermute | solution.py:48
  5.7 1.3 %collective-permute-start.2 = (bf16[4,8192]{1,0:T(4,128)(2,1)}, bf16[4,8192]{1,0:T(4,128)(2,1)S(1)}, u32[]{:S(2)}, u32[]{:S(2)}) collective-permute-start(bf16[4,8192]{1,0:T(4,128)(2,1)} %param.10), channel_id=1, source_target_pairs={{0,24},{1,25},{2,26},{3,27},{4,28},{5,29},{6,30},{7,31},{8,0},{9,1... | collective-permute-start | bytes 196616 | tf_op jit(solution)/shard_map/ppermute | solution.py:48
  7.0 1.3 %broadcast_multiply_fusion = (f32[256]{0:T(256)S(1)}, f32[]{:T(128)}) fusion(f32[256]{0:T(256)} %param.8), kind=kLoop, calls=%fused_computation.63 | loop fusion | flops 511 | bytes 2052 | tf_op jit(solution)/shard_map/mul | solution.py:151
  8.3 3.4 %multiply_reduce_fusion = f32[8192]{0:T(1024)S(1)} fusion(bf16[256,8192]{1,0:T(8,128)(2,1)} %param.7, f32[256]{0:T(256)} %param.8), kind=kLoop, calls=%fused_computation.1 | loop fusion | flops 8380416 | bytes 4228096 | tf_op jit(solution)/shard_map/reduce_sum | solution.py:140
  11.8 0.7 %gather_fusion = s32[256,8]{1,0:T(8,128)S(1)} fusion(s32[8,8]{1,0:T(8,128)S(1)} %bitcast.82, s32[1024]{0:T(1024)S(1)} %pad_clamp_fusion), kind=kCustom, calls=%fused_computation | custom fusion | bytes 17408 | tf_op jit(solution)/shard_map/jit(_take)/gather | solution.py:149
  13.6 0.7 %select_maximum_fusion = f32[8320]{0:T(1024)S(1)} fusion(f32[1]{0:T(128)} %bitcast.8, f32[8192]{0:T(1024)S(1)} %multiply_reduce_fusion), kind=kLoop, calls=%fused_computation.46 | loop fusion | flops 24960 | bytes 66052 | tf_op jit(solution)/shard_map/concatenate | solution.py:141
  14.9 1.6 %collective-permute-start.10 = (bf16[16,4096]{1,0:T(8,128)(2,1)S(1)}, bf16[16,4096]{1,0:T(8,128)(2,1)S(1)}, u32[]{:S(2)}, u32[]{:S(2)}) collective-permute-start(bf16[16,4096]{1,0:T(8,128)(2,1)S(1)} %get-tuple-element.24), channel_id=1, source_target_pairs={{0,2},{1,3},{2,0},{3,1},{4,6},{5,7},{6,4},{7,5},{8,10},{9,11},{10,... | collective-permute-start | bytes 393224 | tf_op jit(solution)/shard_map/ppermute | solution.py:48
  16.4 1.5 %collective-permute-start.3 = (bf16[16,4096]{1,0:T(8,128)(2,1)S(1)}, bf16[16,4096]{1,0:T(8,128)(2,1)S(1)}, u32[]{:S(2)}, u32[]{:S(2)}) collective-permute-start(bf16[16,4096]{1,0:T(8,128)(2,1)S(1)} %get-tuple-element.23), channel_id=1, source_target_pairs={{0,4},{1,5},{2,6},{3,7},{4,0},{5,1},{6,2},{7,3},{8,12},{9,13},{10,... | collective-permute-start | bytes 393224 | tf_op jit(solution)/shard_map/ppermute | solution.py:48
  17.9 0.7 %collective-permute-start.6 = (f32[8320]{0:T(1024)S(1)}, f32[8320]{0:T(1024)S(1)}, u32[]{:S(2)}, u32[]{:S(2)}) collective-permute-start(f32[8320]{0:T(1024)S(1)} %add.157), channel_id=1, source_target_pairs={{0,8},{1,9},{2,10},{3,11},{4,12},{5,13},{6,14},{7,15},{8,0},{9,1},... | collective-permute-start | bytes 99848 | tf_op jit(solution)/shard_map/ppermute | solution.py:121
  18.7 3.2 %collective-permute-done.6 = f32[8320]{0:T(1024)S(1)} collective-permute-done((f32[8320]{0:T(1024)S(1)}, f32[8320]{0:T(1024)S(1)}, u32[]{:S(2)}, u32[]{:S(2)}) %collective-permute-start.6) | collective-permute-done | bytes 33312 | tf_op jit(solution)/shard_map/ppermute | solution.py:121
  22.4 4.9 %collective-permute-done.7 = f32[8320]{0:T(1024)S(1)} collective-permute-done((f32[8320]{0:T(1024)S(1)}, f32[8320]{0:T(1024)S(1)}, u32[]{:S(2)}, u32[]{:S(2)}) %collective-permute-start.7) | collective-permute-done | bytes 33312 | tf_op jit(solution)/shard_map/ppermute | solution.py:121
  27.8 1.6 %collective-permute-start.11 = (bf16[2,16,4096]{2,1,0:T(8,128)(2,1)S(1)}, bf16[2,16,4096]{2,1,0:T(8,128)(2,1)S(1)}, u32[]{:S(2)}, u32[]{:S(2)}) collective-permute-start(bf16[2,16,4096]{2,1,0:T(8,128)(2,1)S(1)} %bitcast_dynamic-update-slice_fusion.4), channel_id=1, source_target_pairs={{0,4},{1,5},{2,6},{3,7},{4,0},{5,1},{6,2},{7,3},{8,12},{9,13},{10,... | collective-permute-start | bytes 786440 | tf_op jit(solution)/shard_map/ppermute | solution.py:48
  29.5 0.6 %collective-permute-start.4 = (bf16[2,16,4096]{2,1,0:T(8,128)(2,1)S(1)}, bf16[2,16,4096]{2,1,0:T(8,128)(2,1)S(1)}, u32[]{:S(2)}, u32[]{:S(2)}) collective-permute-start(bf16[2,16,4096]{2,1,0:T(8,128)(2,1)S(1)} %bitcast_dynamic-update-slice_fusion.6), channel_id=1, source_target_pairs={{0,2},{1,3},{2,0},{3,1},{4,6},{5,7},{6,4},{7,5},{8,10},{9,11},{10,... | collective-permute-start | bytes 786440 | tf_op jit(solution)/shard_map/ppermute | solution.py:48
  30.1 1.3 %collective-permute-done.8 = f32[8320]{0:T(1024)S(1)} collective-permute-done((f32[8320]{0:T(1024)S(1)}, f32[8320]{0:T(1024)S(1)}, u32[]{:S(2)}, u32[]{:S(2)}) %collective-permute-start.8) | collective-permute-done | bytes 33312 | tf_op jit(solution)/shard_map/ppermute | solution.py:121
  31.4 0.7 %collective-permute-start.9 = (f32[8320]{0:T(1024)S(1)}, f32[8320]{0:T(1024)S(1)}, u32[]{:S(2)}, u32[]{:S(2)}) collective-permute-start(f32[8320]{0:T(1024)S(1)} %add.160), channel_id=1, source_target_pairs={{0,2},{1,3},{2,0},{3,1},{4,6},{5,7},{6,4},{7,5},{8,10},{9,11},{10,... | collective-permute-start | bytes 99848 | tf_op jit(solution)/shard_map/ppermute | solution.py:121
  32.1 4.2 %collective-permute-done.9 = f32[8320]{0:T(1024)S(1)} collective-permute-done((f32[8320]{0:T(1024)S(1)}, f32[8320]{0:T(1024)S(1)}, u32[]{:S(2)}, u32[]{:S(2)}) %collective-permute-start.9) | collective-permute-done | bytes 33312 | tf_op jit(solution)/shard_map/ppermute | solution.py:121
  37.0 0.7 %fusion.29 = f32[8192]{0:T(1024)S(1)} fusion(f32[8320]{0:T(1024)S(1)} %add.161, f32[]{:T(128)} %bitcast.14), kind=kLoop, calls=%fused_computation.50 | loop fusion | flops 16384 | bytes 65540 | tf_op jit(solution)/shard_map/rsqrt | solution.py:146
  37.7 0.8 %fusion.14 = f32[256,64]{0,1:T(8,128)S(1)} fusion(bf16[256,8192]{1,0:T(8,128)(2,1)S(1)} %copy-done, bf16[64,4096]{1,0:T(8,128)(2,1)S(1)} %bitcast.86, f32[4096]{0:T(1024)S(1)} %get-tuple-element.26), kind=kOutput, calls=%fused_computation.13 | convolution fusion | flops 135004160 | bytes 2703360 | tf_op jit(solution)/shard_map/rk,qk->rq/dot_general | solution.py:91
  38.5 2.4 %fusion.8 = f32[256,64]{0,1:T(8,128)S(1)} fusion(bf16[256,8192]{1,0:T(8,128)(2,1)} %param.7, bf16[64,4096]{1,0:T(8,128)(2,1)S(1)} %bitcast.84, f32[4096]{0:T(1024)S(1)} %get-tuple-element.25), kind=kOutput, calls=%fused_computation.11 | convolution fusion | flops 135004160 | bytes 2703360 | tf_op jit(solution)/shard_map/rk,qk->rq/dot_general | solution.py:91
  41.0 2.4 %fusion.17 = f32[256,64]{0,1:T(8,128)S(1)} fusion(bf16[256,8192]{1,0:T(8,128)(2,1)} %param.7, bf16[64,8192]{1,0:T(8,128)(2,1)S(1)} %collective-permute-done.12, f32[4096]{0:T(1024)S(1)} %get-tuple-element.26), kind=kOutput, calls=%fused_computation.14 | convolution fusion | flops 135004160 | bytes 2703360 | tf_op jit(solution)/shard_map/rk,qk->rq/dot_general | solution.py:91
  43.4 2.4 %fusion.11 = f32[256,64]{0,1:T(8,128)S(1)} fusion(bf16[256,8192]{1,0:T(8,128)(2,1)} %param.7, bf16[64,8192]{1,0:T(8,128)(2,1)S(1)} %collective-permute-done.12, f32[4096]{0:T(1024)S(1)} %get-tuple-element.25), kind=kOutput, calls=%fused_computation.12 | convolution fusion | flops 135004160 | bytes 2703360 | tf_op jit(solution)/shard_map/rk,qk->rq/dot_general | solution.py:91
  46.1 9.8 %all_to_all.5 = bf16[8,48,128]{2,1,0:T(8,128)(2,1)S(1)} all-to-all(bf16[8,48,128]{2,1,0:T(8,128)(2,1)S(1)} %bitcast.89), channel_id=1, replica_groups=mesh['blk'=8,'harvest'=4] {'blk'}, dimensions={0} | all-to-all | bytes 196608 | tf_op jit(solution)/shard_map/all_to_all | solution.py:161
  55.9 0.6 %copy.40 = bf16[384,128]{1,0:T(8,128)(2,1)} copy(bf16[384,128]{1,0:T(8,128)(2,1)S(1)} %bitcast.88) | data formatting | bytes 196608
  (70 shorter events, 3.8 us)
Async XLA Ops:
  0.0 13.5 %copy-start.1 = (bf16[4,8192]{1,0:T(4,128)(2,1)S(1)}, bf16[4,8192]{1,0:T(4,128)(2,1)}, u32[]{:S(2)}) copy-start(bf16[4,8192]{1,0:T(4,128)(2,1)} %param.10) | copy-start | bytes 196612
  0.0 11.7 %copy-start.3 = (s32[8,8]{1,0:T(8,128)S(1)}, s32[8,8]{1,0:T(8,128)}, u32[]{:S(2)}) copy-start(s32[8,8]{1,0:T(8,128)} %param.11) | copy-start | bytes 772
  0.0 11.7 %copy-start.2 = (s32[256,1]{0,1:T(1,128)S(1)}, s32[256,1]{0,1:T(1,128)}, u32[]{:S(2)}) copy-start(s32[256,1]{0,1:T(1,128)} %param.9) | copy-start | bytes 3076
  0.0 14.5 %collective-permute-start = (bf16[4,8192]{1,0:T(4,128)(2,1)}, bf16[4,8192]{1,0:T(4,128)(2,1)S(1)}, u32[]{:S(2)}, u32[]{:S(2)}) collective-permute-start(bf16[4,8192]{1,0:T(4,128)(2,1)} %param.10), channel_id=1, source_target_pairs={{0,8},{1,9},{2,10},{3,11},{4,12},{5,13},{6,14},{7,15},{8,16},{9,17... | collective-permute-start | bytes 196616 | tf_op jit(solution)/shard_map/ppermute | solution.py:48
  3.1 11.5 %collective-permute-start.1 = (bf16[4,8192]{1,0:T(4,128)(2,1)}, bf16[4,8192]{1,0:T(4,128)(2,1)S(1)}, u32[]{:S(2)}, u32[]{:S(2)}) collective-permute-start(bf16[4,8192]{1,0:T(4,128)(2,1)} %param.10), channel_id=1, source_target_pairs={{0,16},{1,17},{2,18},{3,19},{4,20},{5,21},{6,22},{7,23},{8,24},{9,... | collective-permute-start | bytes 196616 | tf_op jit(solution)/shard_map/ppermute | solution.py:48
  5.7 8.9 %collective-permute-start.2 = (bf16[4,8192]{1,0:T(4,128)(2,1)}, bf16[4,8192]{1,0:T(4,128)(2,1)S(1)}, u32[]{:S(2)}, u32[]{:S(2)}) collective-permute-start(bf16[4,8192]{1,0:T(4,128)(2,1)} %param.10), channel_id=1, source_target_pairs={{0,24},{1,25},{2,26},{3,27},{4,28},{5,29},{6,30},{7,31},{8,0},{9,1... | collective-permute-start | bytes 196616 | tf_op jit(solution)/shard_map/ppermute | solution.py:48
  14.7 23.0 %copy-start = (bf16[256,8192]{1,0:T(8,128)(2,1)S(1)}, bf16[256,8192]{1,0:T(8,128)(2,1)}, u32[]{:S(2)}) copy-start(bf16[256,8192]{1,0:T(8,128)(2,1)} %param.7) | copy-start | bytes 12582916
  14.8 3.2 %collective-permute-start.5 = (f32[8320]{0:T(1024)S(1)}, f32[8320]{0:T(1024)S(1)}, u32[]{:S(2)}, u32[]{:S(2)}) collective-permute-start(f32[8320]{0:T(1024)S(1)} %select_maximum_fusion), channel_id=1, source_target_pairs={{0,1},{1,0},{2,3},{3,2},{4,5},{5,4},{6,7},{7,6},{8,9},{9,8},{10,11... | collective-permute-start | bytes 99848 | tf_op jit(solution)/shard_map/ppermute | solution.py:121
  14.9 12.9 %collective-permute-start.10 = (bf16[16,4096]{1,0:T(8,128)(2,1)S(1)}, bf16[16,4096]{1,0:T(8,128)(2,1)S(1)}, u32[]{:S(2)}, u32[]{:S(2)}) collective-permute-start(bf16[16,4096]{1,0:T(8,128)(2,1)S(1)} %get-tuple-element.24), channel_id=1, source_target_pairs={{0,2},{1,3},{2,0},{3,1},{4,6},{5,7},{6,4},{7,5},{8,10},{9,11},{10,... | collective-permute-start | bytes 393224 | tf_op jit(solution)/shard_map/ppermute | solution.py:48
  16.4 13.0 %collective-permute-start.3 = (bf16[16,4096]{1,0:T(8,128)(2,1)S(1)}, bf16[16,4096]{1,0:T(8,128)(2,1)S(1)}, u32[]{:S(2)}, u32[]{:S(2)}) collective-permute-start(bf16[16,4096]{1,0:T(8,128)(2,1)S(1)} %get-tuple-element.23), channel_id=1, source_target_pairs={{0,4},{1,5},{2,6},{3,7},{4,0},{5,1},{6,2},{7,3},{8,12},{9,13},{10,... | collective-permute-start | bytes 393224 | tf_op jit(solution)/shard_map/ppermute | solution.py:48
  17.9 4.0 %collective-permute-start.6 = (f32[8320]{0:T(1024)S(1)}, f32[8320]{0:T(1024)S(1)}, u32[]{:S(2)}, u32[]{:S(2)}) collective-permute-start(f32[8320]{0:T(1024)S(1)} %add.157), channel_id=1, source_target_pairs={{0,8},{1,9},{2,10},{3,11},{4,12},{5,13},{6,14},{7,15},{8,0},{9,1},... | collective-permute-start | bytes 99848 | tf_op jit(solution)/shard_map/ppermute | solution.py:121
  22.0 5.3 %collective-permute-start.7 = (f32[8320]{0:T(1024)S(1)}, f32[8320]{0:T(1024)S(1)}, u32[]{:S(2)}, u32[]{:S(2)}) collective-permute-start(f32[8320]{0:T(1024)S(1)} %add.158), channel_id=1, source_target_pairs={{0,16},{1,17},{2,18},{3,19},{4,20},{5,21},{6,22},{7,23},{8,24},{9,... | collective-permute-start | bytes 99848 | tf_op jit(solution)/shard_map/ppermute | solution.py:121
  27.2 4.1 %collective-permute-start.8 = (f32[8320]{0:T(1024)S(1)}, f32[8320]{0:T(1024)S(1)}, u32[]{:S(2)}, u32[]{:S(2)}) collective-permute-start(f32[8320]{0:T(1024)S(1)} %add.159), channel_id=1, source_target_pairs={{0,4},{1,5},{2,6},{3,7},{4,0},{5,1},{6,2},{7,3},{8,12},{9,13},{10,... | collective-permute-start | bytes 99848 | tf_op jit(solution)/shard_map/ppermute | solution.py:121
  27.8 9.0 %collective-permute-start.11 = (bf16[2,16,4096]{2,1,0:T(8,128)(2,1)S(1)}, bf16[2,16,4096]{2,1,0:T(8,128)(2,1)S(1)}, u32[]{:S(2)}, u32[]{:S(2)}) collective-permute-start(bf16[2,16,4096]{2,1,0:T(8,128)(2,1)S(1)} %bitcast_dynamic-update-slice_fusion.4), channel_id=1, source_target_pairs={{0,4},{1,5},{2,6},{3,7},{4,0},{5,1},{6,2},{7,3},{8,12},{9,13},{10,... | collective-permute-start | bytes 786440 | tf_op jit(solution)/shard_map/ppermute | solution.py:48
  29.5 7.4 %collective-permute-start.4 = (bf16[2,16,4096]{2,1,0:T(8,128)(2,1)S(1)}, bf16[2,16,4096]{2,1,0:T(8,128)(2,1)S(1)}, u32[]{:S(2)}, u32[]{:S(2)}) collective-permute-start(bf16[2,16,4096]{2,1,0:T(8,128)(2,1)S(1)} %bitcast_dynamic-update-slice_fusion.6), channel_id=1, source_target_pairs={{0,2},{1,3},{2,0},{3,1},{4,6},{5,7},{6,4},{7,5},{8,10},{9,11},{10,... | collective-permute-start | bytes 786440 | tf_op jit(solution)/shard_map/ppermute | solution.py:48
  31.4 4.9 %collective-permute-start.9 = (f32[8320]{0:T(1024)S(1)}, f32[8320]{0:T(1024)S(1)}, u32[]{:S(2)}, u32[]{:S(2)}) collective-permute-start(f32[8320]{0:T(1024)S(1)} %add.160), channel_id=1, source_target_pairs={{0,2},{1,3},{2,0},{3,1},{4,6},{5,7},{6,4},{7,5},{8,10},{9,11},{10,... | collective-permute-start | bytes 99848 | tf_op jit(solution)/shard_map/ppermute | solution.py:121
  37.0 4.0 %collective-permute-start.12 = (bf16[64,8192]{1,0:T(8,128)(2,1)S(1)}, bf16[64,8192]{1,0:T(8,128)(2,1)S(1)}, u32[]{:S(2)}, u32[]{:S(2)}) collective-permute-start(bf16[64,8192]{1,0:T(8,128)(2,1)S(1)} %pad_maximum_fusion), channel_id=1, source_target_pairs={{0,1},{1,0},{2,3},{3,2},{4,5},{5,4},{6,7},{7,6},{8,9},{9,8},{10,11... | collective-permute-start | bytes 3145736 | tf_op jit(solution)/shard_map/ppermute | solution.py:108

commit v7 on v3

--- a/solution.py
+++ b/solution.py
@@ -62,32 +62,51 @@
     return list(zip(starts, sizes))
 
 
-def streamed_scores(grad_rows, queries, scaling, factors, device_count):
+def gather_streams(first, factors, device_count):
     rank = len(factors)
-    rows = queries.shape[0]
-    first = gather_rows(queries, factors[0], device_count)
-    rest = list(range(1, rank))
-    streams = max(len(rest), 1)
-    raw = None
-    for j, (start, size) in enumerate(column_splits(queries.shape[1], streams)):
-        order = rest[j:] + rest[:j]
+    middle = list(range(1, rank - 1))
+    splits = column_splits(first.shape[1], max(len(middle), 1))
+    parts, orders = [], []
+    for j, (start, size) in enumerate(splits):
+        order = middle[j:] + middle[:j]
         part = first[:, start:start + size]
         for position in order:
             part = gather_factor(part, factors[position], device_count)
-        held = list(reversed(order))
-        stacked_rows = part.reshape(-1, size)
-        prepared = (stacked_rows.astype(jnp.float32) * scaling[start:start + size]).astype(jnp.bfloat16)
+        parts.append(part.reshape(-1, size))
+        orders.append(order)
+    joined = jnp.concatenate(parts, axis=1) if len(parts) > 1 else parts[0]
+    return joined, splits, orders
+
+
+def exchange_and_score(grad_rows, joined, scaling, splits, orders, factors, rows, device_count):
+    rank = len(factors)
+    middle = list(range(1, rank - 1))
+    last = rank - 1
+    row_count = grad_rows.shape[0]
+    size_last = factors[last][0]
+    own = coordinate(lax.axis_index(AXES), factors[last])
+    blocks = [joined] + [
+        lax.ppermute(joined, AXES, shifted(factors[last], shift, device_count)) for shift in range(1, size_last)
+    ]
+    full = jnp.concatenate(blocks, axis=0) if size_last > 1 else joined
+    total = None
+    for (start, size), order in zip(splits, orders):
+        prepared = (full[:, start:start + size].astype(jnp.float32) * scaling[start:start + size]).astype(jnp.bfloat16)
         partial = jnp.einsum(
             "rk,qk->rq", grad_rows[:, start:start + size], prepared, preferred_element_type=jnp.float32
         )
-        shape = [factors[p][0] for p in held] + [factors[0][0], rows]
-        partial = partial.reshape((grad_rows.shape[0],) + tuple(shape))
-        canonical = [held.index(p) + 1 for p in rest]
-        lead = len(held) + 1
-        partial = jnp.transpose(partial, [0, lead] + canonical + [lead + 1])
-        partial = partial.reshape(grad_rows.shape[0], -1)
-        raw = partial if raw is None else raw + partial
-    return raw
+        held = list(reversed(order))
+        shape = [size_last] + [factors[p][0] for p in held] + [factors[0][0], rows]
+        partial = partial.reshape((row_count,) + tuple(shape))
+        axes = [0, 1, len(held) + 2] + [held.index(p) + 2 for p in middle] + [len(held) + 3]
+        partial = jnp.transpose(partial, axes)
+        total = partial if total is None else total + partial
+    reverse = jnp.flip(total, axis=1)
+    doubled = jnp.concatenate([reverse, reverse], axis=1)
+    ordered = lax.dynamic_slice_in_dim(doubled, size_last - 1 - own, size_last, axis=1)
+    dims = ordered.ndim
+    ordered = jnp.transpose(ordered, [0] + list(range(2, dims - 1)) + [1, dims - 1])
+    return ordered.reshape(row_count, -1)
 
 
 def butterfly_sum(values, factors, device_count):
@@ -117,10 +136,16 @@
 
     squares = jnp.sum(row_weights[:, None] * jnp.square(grad_rows.astype(jnp.float32)), axis=0)
     packed = jnp.concatenate([squares, jnp.zeros((128,), jnp.float32).at[0].set(jnp.sum(row_weights))])
-    packed = butterfly_sum(packed, factors, device_count)
+    first = gather_rows(queries, factors[0], device_count)
+    first, packed = lax.optimization_barrier((first, packed))
+    levels = factors[-1:] + factors[:-1]
+    packed = butterfly_sum(packed, levels[:-1], device_count)
+    joined, splits, orders = gather_streams(first, factors, device_count)
+    joined, packed = lax.optimization_barrier((joined, packed))
+    packed = butterfly_sum(packed, levels[-1:], device_count)
     total_sq, total_weight = packed[:width], packed[width]
     scaling = lax.rsqrt(total_sq / total_weight + 1e-06)
-    raw = streamed_scores(grad_rows, queries, scaling, factors, device_count)
+    raw = exchange_and_score(grad_rows, joined, scaling, splits, orders, factors, queries.shape[0], device_count)
     owner_ids = destinations[:, 0]
     pattern_rows = jnp.take(tile_pattern.T, owner_ids, axis=0).astype(jnp.float32)
     full_mask = jnp.repeat(pattern_rows, block_size, axis=1)

time: 65.4 us -> 54.7 us (0.84)
  starting transfers between devices: 20.9 us -> 15.4 us
  matrix products: 6.03 us -> 3.5 us
  waiting for transfers between devices: 16.9 us -> 15.3 us
    ppermute x12 -> x7, waiting for transfers between devices: 9.49 us -> 3.26 us  [gather_factor(): received = lax.ppermute(piece, AXES, shifted(factor, shift, device_count))]
    ppermute x12 -> x7, starting transfers between devices: 16.9 us -> 12.2 us  [gather_factor(): received = lax.ppermute(piece, AXES, shifted(factor, shift, device_count))]
    ppermute x5, waiting for transfers between devices: 7.4 us -> 12 us  [butterfly_sum(): values = values + lax.ppermute(values, AXES, pairs)]
    dot_general x3 -> x2, matrix products: 5.82 us -> 3.28 us  [exchange_and_score(): jnp.einsum('rk,qk->rq', grad_rows[:, start:start + size], prepared, prefe...]
    ppermute x5, starting transfers between devices: 3.94 us -> 3.19 us  [butterfly_sum(): values = values + lax.ppermute(values, AXES, pairs)]
  transfers between devices with their start and end apart: 17 -> 13, of which waited for: 7 -> 6; matrix products, arithmetic and copies ran while one was open for 21% -> 16% of each run, Pallas kernels for 0% -> 0%
where the time goes in v7:
time: 54.7 us; the launch traced here: 54.5 us
  starting transfers between devices  15.4 us (28%)
  waiting for transfers between devices  15.3 us (28%)
  blocking collectives  9.69 us (18%)
  other arithmetic  6.95 us (13%)
  matrix products  3.5 us (6%)
  local copies, waits for them, and re-layouts  3.11 us (6%)
    ppermute x7, starting transfers between devices, gather_factor(): received = lax.ppermute(piece, AXES, shifted(factor, shift, device_count))  12.2 us
    ppermute x5, waiting for transfers between devices, butterfly_sum(): values = values + lax.ppermute(values, AXES, pairs)  12 us
    all_to_all x1, blocking collectives, local(): lax.all_to_all(bucket.reshape(blk_count, capacity, query_count), 'blk', s...  9.69 us
    reduce_sum x1, other arithmetic, local(): jnp.sum(row_weights[:, None] * jnp.square(grad_rows.astype(jnp.float32)),...  3.39 us
    dot_general x2, matrix products, exchange_and_score(): jnp.einsum('rk,qk->rq', grad_rows[:, start:start + size], prepared, prefe...  3.28 us
    ppermute x7, waiting for transfers between devices, gather_factor(): received = lax.ppermute(piece, AXES, shifted(factor, shift, device_count))  3.26 us
    ppermute x5, starting transfers between devices, butterfly_sum(): values = values + lax.ppermute(values, AXES, pairs)  3.19 us
    mul x1, other arithmetic, local(): weight_scale = row_weights * inv_root  1.28 us
  transfers between devices with their start and end apart: 13, of which 6 were waited for; matrix products, arithmetic and copies ran while one was open for 16% of the time, Pallas kernels for 0%

profile of v7, /device:TPU:0, one launch (start us, length us, event | category | flops | bytes accessed | tf_op | source)
XLA Modules:
  0.0 54.5 jit_solution(15976685831924922883)
XLA Ops:
  0.0 3.0 %collective-permute-start = (bf16[4,8192]{1,0:T(4,128)(2,1)}, bf16[4,8192]{1,0:T(4,128)(2,1)S(1)}, u32[]{:S(2)}, u32[]{:S(2)}) collective-permute-start(bf16[4,8192]{1,0:T(4,128)(2,1)} %param.10), channel_id=1, source_target_pairs={{0,8},{1,9},{2,10},{3,11},{4,12},{5,13},{6,14},{7,15},{8,16},{9,17... | collective-permute-start | bytes 196616 | tf_op jit(solution)/shard_map/ppermute | solution.py:48
  3.0 2.6 %collective-permute-start.1 = (bf16[4,8192]{1,0:T(4,128)(2,1)}, bf16[4,8192]{1,0:T(4,128)(2,1)S(1)}, u32[]{:S(2)}, u32[]{:S(2)}) collective-permute-start(bf16[4,8192]{1,0:T(4,128)(2,1)} %param.10), channel_id=1, source_target_pairs={{0,16},{1,17},{2,18},{3,19},{4,20},{5,21},{6,22},{7,23},{8,24},{9,... | collective-permute-start | bytes 196616 | tf_op jit(solution)/shard_map/ppermute | solution.py:48
  5.6 1.3 %collective-permute-start.2 = (bf16[4,8192]{1,0:T(4,128)(2,1)}, bf16[4,8192]{1,0:T(4,128)(2,1)S(1)}, u32[]{:S(2)}, u32[]{:S(2)}) collective-permute-start(bf16[4,8192]{1,0:T(4,128)(2,1)} %param.10), channel_id=1, source_target_pairs={{0,24},{1,25},{2,26},{3,27},{4,28},{5,29},{6,30},{7,31},{8,0},{9,1... | collective-permute-start | bytes 196616 | tf_op jit(solution)/shard_map/ppermute | solution.py:48
  7.0 1.3 %broadcast_multiply_fusion = (f32[256]{0:T(256)S(1)}, f32[]{:T(128)}) fusion(f32[256]{0:T(256)} %param.8), kind=kLoop, calls=%fused_computation.56 | loop fusion | flops 511 | bytes 2052 | tf_op jit(solution)/shard_map/mul | solution.py:152
  8.3 3.4 %multiply_reduce_fusion = f32[8192]{0:T(1024)S(1)} fusion(bf16[256,8192]{1,0:T(8,128)(2,1)} %param.7, f32[256]{0:T(256)} %param.8), kind=kLoop, calls=%fused_computation.1 | loop fusion | flops 8380416 | bytes 4228096 | tf_op jit(solution)/shard_map/reduce_sum | solution.py:137
  11.8 0.7 %gather_fusion = s32[256,8]{1,0:T(8,128)S(1)} fusion(s32[8,8]{1,0:T(8,128)S(1)} %bitcast.63, s32[1024]{0:T(1024)S(1)} %pad_clamp_fusion), kind=kCustom, calls=%fused_computation | custom fusion | bytes 17408 | tf_op jit(solution)/shard_map/jit(_take)/gather | solution.py:150
  13.5 0.7 %select_maximum_fusion = f32[8320]{0:T(1024)S(1)} fusion(f32[1]{0:T(128)} %bitcast.8, f32[8192]{0:T(1024)S(1)} %multiply_reduce_fusion), kind=kLoop, calls=%fused_computation.37 | loop fusion | flops 24960 | bytes 66052 | tf_op jit(solution)/shard_map/concatenate | solution.py:138
  14.8 1.6 %collective-permute-start.3 = (bf16[16,4096]{1,0:T(8,128)(2,1)S(1)}, bf16[16,4096]{1,0:T(8,128)(2,1)S(1)}, u32[]{:S(2)}, u32[]{:S(2)}) collective-permute-start(bf16[16,4096]{1,0:T(8,128)(2,1)S(1)} %get-tuple-element.27), channel_id=1, source_target_pairs={{0,4},{1,5},{2,6},{3,7},{4,0},{5,1},{6,2},{7,3},{8,12},{9,13},{10,... | collective-permute-start | bytes 393224 | tf_op jit(solution)/shard_map/ppermute | solution.py:48
  16.4 1.5 %collective-permute-start.5 = (bf16[16,4096]{1,0:T(8,128)(2,1)S(1)}, bf16[16,4096]{1,0:T(8,128)(2,1)S(1)}, u32[]{:S(2)}, u32[]{:S(2)}) collective-permute-start(bf16[16,4096]{1,0:T(8,128)(2,1)S(1)} %get-tuple-element.28), channel_id=1, source_target_pairs={{0,2},{1,3},{2,0},{3,1},{4,6},{5,7},{6,4},{7,5},{8,10},{9,11},{10,... | collective-permute-start | bytes 393224 | tf_op jit(solution)/shard_map/ppermute | solution.py:48
  17.9 0.7 %collective-permute-start.8 = (f32[8320]{0:T(1024)S(1)}, f32[8320]{0:T(1024)S(1)}, u32[]{:S(2)}, u32[]{:S(2)}) collective-permute-start(f32[8320]{0:T(1024)S(1)} %add.147), channel_id=1, source_target_pairs={{0,8},{1,9},{2,10},{3,11},{4,12},{5,13},{6,14},{7,15},{8,0},{9,1},... | collective-permute-start | bytes 99848 | tf_op jit(solution)/shard_map/ppermute | solution.py:118
  18.7 3.2 %collective-permute-done.8 = f32[8320]{0:T(1024)S(1)} collective-permute-done((f32[8320]{0:T(1024)S(1)}, f32[8320]{0:T(1024)S(1)}, u32[]{:S(2)}, u32[]{:S(2)}) %collective-permute-start.8) | collective-permute-done | bytes 33312 | tf_op jit(solution)/shard_map/ppermute | solution.py:118
  22.3 4.9 %collective-permute-done.9 = f32[8320]{0:T(1024)S(1)} collective-permute-done((f32[8320]{0:T(1024)S(1)}, f32[8320]{0:T(1024)S(1)}, u32[]{:S(2)}, u32[]{:S(2)}) %collective-permute-start.9) | collective-permute-done | bytes 33312 | tf_op jit(solution)/shard_map/ppermute | solution.py:118
  27.7 0.6 %collective-permute-start.4 = (bf16[2,16,4096]{2,1,0:T(8,128)(2,1)S(1)}, bf16[2,16,4096]{2,1,0:T(8,128)(2,1)S(1)}, u32[]{:S(2)}, u32[]{:S(2)}) collective-permute-start(bf16[2,16,4096]{2,1,0:T(8,128)(2,1)S(1)} %bitcast_dynamic-update-slice_fusion.6), channel_id=1, source_target_pairs={{0,2},{1,3},{2,0},{3,1},{4,6},{5,7},{6,4},{7,5},{8,10},{9,11},{10,... | collective-permute-start | bytes 786440 | tf_op jit(solution)/shard_map/ppermute | solution.py:48
  28.5 1.6 %collective-permute-start.6 = (bf16[2,16,4096]{2,1,0:T(8,128)(2,1)S(1)}, bf16[2,16,4096]{2,1,0:T(8,128)(2,1)S(1)}, u32[]{:S(2)}, u32[]{:S(2)}) collective-permute-start(bf16[2,16,4096]{2,1,0:T(8,128)(2,1)S(1)} %bitcast_dynamic-update-slice_fusion.4), channel_id=1, source_target_pairs={{0,4},{1,5},{2,6},{3,7},{4,0},{5,1},{6,2},{7,3},{8,12},{9,13},{10,... | collective-permute-start | bytes 786440 | tf_op jit(solution)/shard_map/ppermute | solution.py:48
  30.1 1.5 %collective-permute-done.10 = f32[8320]{0:T(1024)S(1)} collective-permute-done((f32[8320]{0:T(1024)S(1)}, f32[8320]{0:T(1024)S(1)}, u32[]{:S(2)}, u32[]{:S(2)}) %collective-permute-start.10) | collective-permute-done | bytes 33312 | tf_op jit(solution)/shard_map/ppermute | solution.py:118
  31.6 2.5 %collective-permute-done.4 = bf16[2,16,4096]{2,1,0:T(8,128)(2,1)S(1)} collective-permute-done((bf16[2,16,4096]{2,1,0:T(8,128)(2,1)S(1)}, bf16[2,16,4096]{2,1,0:T(8,128)(2,1)S(1)}, u32[]{:S(2)}, u32[]{:S(2)}) %collective-permute-start.4) | collective-permute-done | bytes 262176 | tf_op jit(solution)/shard_map/ppermute | solution.py:48
  34.2 0.7 %collective-permute-done.6 = bf16[2,16,4096]{2,1,0:T(8,128)(2,1)S(1)} collective-permute-done((bf16[2,16,4096]{2,1,0:T(8,128)(2,1)S(1)}, bf16[2,16,4096]{2,1,0:T(8,128)(2,1)S(1)}, u32[]{:S(2)}, u32[]{:S(2)}) %collective-permute-start.6) | collective-permute-done | bytes 262176 | tf_op jit(solution)/shard_map/ppermute | solution.py:48
  35.0 1.5 %collective-permute-start.12 = (f32[8320]{0:T(1024)S(1)}, f32[8320]{0:T(1024)S(1)}, u32[]{:S(2)}, u32[]{:S(2)}) collective-permute-start(f32[8320]{0:T(1024)S(1)} %add.150), channel_id=1, source_target_pairs={{0,2},{1,3},{2,0},{3,1},{4,6},{5,7},{6,4},{7,5},{8,10},{9,11},{10,... | collective-permute-start | bytes 99848 | tf_op jit(solution)/shard_map/ppermute | solution.py:118
  36.6 2.4 %collective-permute-done.12 = f32[8320]{0:T(1024)S(1)} collective-permute-done((f32[8320]{0:T(1024)S(1)}, f32[8320]{0:T(1024)S(1)}, u32[]{:S(2)}, u32[]{:S(2)}) %collective-permute-start.12) | collective-permute-done | bytes 33312 | tf_op jit(solution)/shard_map/ppermute | solution.py:118
  39.6 0.7 %fusion.19 = f32[8192]{0:T(1024)S(1)} fusion(f32[8320]{0:T(1024)S(1)} %add.151, f32[]{:T(128)} %bitcast.19), kind=kLoop, calls=%fused_computation.41 | loop fusion | flops 16384 | bytes 65540 | tf_op jit(solution)/shard_map/rsqrt | solution.py:147
  40.3 0.9 %fusion.4 = f32[256,128]{0,1:T(8,128)S(1)} fusion(bf16[256,8192]{1,0:T(8,128)(2,1)S(1)} %copy-done, bf16[128,8192]{1,0:T(8,128)(2,1)S(1)} %constant_dynamic-update-slice_fusion, f32[4096]{0:T(1024)S(1)} %get-tuple-element.29), kind=kOutput, calls=%fused_computation.9 | convolution fusion | flops 270008320 | bytes 3293184 | tf_op jit(solution)/shard_map/rk,qk->rq/dot_general | solution.py:95
  41.2 2.4 %fusion.7 = f32[256,128]{0,1:T(8,128)S(1)} fusion(bf16[256,8192]{1,0:T(8,128)(2,1)} %param.7, bf16[128,8192]{1,0:T(8,128)(2,1)S(1)} %constant_dynamic-update-slice_fusion, f32[4096]{0:T(1024)S(1)} %get-tuple-element.30), kind=kOutput, calls=%fused_computation.10 | convolution fusion | flops 270008320 | bytes 3293184 | tf_op jit(solution)/shard_map/rk,qk->rq/dot_general | solution.py:95
  44.2 9.7 %all_to_all.5 = bf16[8,48,128]{2,1,0:T(8,128)(2,1)S(1)} all-to-all(bf16[8,48,128]{2,1,0:T(8,128)(2,1)S(1)} %bitcast.67), channel_id=1, replica_groups=mesh['blk'=8,'harvest'=4] {'blk'}, dimensions={0} | all-to-all | bytes 196608 | tf_op jit(solution)/shard_map/all_to_all | solution.py:162
  53.9 0.6 %copy.32 = bf16[384,128]{1,0:T(8,128)(2,1)} copy(bf16[384,128]{1,0:T(8,128)(2,1)S(1)} %bitcast.66) | data formatting | bytes 196608
  (68 shorter events, 3.9 us)
Async XLA Ops:
  0.0 14.5 %collective-permute-start = (bf16[4,8192]{1,0:T(4,128)(2,1)}, bf16[4,8192]{1,0:T(4,128)(2,1)S(1)}, u32[]{:S(2)}, u32[]{:S(2)}) collective-permute-start(bf16[4,8192]{1,0:T(4,128)(2,1)} %param.10), channel_id=1, source_target_pairs={{0,8},{1,9},{2,10},{3,11},{4,12},{5,13},{6,14},{7,15},{8,16},{9,17... | collective-permute-start | bytes 196616 | tf_op jit(solution)/shard_map/ppermute | solution.py:48
  3.0 11.5 %collective-permute-start.1 = (bf16[4,8192]{1,0:T(4,128)(2,1)}, bf16[4,8192]{1,0:T(4,128)(2,1)S(1)}, u32[]{:S(2)}, u32[]{:S(2)}) collective-permute-start(bf16[4,8192]{1,0:T(4,128)(2,1)} %param.10), channel_id=1, source_target_pairs={{0,16},{1,17},{2,18},{3,19},{4,20},{5,21},{6,22},{7,23},{8,24},{9,... | collective-permute-start | bytes 196616 | tf_op jit(solution)/shard_map/ppermute | solution.py:48
  5.6 9.0 %collective-permute-start.2 = (bf16[4,8192]{1,0:T(4,128)(2,1)}, bf16[4,8192]{1,0:T(4,128)(2,1)S(1)}, u32[]{:S(2)}, u32[]{:S(2)}) collective-permute-start(bf16[4,8192]{1,0:T(4,128)(2,1)} %param.10), channel_id=1, source_target_pairs={{0,24},{1,25},{2,26},{3,27},{4,28},{5,29},{6,30},{7,31},{8,0},{9,1... | collective-permute-start | bytes 196616 | tf_op jit(solution)/shard_map/ppermute | solution.py:48
  8.2 3.4 %copy-start.2 = (s32[256,1]{0,1:T(1,128)S(1)}, s32[256,1]{0,1:T(1,128)}, u32[]{:S(2)}) copy-start(s32[256,1]{0,1:T(1,128)} %param.9) | copy-start | bytes 3076
  8.2 3.4 %copy-start.3 = (s32[8,8]{1,0:T(8,128)S(1)}, s32[8,8]{1,0:T(8,128)}, u32[]{:S(2)}) copy-start(s32[8,8]{1,0:T(8,128)} %param.11) | copy-start | bytes 772
  8.3 5.2 %copy-start.1 = (bf16[4,8192]{1,0:T(4,128)(2,1)S(1)}, bf16[4,8192]{1,0:T(4,128)(2,1)}, u32[]{:S(2)}) copy-start(bf16[4,8192]{1,0:T(4,128)(2,1)} %param.10) | copy-start | bytes 196612
  14.7 3.2 %collective-permute-start.7 = (f32[8320]{0:T(1024)S(1)}, f32[8320]{0:T(1024)S(1)}, u32[]{:S(2)}, u32[]{:S(2)}) collective-permute-start(f32[8320]{0:T(1024)S(1)} %select_maximum_fusion), channel_id=1, source_target_pairs={{0,1},{1,0},{2,3},{3,2},{4,5},{5,4},{6,7},{7,6},{8,9},{9,8},{10,11... | collective-permute-start | bytes 99848 | tf_op jit(solution)/shard_map/ppermute | solution.py:118
  14.8 12.9 %collective-permute-start.3 = (bf16[16,4096]{1,0:T(8,128)(2,1)S(1)}, bf16[16,4096]{1,0:T(8,128)(2,1)S(1)}, u32[]{:S(2)}, u32[]{:S(2)}) collective-permute-start(bf16[16,4096]{1,0:T(8,128)(2,1)S(1)} %get-tuple-element.27), channel_id=1, source_target_pairs={{0,4},{1,5},{2,6},{3,7},{4,0},{5,1},{6,2},{7,3},{8,12},{9,13},{10,... | collective-permute-start | bytes 393224 | tf_op jit(solution)/shard_map/ppermute | solution.py:48
  16.4 12.0 %collective-permute-start.5 = (bf16[16,4096]{1,0:T(8,128)(2,1)S(1)}, bf16[16,4096]{1,0:T(8,128)(2,1)S(1)}, u32[]{:S(2)}, u32[]{:S(2)}) collective-permute-start(bf16[16,4096]{1,0:T(8,128)(2,1)S(1)} %get-tuple-element.28), channel_id=1, source_target_pairs={{0,2},{1,3},{2,0},{3,1},{4,6},{5,7},{6,4},{7,5},{8,10},{9,11},{10,... | collective-permute-start | bytes 393224 | tf_op jit(solution)/shard_map/ppermute | solution.py:48
  17.9 4.0 %collective-permute-start.8 = (f32[8320]{0:T(1024)S(1)}, f32[8320]{0:T(1024)S(1)}, u32[]{:S(2)}, u32[]{:S(2)}) collective-permute-start(f32[8320]{0:T(1024)S(1)} %add.147), channel_id=1, source_target_pairs={{0,8},{1,9},{2,10},{3,11},{4,12},{5,13},{6,14},{7,15},{8,0},{9,1},... | collective-permute-start | bytes 99848 | tf_op jit(solution)/shard_map/ppermute | solution.py:118
  21.9 5.3 %collective-permute-start.9 = (f32[8320]{0:T(1024)S(1)}, f32[8320]{0:T(1024)S(1)}, u32[]{:S(2)}, u32[]{:S(2)}) collective-permute-start(f32[8320]{0:T(1024)S(1)} %add.148), channel_id=1, source_target_pairs={{0,16},{1,17},{2,18},{3,19},{4,20},{5,21},{6,22},{7,23},{8,24},{9,... | collective-permute-start | bytes 99848 | tf_op jit(solution)/shard_map/ppermute | solution.py:118
  27.2 4.4 %collective-permute-start.10 = (f32[8320]{0:T(1024)S(1)}, f32[8320]{0:T(1024)S(1)}, u32[]{:S(2)}, u32[]{:S(2)}) collective-permute-start(f32[8320]{0:T(1024)S(1)} %add.149), channel_id=1, source_target_pairs={{0,4},{1,5},{2,6},{3,7},{4,0},{5,1},{6,2},{7,3},{8,12},{9,13},{10,... | collective-permute-start | bytes 99848 | tf_op jit(solution)/shard_map/ppermute | solution.py:118
  27.7 6.4 %collective-permute-start.4 = (bf16[2,16,4096]{2,1,0:T(8,128)(2,1)S(1)}, bf16[2,16,4096]{2,1,0:T(8,128)(2,1)S(1)}, u32[]{:S(2)}, u32[]{:S(2)}) collective-permute-start(bf16[2,16,4096]{2,1,0:T(8,128)(2,1)S(1)} %bitcast_dynamic-update-slice_fusion.6), channel_id=1, source_target_pairs={{0,2},{1,3},{2,0},{3,1},{4,6},{5,7},{6,4},{7,5},{8,10},{9,11},{10,... | collective-permute-start | bytes 786440 | tf_op jit(solution)/shard_map/ppermute | solution.py:48
  28.5 6.4 %collective-permute-start.6 = (bf16[2,16,4096]{2,1,0:T(8,128)(2,1)S(1)}, bf16[2,16,4096]{2,1,0:T(8,128)(2,1)S(1)}, u32[]{:S(2)}, u32[]{:S(2)}) collective-permute-start(bf16[2,16,4096]{2,1,0:T(8,128)(2,1)S(1)} %bitcast_dynamic-update-slice_fusion.4), channel_id=1, source_target_pairs={{0,4},{1,5},{2,6},{3,7},{4,0},{5,1},{6,2},{7,3},{8,12},{9,13},{10,... | collective-permute-start | bytes 786440 | tf_op jit(solution)/shard_map/ppermute | solution.py:48
  35.0 5.3 %copy-start = (bf16[256,8192]{1,0:T(8,128)(2,1)S(1)}, bf16[256,8192]{1,0:T(8,128)(2,1)}, u32[]{:S(2)}) copy-start(bf16[256,8192]{1,0:T(8,128)(2,1)} %param.7) | copy-start | bytes 12582916
  35.0 4.0 %collective-permute-start.12 = (f32[8320]{0:T(1024)S(1)}, f32[8320]{0:T(1024)S(1)}, u32[]{:S(2)}, u32[]{:S(2)}) collective-permute-start(f32[8320]{0:T(1024)S(1)} %add.150), channel_id=1, source_target_pairs={{0,2},{1,3},{2,0},{3,1},{4,6},{5,7},{6,4},{7,5},{8,10},{9,11},{10,... | collective-permute-start | bytes 99848 | tf_op jit(solution)/shard_map/ppermute | solution.py:118
  36.5 3.7 %collective-permute-start.11 = (bf16[64,8192]{1,0:T(8,128)(2,1)S(1)}, bf16[64,8192]{1,0:T(8,128)(2,1)S(1)}, u32[]{:S(2)}, u32[]{:S(2)}) collective-permute-start(bf16[64,8192]{1,0:T(8,128)(2,1)S(1)} %pad_maximum_fusion), channel_id=1, source_target_pairs={{0,1},{1,0},{2,3},{3,2},{4,5},{5,4},{6,7},{7,6},{8,9},{9,8},{10,11... | collective-permute-start | bytes 3145736 | tf_op jit(solution)/shard_map/ppermute | solution.py:89

commit v8 on v7

--- a/solution.py
+++ b/solution.py
@@ -137,8 +137,8 @@
     squares = jnp.sum(row_weights[:, None] * jnp.square(grad_rows.astype(jnp.float32)), axis=0)
     packed = jnp.concatenate([squares, jnp.zeros((128,), jnp.float32).at[0].set(jnp.sum(row_weights))])
     first = gather_rows(queries, factors[0], device_count)
-    first, packed = lax.optimization_barrier((first, packed))
-    levels = factors[-1:] + factors[:-1]
+    first, packed, destinations, tile_pattern = lax.optimization_barrier((first, packed, destinations, tile_pattern))
+    levels = list(factors)
     packed = butterfly_sum(packed, levels[:-1], device_count)
     joined, splits, orders = gather_streams(first, factors, device_count)
     joined, packed = lax.optimization_barrier((joined, packed))

time: 54.7 us -> 53.6 us (0.980)
  waiting for transfers between devices: 15.3 us -> 14.3 us
    ppermute x5, waiting for transfers between devices: 12 us -> 9.25 us  [butterfly_sum(): values = values + lax.ppermute(values, AXES, pairs)]
    ppermute x7, waiting for transfers between devices: 3.26 us -> 4.68 us  [gather_factor(): received = lax.ppermute(piece, AXES, shifted(factor, shift, device_count))]
    ppermute x5, starting transfers between devices: 3.19 us -> 2.61 us  [butterfly_sum(): values = values + lax.ppermute(values, AXES, pairs)]
  transfers between devices with their start and end apart: 13 -> 13, of which waited for: 6 -> 7; matrix products, arithmetic and copies ran while one was open for 16% -> 17% of each run, Pallas kernels for 0% -> 0%
where the time goes in v8:
time: 53.6 us; the launch traced here: 53.4 us
  starting transfers between devices  15.3 us (29%)
  waiting for transfers between devices  14.3 us (27%)
  blocking collectives  9.71 us (18%)
  other arithmetic  6.94 us (13%)
  matrix products  3.49 us (7%)
  local copies, waits for them, and re-layouts  3.11 us (6%)
    ppermute x7, starting transfers between devices, gather_factor(): received = lax.ppermute(piece, AXES, shifted(factor, shift, device_count))  12.2 us
    all_to_all x1, blocking collectives, local(): lax.all_to_all(bucket.reshape(blk_count, capacity, query_count), 'blk', s...  9.71 us
    ppermute x5, waiting for transfers between devices, butterfly_sum(): values = values + lax.ppermute(values, AXES, pairs)  9.25 us
    ppermute x7, waiting for transfers between devices, gather_factor(): received = lax.ppermute(piece, AXES, shifted(factor, shift, device_count))  4.68 us
    reduce_sum x1, other arithmetic, local(): jnp.sum(row_weights[:, None] * jnp.square(grad_rows.astype(jnp.float32)),...  3.38 us
    dot_general x2, matrix products, exchange_and_score(): jnp.einsum('rk,qk->rq', grad_rows[:, start:start + size], prepared, prefe...  3.28 us
    ppermute x5, starting transfers between devices, butterfly_sum(): values = values + lax.ppermute(values, AXES, pairs)  2.61 us
    mul x1, other arithmetic, local(): weight_scale = row_weights * inv_root  1.28 us
  transfers between devices with their start and end apart: 13, of which 7 were waited for; matrix products, arithmetic and copies ran while one was open for 17% of the time, Pallas kernels for 0%

profile of v8, /device:TPU:0, one launch (start us, length us, event | category | flops | bytes accessed | tf_op | source)
XLA Modules:
  0.0 53.4 jit_solution(10479683636548922302)
XLA Ops:
  0.0 3.0 %collective-permute-start = (bf16[4,8192]{1,0:T(4,128)(2,1)}, bf16[4,8192]{1,0:T(4,128)(2,1)S(1)}, u32[]{:S(2)}, u32[]{:S(2)}) collective-permute-start(bf16[4,8192]{1,0:T(4,128)(2,1)} %param.10), channel_id=1, source_target_pairs={{0,8},{1,9},{2,10},{3,11},{4,12},{5,13},{6,14},{7,15},{8,16},{9,17... | collective-permute-start | bytes 196616 | tf_op jit(solution)/shard_map/ppermute | solution.py:48
  3.0 2.6 %collective-permute-start.1 = (bf16[4,8192]{1,0:T(4,128)(2,1)}, bf16[4,8192]{1,0:T(4,128)(2,1)S(1)}, u32[]{:S(2)}, u32[]{:S(2)}) collective-permute-start(bf16[4,8192]{1,0:T(4,128)(2,1)} %param.10), channel_id=1, source_target_pairs={{0,16},{1,17},{2,18},{3,19},{4,20},{5,21},{6,22},{7,23},{8,24},{9,... | collective-permute-start | bytes 196616 | tf_op jit(solution)/shard_map/ppermute | solution.py:48
  5.6 1.3 %collective-permute-start.2 = (bf16[4,8192]{1,0:T(4,128)(2,1)}, bf16[4,8192]{1,0:T(4,128)(2,1)S(1)}, u32[]{:S(2)}, u32[]{:S(2)}) collective-permute-start(bf16[4,8192]{1,0:T(4,128)(2,1)} %param.10), channel_id=1, source_target_pairs={{0,24},{1,25},{2,26},{3,27},{4,28},{5,29},{6,30},{7,31},{8,0},{9,1... | collective-permute-start | bytes 196616 | tf_op jit(solution)/shard_map/ppermute | solution.py:48
  7.0 1.3 %broadcast_multiply_fusion = (f32[256]{0:T(256)S(1)}, f32[]{:T(128)}) fusion(f32[256]{0:T(256)} %param.8), kind=kLoop, calls=%fused_computation.56 | loop fusion | flops 511 | bytes 2052 | tf_op jit(solution)/shard_map/mul | solution.py:152
  8.2 3.4 %multiply_reduce_fusion = f32[8192]{0:T(1024)S(1)} fusion(bf16[256,8192]{1,0:T(8,128)(2,1)} %param.7, f32[256]{0:T(256)} %param.8), kind=kLoop, calls=%fused_computation.1 | loop fusion | flops 8380416 | bytes 4228096 | tf_op jit(solution)/shard_map/reduce_sum | solution.py:137
  11.8 0.7 %select_maximum_fusion = f32[8320]{0:T(1024)S(1)} fusion(f32[1]{0:T(128)} %bitcast.4, f32[8192]{0:T(1024)S(1)} %multiply_reduce_fusion), kind=kLoop, calls=%fused_computation.37 | loop fusion | flops 24960 | bytes 66052 | tf_op jit(solution)/shard_map/concatenate | solution.py:138
  12.9 0.7 %collective-permute-start.7 = (f32[8320]{0:T(1024)S(1)}, f32[8320]{0:T(1024)S(1)}, u32[]{:S(2)}, u32[]{:S(2)}) collective-permute-start(f32[8320]{0:T(1024)S(1)} %select_maximum_fusion), channel_id=1, source_target_pairs={{0,8},{1,9},{2,10},{3,11},{4,12},{5,13},{6,14},{7,15},{8,0},{9,1},... | collective-permute-start | bytes 99848 | tf_op jit(solution)/shard_map/ppermute | solution.py:118
  13.6 1.6 %collective-permute-start.3 = (bf16[16,4096]{1,0:T(8,128)(2,1)S(1)}, bf16[16,4096]{1,0:T(8,128)(2,1)S(1)}, u32[]{:S(2)}, u32[]{:S(2)}) collective-permute-start(bf16[16,4096]{1,0:T(8,128)(2,1)S(1)} %get-tuple-element.31), channel_id=1, source_target_pairs={{0,4},{1,5},{2,6},{3,7},{4,0},{5,1},{6,2},{7,3},{8,12},{9,13},{10,... | collective-permute-start | bytes 393224 | tf_op jit(solution)/shard_map/ppermute | solution.py:48
  15.2 1.5 %collective-permute-start.5 = (bf16[16,4096]{1,0:T(8,128)(2,1)S(1)}, bf16[16,4096]{1,0:T(8,128)(2,1)S(1)}, u32[]{:S(2)}, u32[]{:S(2)}) collective-permute-start(bf16[16,4096]{1,0:T(8,128)(2,1)S(1)} %get-tuple-element.32), channel_id=1, source_target_pairs={{0,2},{1,3},{2,0},{3,1},{4,6},{5,7},{6,4},{7,5},{8,10},{9,11},{10,... | collective-permute-start | bytes 393224 | tf_op jit(solution)/shard_map/ppermute | solution.py:48
  16.8 0.7 %gather_fusion = s32[256,8]{1,0:T(8,128)S(1)} fusion(s32[8,8]{1,0:T(8,128)S(1)} %bitcast.63, s32[1024]{0:T(1024)S(1)} %pad_clamp_fusion), kind=kCustom, calls=%fused_computation | custom fusion | bytes 17408 | tf_op jit(solution)/shard_map/jit(_take)/gather | solution.py:150
  17.6 0.6 %reduce-window.6 = s32[8,2,128]{2,0,1:T(8,128)S(1)} reduce-window(s32[8,2,128]{2,0,1:T(8,128)S(1)} %fusion.22, s32[]{:T(128)} %constant.191.clone.1), window={size=1x1x128 pad=0_0x0_0x127_0}, to_apply=%region_2.0 | reduce-window | flops 260096 | bytes 16388 | tf_op jit(solution)/shard_map/reduce-window
  18.6 0.8 %collective-permute-start.8 = (f32[8320]{0:T(1024)S(1)}, f32[8320]{0:T(1024)S(1)}, u32[]{:S(2)}, u32[]{:S(2)}) collective-permute-start(f32[8320]{0:T(1024)S(1)} %add.147), channel_id=1, source_target_pairs={{0,16},{1,17},{2,18},{3,19},{4,20},{5,21},{6,22},{7,23},{8,24},{9,... | collective-permute-start | bytes 99848 | tf_op jit(solution)/shard_map/ppermute | solution.py:118
  19.4 4.1 %collective-permute-done.8 = f32[8320]{0:T(1024)S(1)} collective-permute-done((f32[8320]{0:T(1024)S(1)}, f32[8320]{0:T(1024)S(1)}, u32[]{:S(2)}, u32[]{:S(2)}) %collective-permute-start.8) | collective-permute-done | bytes 33312 | tf_op jit(solution)/shard_map/ppermute | solution.py:118
  24.0 3.4 %collective-permute-done.9 = f32[8320]{0:T(1024)S(1)} collective-permute-done((f32[8320]{0:T(1024)S(1)}, f32[8320]{0:T(1024)S(1)}, u32[]{:S(2)}, u32[]{:S(2)}) %collective-permute-start.9) | collective-permute-done | bytes 33312 | tf_op jit(solution)/shard_map/ppermute | solution.py:118
  28.0 1.6 %collective-permute-start.4 = (bf16[2,16,4096]{2,1,0:T(8,128)(2,1)S(1)}, bf16[2,16,4096]{2,1,0:T(8,128)(2,1)S(1)}, u32[]{:S(2)}, u32[]{:S(2)}) collective-permute-start(bf16[2,16,4096]{2,1,0:T(8,128)(2,1)S(1)} %bitcast_dynamic-update-slice_fusion.6), channel_id=1, source_target_pairs={{0,2},{1,3},{2,0},{3,1},{4,6},{5,7},{6,4},{7,5},{8,10},{9,11},{10,... | collective-permute-start | bytes 786440 | tf_op jit(solution)/shard_map/ppermute | solution.py:48
  30.3 1.1 %collective-permute-done.10 = f32[8320]{0:T(1024)S(1)} collective-permute-done((f32[8320]{0:T(1024)S(1)}, f32[8320]{0:T(1024)S(1)}, u32[]{:S(2)}, u32[]{:S(2)}) %collective-permute-start.10) | collective-permute-done | bytes 33312 | tf_op jit(solution)/shard_map/ppermute | solution.py:118
  31.4 3.0 %collective-permute-done.4 = bf16[2,16,4096]{2,1,0:T(8,128)(2,1)S(1)} collective-permute-done((bf16[2,16,4096]{2,1,0:T(8,128)(2,1)S(1)}, bf16[2,16,4096]{2,1,0:T(8,128)(2,1)S(1)}, u32[]{:S(2)}, u32[]{:S(2)}) %collective-permute-start.4) | collective-permute-done | bytes 262176 | tf_op jit(solution)/shard_map/ppermute | solution.py:48
  34.5 1.6 %collective-permute-done.6 = bf16[2,16,4096]{2,1,0:T(8,128)(2,1)S(1)} collective-permute-done((bf16[2,16,4096]{2,1,0:T(8,128)(2,1)S(1)}, bf16[2,16,4096]{2,1,0:T(8,128)(2,1)S(1)}, u32[]{:S(2)}, u32[]{:S(2)}) %collective-permute-start.6) | collective-permute-done | bytes 262176 | tf_op jit(solution)/shard_map/ppermute | solution.py:48
  36.9 0.6 %collective-permute-done.12 = f32[8320]{0:T(1024)S(1)} collective-permute-done((f32[8320]{0:T(1024)S(1)}, f32[8320]{0:T(1024)S(1)}, u32[]{:S(2)}, u32[]{:S(2)}) %collective-permute-start.12) | collective-permute-done | bytes 33312 | tf_op jit(solution)/shard_map/ppermute | solution.py:118
  38.0 0.7 %fusion.19 = f32[8192]{0:T(1024)S(1)} fusion(f32[8320]{0:T(1024)S(1)} %add.151, f32[]{:T(128)} %bitcast.19), kind=kLoop, calls=%fused_computation.41 | loop fusion | flops 16384 | bytes 65540 | tf_op jit(solution)/shard_map/rsqrt | solution.py:147
  39.2 0.9 %fusion.4 = f32[256,128]{0,1:T(8,128)S(1)} fusion(bf16[256,8192]{1,0:T(8,128)(2,1)S(1)} %copy-done, bf16[128,8192]{1,0:T(8,128)(2,1)S(1)} %constant_dynamic-update-slice_fusion, f32[4096]{0:T(1024)S(1)} %get-tuple-element.33), kind=kOutput, calls=%fused_computation.9 | convolution fusion | flops 270008320 | bytes 3293184 | tf_op jit(solution)/shard_map/rk,qk->rq/dot_general | solution.py:95
  40.1 2.4 %fusion.7 = f32[256,128]{0,1:T(8,128)S(1)} fusion(bf16[256,8192]{1,0:T(8,128)(2,1)} %param.7, bf16[128,8192]{1,0:T(8,128)(2,1)S(1)} %constant_dynamic-update-slice_fusion, f32[4096]{0:T(1024)S(1)} %get-tuple-element.34), kind=kOutput, calls=%fused_computation.10 | convolution fusion | flops 270008320 | bytes 3293184 | tf_op jit(solution)/shard_map/rk,qk->rq/dot_general | solution.py:95
  43.0 9.7 %all_to_all.5 = bf16[8,48,128]{2,1,0:T(8,128)(2,1)S(1)} all-to-all(bf16[8,48,128]{2,1,0:T(8,128)(2,1)S(1)} %bitcast.67), channel_id=1, replica_groups=mesh['blk'=8,'harvest'=4] {'blk'}, dimensions={0} | all-to-all | bytes 196608 | tf_op jit(solution)/shard_map/all_to_all | solution.py:162
  52.7 0.6 %copy.32 = bf16[384,128]{1,0:T(8,128)(2,1)} copy(bf16[384,128]{1,0:T(8,128)(2,1)S(1)} %bitcast.66) | data formatting | bytes 196608
  (68 shorter events, 4.9 us)
Async XLA Ops:
  0.0 12.6 %collective-permute-start = (bf16[4,8192]{1,0:T(4,128)(2,1)}, bf16[4,8192]{1,0:T(4,128)(2,1)S(1)}, u32[]{:S(2)}, u32[]{:S(2)}) collective-permute-start(bf16[4,8192]{1,0:T(4,128)(2,1)} %param.10), channel_id=1, source_target_pairs={{0,8},{1,9},{2,10},{3,11},{4,12},{5,13},{6,14},{7,15},{8,16},{9,17... | collective-permute-start | bytes 196616 | tf_op jit(solution)/shard_map/ppermute | solution.py:48
  3.0 9.7 %collective-permute-start.1 = (bf16[4,8192]{1,0:T(4,128)(2,1)}, bf16[4,8192]{1,0:T(4,128)(2,1)S(1)}, u32[]{:S(2)}, u32[]{:S(2)}) collective-permute-start(bf16[4,8192]{1,0:T(4,128)(2,1)} %param.10), channel_id=1, source_target_pairs={{0,16},{1,17},{2,18},{3,19},{4,20},{5,21},{6,22},{7,23},{8,24},{9,... | collective-permute-start | bytes 196616 | tf_op jit(solution)/shard_map/ppermute | solution.py:48
  5.6 7.1 %collective-permute-start.2 = (bf16[4,8192]{1,0:T(4,128)(2,1)}, bf16[4,8192]{1,0:T(4,128)(2,1)S(1)}, u32[]{:S(2)}, u32[]{:S(2)}) collective-permute-start(bf16[4,8192]{1,0:T(4,128)(2,1)} %param.10), channel_id=1, source_target_pairs={{0,24},{1,25},{2,26},{3,27},{4,28},{5,29},{6,30},{7,31},{8,0},{9,1... | collective-permute-start | bytes 196616 | tf_op jit(solution)/shard_map/ppermute | solution.py:48
  8.2 3.5 %copy-start.1 = (bf16[4,8192]{1,0:T(4,128)(2,1)S(1)}, bf16[4,8192]{1,0:T(4,128)(2,1)}, u32[]{:S(2)}) copy-start(bf16[4,8192]{1,0:T(4,128)(2,1)} %param.10) | copy-start | bytes 196612
  11.6 5.1 %copy-start.2 = (s32[256,1]{0,1:T(1,128)S(1)}, s32[256,1]{0,1:T(1,128)}, u32[]{:S(2)}) copy-start(s32[256,1]{0,1:T(1,128)} %param.9) | copy-start | bytes 3076
  11.6 5.1 %copy-start.3 = (s32[8,8]{1,0:T(8,128)S(1)}, s32[8,8]{1,0:T(8,128)}, u32[]{:S(2)}) copy-start(s32[8,8]{1,0:T(8,128)} %param.11) | copy-start | bytes 772
  12.9 5.7 %collective-permute-start.7 = (f32[8320]{0:T(1024)S(1)}, f32[8320]{0:T(1024)S(1)}, u32[]{:S(2)}, u32[]{:S(2)}) collective-permute-start(f32[8320]{0:T(1024)S(1)} %select_maximum_fusion), channel_id=1, source_target_pairs={{0,8},{1,9},{2,10},{3,11},{4,12},{5,13},{6,14},{7,15},{8,0},{9,1},... | collective-permute-start | bytes 99848 | tf_op jit(solution)/shard_map/ppermute | solution.py:118
  13.6 14.4 %collective-permute-start.3 = (bf16[16,4096]{1,0:T(8,128)(2,1)S(1)}, bf16[16,4096]{1,0:T(8,128)(2,1)S(1)}, u32[]{:S(2)}, u32[]{:S(2)}) collective-permute-start(bf16[16,4096]{1,0:T(8,128)(2,1)S(1)} %get-tuple-element.31), channel_id=1, source_target_pairs={{0,4},{1,5},{2,6},{3,7},{4,0},{5,1},{6,2},{7,3},{8,12},{9,13},{10,... | collective-permute-start | bytes 393224 | tf_op jit(solution)/shard_map/ppermute | solution.py:48
  15.2 14.5 %collective-permute-start.5 = (bf16[16,4096]{1,0:T(8,128)(2,1)S(1)}, bf16[16,4096]{1,0:T(8,128)(2,1)S(1)}, u32[]{:S(2)}, u32[]{:S(2)}) collective-permute-start(bf16[16,4096]{1,0:T(8,128)(2,1)S(1)} %get-tuple-element.32), channel_id=1, source_target_pairs={{0,2},{1,3},{2,0},{3,1},{4,6},{5,7},{6,4},{7,5},{8,10},{9,11},{10,... | collective-permute-start | bytes 393224 | tf_op jit(solution)/shard_map/ppermute | solution.py:48
  18.6 4.9 %collective-permute-start.8 = (f32[8320]{0:T(1024)S(1)}, f32[8320]{0:T(1024)S(1)}, u32[]{:S(2)}, u32[]{:S(2)}) collective-permute-start(f32[8320]{0:T(1024)S(1)} %add.147), channel_id=1, source_target_pairs={{0,16},{1,17},{2,18},{3,19},{4,20},{5,21},{6,22},{7,23},{8,24},{9,... | collective-permute-start | bytes 99848 | tf_op jit(solution)/shard_map/ppermute | solution.py:118
  23.5 4.0 %collective-permute-start.9 = (f32[8320]{0:T(1024)S(1)}, f32[8320]{0:T(1024)S(1)}, u32[]{:S(2)}, u32[]{:S(2)}) collective-permute-start(f32[8320]{0:T(1024)S(1)} %add.148), channel_id=1, source_target_pairs={{0,4},{1,5},{2,6},{3,7},{4,0},{5,1},{6,2},{7,3},{8,12},{9,13},{10,... | collective-permute-start | bytes 99848 | tf_op jit(solution)/shard_map/ppermute | solution.py:118
  27.5 4.0 %collective-permute-start.10 = (f32[8320]{0:T(1024)S(1)}, f32[8320]{0:T(1024)S(1)}, u32[]{:S(2)}, u32[]{:S(2)}) collective-permute-start(f32[8320]{0:T(1024)S(1)} %add.149), channel_id=1, source_target_pairs={{0,2},{1,3},{2,0},{3,1},{4,6},{5,7},{6,4},{7,5},{8,10},{9,11},{10,... | collective-permute-start | bytes 99848 | tf_op jit(solution)/shard_map/ppermute | solution.py:118
  28.0 6.4 %collective-permute-start.4 = (bf16[2,16,4096]{2,1,0:T(8,128)(2,1)S(1)}, bf16[2,16,4096]{2,1,0:T(8,128)(2,1)S(1)}, u32[]{:S(2)}, u32[]{:S(2)}) collective-permute-start(bf16[2,16,4096]{2,1,0:T(8,128)(2,1)S(1)} %bitcast_dynamic-update-slice_fusion.6), channel_id=1, source_target_pairs={{0,2},{1,3},{2,0},{3,1},{4,6},{5,7},{6,4},{7,5},{8,10},{9,11},{10,... | collective-permute-start | bytes 786440 | tf_op jit(solution)/shard_map/ppermute | solution.py:48
  29.7 6.4 %collective-permute-start.6 = (bf16[2,16,4096]{2,1,0:T(8,128)(2,1)S(1)}, bf16[2,16,4096]{2,1,0:T(8,128)(2,1)S(1)}, u32[]{:S(2)}, u32[]{:S(2)}) collective-permute-start(bf16[2,16,4096]{2,1,0:T(8,128)(2,1)S(1)} %bitcast_dynamic-update-slice_fusion.4), channel_id=1, source_target_pairs={{0,4},{1,5},{2,6},{3,7},{4,0},{5,1},{6,2},{7,3},{8,12},{9,13},{10,... | collective-permute-start | bytes 786440 | tf_op jit(solution)/shard_map/ppermute | solution.py:48
  36.2 2.9 %copy-start = (bf16[256,8192]{1,0:T(8,128)(2,1)S(1)}, bf16[256,8192]{1,0:T(8,128)(2,1)}, u32[]{:S(2)}) copy-start(bf16[256,8192]{1,0:T(8,128)(2,1)} %param.7) | copy-start | bytes 12582916
  36.2 1.3 %collective-permute-start.12 = (f32[8320]{0:T(1024)S(1)}, f32[8320]{0:T(1024)S(1)}, u32[]{:S(2)}, u32[]{:S(2)}) collective-permute-start(f32[8320]{0:T(1024)S(1)} %add.150), channel_id=1, source_target_pairs={{0,1},{1,0},{2,3},{3,2},{4,5},{5,4},{6,7},{7,6},{8,9},{9,8},{10,11... | collective-permute-start | bytes 99848 | tf_op jit(solution)/shard_map/ppermute | solution.py:118
  36.3 2.8 %collective-permute-start.11 = (bf16[64,8192]{1,0:T(8,128)(2,1)S(1)}, bf16[64,8192]{1,0:T(8,128)(2,1)S(1)}, u32[]{:S(2)}, u32[]{:S(2)}) collective-permute-start(bf16[64,8192]{1,0:T(8,128)(2,1)S(1)} %pad_maximum_fusion), channel_id=1, source_target_pairs={{0,1},{1,0},{2,3},{3,2},{4,5},{5,4},{6,7},{7,6},{8,9},{9,8},{10,11... | collective-permute-start | bytes 3145736 | tf_op jit(solution)/shard_map/ppermute | solution.py:89

commit v9 on v8

--- a/solution.py
+++ b/solution.py
@@ -62,20 +62,43 @@
     return list(zip(starts, sizes))
 
 
-def gather_streams(first, factors, device_count):
+def psum_steps(factors):
+    steps = []
+    for factor in factors:
+        bit = 1
+        while bit < factor[0]:
+            steps.append((factor, bit))
+            bit *= 2
+    return steps
+
+
+def psum_step(values, step, device_count):
+    factor, bit = step
+    size, stride = factor
+    pairs = [(i, i + ((coordinate(i, factor) ^ bit) - coordinate(i, factor)) * stride) for i in range(device_count)]
+    return values + lax.ppermute(values, AXES, pairs)
+
+
+def gather_streams(first, packed, steps, factors, device_count):
     rank = len(factors)
     middle = list(range(1, rank - 1))
     splits = column_splits(first.shape[1], max(len(middle), 1))
-    parts, orders = [], []
-    for j, (start, size) in enumerate(splits):
-        order = middle[j:] + middle[:j]
-        part = first[:, start:start + size]
-        for position in order:
-            part = gather_factor(part, factors[position], device_count)
-        parts.append(part.reshape(-1, size))
-        orders.append(order)
+    orders = [middle[j:] + middle[:j] for j in range(len(splits))]
+    parts = [first[:, start:start + size] for start, size in splits]
+    done = 0
+    for level in range(len(middle)):
+        parts = [gather_factor(part, factors[order[level]], device_count) for part, order in zip(parts, orders)]
+        target = min(level + 2, len(steps) - 1) if level + 1 < len(middle) else len(steps) - 1
+        while done < target:
+            packed = psum_step(packed, steps[done], device_count)
+            done += 1
+        parts, packed = lax.optimization_barrier((parts, packed))
+    while done < len(steps):
+        packed = psum_step(packed, steps[done], device_count)
+        done += 1
+    parts = [part.reshape(-1, size) for part, (start, size) in zip(parts, splits)]
     joined = jnp.concatenate(parts, axis=1) if len(parts) > 1 else parts[0]
-    return joined, splits, orders
+    return joined, packed, splits, orders
 
 
 def exchange_and_score(grad_rows, joined, scaling, splits, orders, factors, rows, device_count):
@@ -138,11 +161,7 @@
     packed = jnp.concatenate([squares, jnp.zeros((128,), jnp.float32).at[0].set(jnp.sum(row_weights))])
     first = gather_rows(queries, factors[0], device_count)
     first, packed, destinations, tile_pattern = lax.optimization_barrier((first, packed, destinations, tile_pattern))
-    levels = list(factors)
-    packed = butterfly_sum(packed, levels[:-1], device_count)
-    joined, splits, orders = gather_streams(first, factors, device_count)
-    joined, packed = lax.optimization_barrier((joined, packed))
-    packed = butterfly_sum(packed, levels[-1:], device_count)
+    joined, packed, splits, orders = gather_streams(first, packed, psum_steps(factors), factors, device_count)
     total_sq, total_weight = packed[:width], packed[width]
     scaling = lax.rsqrt(total_sq / total_weight + 1e-06)
     raw = exchange_and_score(grad_rows, joined, scaling, splits, orders, factors, queries.shape[0], device_count)

time: 53.6 us -> 52.3 us (0.976)
  waiting for transfers between devices: 14.3 us -> 9.77 us
  other arithmetic: 6.94 us -> 8.46 us
  starting transfers between devices: 15.3 us -> 16.3 us
  local copies, waits for them, and re-layouts: 3.11 us -> 3.94 us
    ppermute x7, waiting for transfers between devices: 4.68 us -> 0.02 us  [gather_factor(): received = lax.ppermute(piece, AXES, shifted(factor, shift, device_count))]
    ppermute x5, starting transfers between devices: 2.61 us -> 4.16 us  [psum_step(): return values + lax.ppermute(values, AXES, pairs)]
    concatenate x0 -> x1, other arithmetic: none -> 1.51 us  [exchange_and_score(): full = jnp.concatenate(blocks, axis=0) if size_last > 1 else joined]
    unnamed x10 -> x9, local copies, waits for them, and re-layouts: 0.73 us -> 1.63 us
  transfers between devices with their start and end apart: 13 -> 13, of which waited for: 7 -> 4; matrix products, arithmetic and copies ran while one was open for 17% -> 17% of each run, Pallas kernels for 0% -> 0%
where the time goes in v9:
time: 52.3 us; the launch traced here: 52.1 us
  starting transfers between devices  16.3 us (31%)
  waiting for transfers between devices  9.77 us (19%)
  blocking collectives  9.55 us (18%)
  other arithmetic  8.46 us (16%)
  local copies, waits for them, and re-layouts  3.94 us (8%)
  matrix products  3.48 us (7%)
  between operations  0.55 us (1%)
    ppermute x7, starting transfers between devices, gather_factor(): received = lax.ppermute(piece, AXES, shifted(factor, shift, device_count))  12.1 us
    ppermute x5, waiting for transfers between devices, psum_step(): return values + lax.ppermute(values, AXES, pairs)  9.75 us
    all_to_all x1, blocking collectives, local(): lax.all_to_all(bucket.reshape(blk_count, capacity, query_count), 'blk', s...  9.55 us
    ppermute x5, starting transfers between devices, psum_step(): return values + lax.ppermute(values, AXES, pairs)  4.16 us
    reduce_sum x1, other arithmetic, local(): jnp.sum(row_weights[:, None] * jnp.square(grad_rows.astype(jnp.float32)),...  3.38 us
    dot_general x2, matrix products, exchange_and_score(): jnp.einsum('rk,qk->rq', grad_rows[:, start:start + size], prepared, prefe...  3.27 us
    unnamed x9, local copies, waits for them, and re-layouts  1.63 us
    concatenate x1, other arithmetic, exchange_and_score(): full = jnp.concatenate(blocks, axis=0) if size_last > 1 else joined  1.51 us
  transfers between devices with their start and end apart: 13, of which 4 were waited for; matrix products, arithmetic and copies ran while one was open for 17% of the time, Pallas kernels for 0%

profile of v9, /device:TPU:0, one launch (start us, length us, event | category | flops | bytes accessed | tf_op | source)
XLA Modules:
  0.0 52.1 jit_solution(1654670518935295995)
XLA Ops:
  0.0 3.0 %collective-permute-start = (bf16[4,8192]{1,0:T(4,128)(2,1)}, bf16[4,8192]{1,0:T(4,128)(2,1)S(1)}, u32[]{:S(2)}, u32[]{:S(2)}) collective-permute-start(bf16[4,8192]{1,0:T(4,128)(2,1)} %param.10), channel_id=1, source_target_pairs={{0,8},{1,9},{2,10},{3,11},{4,12},{5,13},{6,14},{7,15},{8,16},{9,17... | collective-permute-start | bytes 196616 | tf_op jit(solution)/shard_map/ppermute | solution.py:48
  3.0 2.6 %collective-permute-start.1 = (bf16[4,8192]{1,0:T(4,128)(2,1)}, bf16[4,8192]{1,0:T(4,128)(2,1)S(1)}, u32[]{:S(2)}, u32[]{:S(2)}) collective-permute-start(bf16[4,8192]{1,0:T(4,128)(2,1)} %param.10), channel_id=1, source_target_pairs={{0,16},{1,17},{2,18},{3,19},{4,20},{5,21},{6,22},{7,23},{8,24},{9,... | collective-permute-start | bytes 196616 | tf_op jit(solution)/shard_map/ppermute | solution.py:48
  5.6 1.3 %collective-permute-start.2 = (bf16[4,8192]{1,0:T(4,128)(2,1)}, bf16[4,8192]{1,0:T(4,128)(2,1)S(1)}, u32[]{:S(2)}, u32[]{:S(2)}) collective-permute-start(bf16[4,8192]{1,0:T(4,128)(2,1)} %param.10), channel_id=1, source_target_pairs={{0,24},{1,25},{2,26},{3,27},{4,28},{5,29},{6,30},{7,31},{8,0},{9,1... | collective-permute-start | bytes 196616 | tf_op jit(solution)/shard_map/ppermute | solution.py:48
  7.0 1.3 %broadcast_multiply_fusion = (f32[256]{0:T(256)S(1)}, f32[]{:T(128)}) fusion(f32[256]{0:T(256)} %param.8), kind=kLoop, calls=%fused_computation.55 | loop fusion | flops 511 | bytes 2052 | tf_op jit(solution)/shard_map/mul | solution.py:171
  8.2 3.4 %multiply_reduce_fusion = f32[8192]{0:T(1024)S(1)} fusion(bf16[256,8192]{1,0:T(8,128)(2,1)} %param.7, f32[256]{0:T(256)} %param.8), kind=kLoop, calls=%fused_computation.1 | loop fusion | flops 8380416 | bytes 4228096 | tf_op jit(solution)/shard_map/reduce_sum | solution.py:160
  12.8 0.7 %collective-permute-start.5 = (f32[8320]{0:T(1024)S(1)}, f32[8320]{0:T(1024)S(1)}, u32[]{:S(2)}, u32[]{:S(2)}) collective-permute-start(f32[8320]{0:T(1024)S(1)} %select_maximum_fusion), channel_id=1, source_target_pairs={{0,8},{1,9},{2,10},{3,11},{4,12},{5,13},{6,14},{7,15},{8,0},{9,1},... | collective-permute-start | bytes 99848 | tf_op jit(solution)/shard_map/ppermute | solution.py:79
  13.6 1.6 %collective-permute-start.4 = (bf16[16,4096]{1,0:T(8,128)(2,1)S(1)}, bf16[16,4096]{1,0:T(8,128)(2,1)S(1)}, u32[]{:S(2)}, u32[]{:S(2)}) collective-permute-start(bf16[16,4096]{1,0:T(8,128)(2,1)S(1)} %get-tuple-element.39), channel_id=1, source_target_pairs={{0,2},{1,3},{2,0},{3,1},{4,6},{5,7},{6,4},{7,5},{8,10},{9,11},{10,... | collective-permute-start | bytes 393224 | tf_op jit(solution)/shard_map/ppermute | solution.py:48
  15.2 1.5 %collective-permute-start.3 = (bf16[16,4096]{1,0:T(8,128)(2,1)S(1)}, bf16[16,4096]{1,0:T(8,128)(2,1)S(1)}, u32[]{:S(2)}, u32[]{:S(2)}) collective-permute-start(bf16[16,4096]{1,0:T(8,128)(2,1)S(1)} %get-tuple-element.40), channel_id=1, source_target_pairs={{0,4},{1,5},{2,6},{3,7},{4,0},{5,1},{6,2},{7,3},{8,12},{9,13},{10,... | collective-permute-start | bytes 393224 | tf_op jit(solution)/shard_map/ppermute | solution.py:48
  17.4 0.8 %collective-permute-start.6 = (f32[8320]{0:T(1024)S(1)}, f32[8320]{0:T(1024)S(1)}, u32[]{:S(2)}, u32[]{:S(2)}) collective-permute-start(f32[8320]{0:T(1024)S(1)} %add.147), channel_id=1, source_target_pairs={{0,16},{1,17},{2,18},{3,19},{4,20},{5,21},{6,22},{7,23},{8,24},{9,... | collective-permute-start | bytes 99848 | tf_op jit(solution)/shard_map/ppermute | solution.py:79
  18.4 3.9 %collective-permute-done.6 = f32[8320]{0:T(1024)S(1)} collective-permute-done((f32[8320]{0:T(1024)S(1)}, f32[8320]{0:T(1024)S(1)}, u32[]{:S(2)}, u32[]{:S(2)}) %collective-permute-start.6) | collective-permute-done | bytes 33312 | tf_op jit(solution)/shard_map/ppermute | solution.py:79
  22.4 1.0 %collective-permute-start.9 = (f32[8320]{0:T(1024)S(1)}, f32[8320]{0:T(1024)S(1)}, u32[]{:S(2)}, u32[]{:S(2)}) collective-permute-start(f32[8320]{0:T(1024)S(1)} %add.148), channel_id=1, source_target_pairs={{0,4},{1,5},{2,6},{3,7},{4,0},{5,1},{6,2},{7,3},{8,12},{9,13},{10,... | collective-permute-start | bytes 99848 | tf_op jit(solution)/shard_map/ppermute | solution.py:79
  23.4 1.1 %collective-permute-start.8 = (bf16[2,16,4096]{2,1,0:T(8,128)(2,1)S(1)}, bf16[2,16,4096]{2,1,0:T(8,128)(2,1)S(1)}, u32[]{:S(2)}, u32[]{:S(2)}) collective-permute-start(bf16[2,16,4096]{2,1,0:T(8,128)(2,1)S(1)} %bitcast_dynamic-update-slice_fusion.4), channel_id=1, source_target_pairs={{0,4},{1,5},{2,6},{3,7},{4,0},{5,1},{6,2},{7,3},{8,12},{9,13},{10,... | collective-permute-start | bytes 786440 | tf_op jit(solution)/shard_map/ppermute | solution.py:48
  24.6 0.9 %collective-permute-start.7 = (bf16[2,16,4096]{2,1,0:T(8,128)(2,1)S(1)}, bf16[2,16,4096]{2,1,0:T(8,128)(2,1)S(1)}, u32[]{:S(2)}, u32[]{:S(2)}) collective-permute-start(bf16[2,16,4096]{2,1,0:T(8,128)(2,1)S(1)} %bitcast_dynamic-update-slice_fusion.6), channel_id=1, source_target_pairs={{0,2},{1,3},{2,0},{3,1},{4,6},{5,7},{6,4},{7,5},{8,10},{9,11},{10,... | collective-permute-start | bytes 786440 | tf_op jit(solution)/shard_map/ppermute | solution.py:48
  25.5 0.9 %collective-permute-done.9 = f32[8320]{0:T(1024)S(1)} collective-permute-done((f32[8320]{0:T(1024)S(1)}, f32[8320]{0:T(1024)S(1)}, u32[]{:S(2)}, u32[]{:S(2)}) %collective-permute-start.9) | collective-permute-done | bytes 33312 | tf_op jit(solution)/shard_map/ppermute | solution.py:79
  26.5 1.1 %collective-permute-start.10 = (f32[8320]{0:T(1024)S(1)}, f32[8320]{0:T(1024)S(1)}, u32[]{:S(2)}, u32[]{:S(2)}) collective-permute-start(f32[8320]{0:T(1024)S(1)} %add.149), channel_id=1, source_target_pairs={{0,2},{1,3},{2,0},{3,1},{4,6},{5,7},{6,4},{7,5},{8,10},{9,11},{10,... | collective-permute-start | bytes 99848 | tf_op jit(solution)/shard_map/ppermute | solution.py:79
  27.6 3.8 %collective-permute-done.10 = f32[8320]{0:T(1024)S(1)} collective-permute-done((f32[8320]{0:T(1024)S(1)}, f32[8320]{0:T(1024)S(1)}, u32[]{:S(2)}, u32[]{:S(2)}) %collective-permute-start.10) | collective-permute-done | bytes 33312 | tf_op jit(solution)/shard_map/ppermute | solution.py:79
  31.8 0.7 %gather_fusion = s32[256,8]{1,0:T(8,128)S(1)} fusion(s32[8,8]{1,0:T(8,128)S(1)} %bitcast.63, s32[1024]{0:T(1024)S(1)} %pad_clamp_fusion), kind=kCustom, calls=%fused_computation | custom fusion | bytes 17408 | tf_op jit(solution)/shard_map/jit(_take)/gather | solution.py:169
  33.3 1.1 %collective-permute-done.12 = f32[8320]{0:T(1024)S(1)} collective-permute-done((f32[8320]{0:T(1024)S(1)}, f32[8320]{0:T(1024)S(1)}, u32[]{:S(2)}, u32[]{:S(2)}) %collective-permute-start.12) | collective-permute-done | bytes 33312 | tf_op jit(solution)/shard_map/ppermute | solution.py:79
  34.9 0.7 %fusion.19 = f32[8192]{0:T(1024)S(1)} fusion(f32[8320]{0:T(1024)S(1)} %add.151, f32[]{:T(128)} %bitcast.19), kind=kLoop, calls=%fused_computation.42 | loop fusion | flops 16384 | bytes 65540 | tf_op jit(solution)/shard_map/rsqrt | solution.py:166
  35.6 1.5 %pad_maximum_fusion = bf16[128,8192]{1,0:T(8,128)(2,1)S(1)} fusion(bf16[64,8192]{1,0:T(8,128)(2,1)} %collective-permute-done.11, bf16[64,4096]{1,0:T(8,128)(2,1)S(1)} %bitcast.67, bf16[64,4096]{1,0:T(8,128)(2,1)S(1)} %bitcast.65), kind=kLoop, calls=%fused_computation.2 | loop fusion | flops 6291456 | bytes 4194304 | tf_op jit(solution)/shard_map/concatenate | solution.py:114
  37.1 1.0 %copy-done = bf16[256,8192]{1,0:T(8,128)(2,1)S(1)} copy-done((bf16[256,8192]{1,0:T(8,128)(2,1)S(1)}, bf16[256,8192]{1,0:T(8,128)(2,1)}, u32[]{:S(2)}) %copy-start) | copy-done | bytes 4194328
  38.1 0.8 %fusion.4 = f32[256,128]{0,1:T(8,128)S(1)} fusion(bf16[256,8192]{1,0:T(8,128)(2,1)S(1)} %copy-done, bf16[128,8192]{1,0:T(8,128)(2,1)S(1)} %pad_maximum_fusion, f32[4096]{0:T(1024)S(1)} %get-tuple-element.41), kind=kOutput, calls=%fused_computation.10 | convolution fusion | flops 270008320 | bytes 3293184 | tf_op jit(solution)/shard_map/rk,qk->rq/dot_general | solution.py:118
  39.0 2.4 %fusion.7 = f32[256,128]{0,1:T(8,128)S(1)} fusion(bf16[256,8192]{1,0:T(8,128)(2,1)} %param.7, bf16[128,8192]{1,0:T(8,128)(2,1)S(1)} %pad_maximum_fusion, f32[4096]{0:T(1024)S(1)} %get-tuple-element.42), kind=kOutput, calls=%fused_computation.11 | convolution fusion | flops 270008320 | bytes 3293184 | tf_op jit(solution)/shard_map/rk,qk->rq/dot_general | solution.py:118
  41.9 9.5 %all_to_all.5 = bf16[8,48,128]{2,1,0:T(8,128)(2,1)S(1)} all-to-all(bf16[8,48,128]{2,1,0:T(8,128)(2,1)S(1)} %bitcast.69), channel_id=1, replica_groups=mesh['blk'=8,'harvest'=4] {'blk'}, dimensions={0} | all-to-all | bytes 196608 | tf_op jit(solution)/shard_map/all_to_all | solution.py:181
  (67 shorter events, 4.7 us)
Async XLA Ops:
  0.0 12.6 %collective-permute-start = (bf16[4,8192]{1,0:T(4,128)(2,1)}, bf16[4,8192]{1,0:T(4,128)(2,1)S(1)}, u32[]{:S(2)}, u32[]{:S(2)}) collective-permute-start(bf16[4,8192]{1,0:T(4,128)(2,1)} %param.10), channel_id=1, source_target_pairs={{0,8},{1,9},{2,10},{3,11},{4,12},{5,13},{6,14},{7,15},{8,16},{9,17... | collective-permute-start | bytes 196616 | tf_op jit(solution)/shard_map/ppermute | solution.py:48
  3.0 9.6 %collective-permute-start.1 = (bf16[4,8192]{1,0:T(4,128)(2,1)}, bf16[4,8192]{1,0:T(4,128)(2,1)S(1)}, u32[]{:S(2)}, u32[]{:S(2)}) collective-permute-start(bf16[4,8192]{1,0:T(4,128)(2,1)} %param.10), channel_id=1, source_target_pairs={{0,16},{1,17},{2,18},{3,19},{4,20},{5,21},{6,22},{7,23},{8,24},{9,... | collective-permute-start | bytes 196616 | tf_op jit(solution)/shard_map/ppermute | solution.py:48
  5.6 7.1 %collective-permute-start.2 = (bf16[4,8192]{1,0:T(4,128)(2,1)}, bf16[4,8192]{1,0:T(4,128)(2,1)S(1)}, u32[]{:S(2)}, u32[]{:S(2)}) collective-permute-start(bf16[4,8192]{1,0:T(4,128)(2,1)} %param.10), channel_id=1, source_target_pairs={{0,24},{1,25},{2,26},{3,27},{4,28},{5,29},{6,30},{7,31},{8,0},{9,1... | collective-permute-start | bytes 196616 | tf_op jit(solution)/shard_map/ppermute | solution.py:48
  8.2 3.5 %copy-start.1 = (bf16[4,8192]{1,0:T(4,128)(2,1)S(1)}, bf16[4,8192]{1,0:T(4,128)(2,1)}, u32[]{:S(2)}) copy-start(bf16[4,8192]{1,0:T(4,128)(2,1)} %param.10) | copy-start | bytes 196612
  11.6 5.1 %copy-start.2 = (s32[256,1]{0,1:T(1,128)S(1)}, s32[256,1]{0,1:T(1,128)}, u32[]{:S(2)}) copy-start(s32[256,1]{0,1:T(1,128)} %param.9) | copy-start | bytes 3076
  12.8 4.6 %collective-permute-start.5 = (f32[8320]{0:T(1024)S(1)}, f32[8320]{0:T(1024)S(1)}, u32[]{:S(2)}, u32[]{:S(2)}) collective-permute-start(f32[8320]{0:T(1024)S(1)} %select_maximum_fusion), channel_id=1, source_target_pairs={{0,8},{1,9},{2,10},{3,11},{4,12},{5,13},{6,14},{7,15},{8,0},{9,1},... | collective-permute-start | bytes 99848 | tf_op jit(solution)/shard_map/ppermute | solution.py:79
  13.6 8.7 %collective-permute-start.4 = (bf16[16,4096]{1,0:T(8,128)(2,1)S(1)}, bf16[16,4096]{1,0:T(8,128)(2,1)S(1)}, u32[]{:S(2)}, u32[]{:S(2)}) collective-permute-start(bf16[16,4096]{1,0:T(8,128)(2,1)S(1)} %get-tuple-element.39), channel_id=1, source_target_pairs={{0,2},{1,3},{2,0},{3,1},{4,6},{5,7},{6,4},{7,5},{8,10},{9,11},{10,... | collective-permute-start | bytes 393224 | tf_op jit(solution)/shard_map/ppermute | solution.py:48
  15.2 7.2 %collective-permute-start.3 = (bf16[16,4096]{1,0:T(8,128)(2,1)S(1)}, bf16[16,4096]{1,0:T(8,128)(2,1)S(1)}, u32[]{:S(2)}, u32[]{:S(2)}) collective-permute-start(bf16[16,4096]{1,0:T(8,128)(2,1)S(1)} %get-tuple-element.40), channel_id=1, source_target_pairs={{0,4},{1,5},{2,6},{3,7},{4,0},{5,1},{6,2},{7,3},{8,12},{9,13},{10,... | collective-permute-start | bytes 393224 | tf_op jit(solution)/shard_map/ppermute | solution.py:48
  17.4 4.9 %collective-permute-start.6 = (f32[8320]{0:T(1024)S(1)}, f32[8320]{0:T(1024)S(1)}, u32[]{:S(2)}, u32[]{:S(2)}) collective-permute-start(f32[8320]{0:T(1024)S(1)} %add.147), channel_id=1, source_target_pairs={{0,16},{1,17},{2,18},{3,19},{4,20},{5,21},{6,22},{7,23},{8,24},{9,... | collective-permute-start | bytes 99848 | tf_op jit(solution)/shard_map/ppermute | solution.py:79
  22.4 4.0 %collective-permute-start.9 = (f32[8320]{0:T(1024)S(1)}, f32[8320]{0:T(1024)S(1)}, u32[]{:S(2)}, u32[]{:S(2)}) collective-permute-start(f32[8320]{0:T(1024)S(1)} %add.148), channel_id=1, source_target_pairs={{0,4},{1,5},{2,6},{3,7},{4,0},{5,1},{6,2},{7,3},{8,12},{9,13},{10,... | collective-permute-start | bytes 99848 | tf_op jit(solution)/shard_map/ppermute | solution.py:79
  23.4 8.0 %collective-permute-start.8 = (bf16[2,16,4096]{2,1,0:T(8,128)(2,1)S(1)}, bf16[2,16,4096]{2,1,0:T(8,128)(2,1)S(1)}, u32[]{:S(2)}, u32[]{:S(2)}) collective-permute-start(bf16[2,16,4096]{2,1,0:T(8,128)(2,1)S(1)} %bitcast_dynamic-update-slice_fusion.4), channel_id=1, source_target_pairs={{0,4},{1,5},{2,6},{3,7},{4,0},{5,1},{6,2},{7,3},{8,12},{9,13},{10,... | collective-permute-start | bytes 786440 | tf_op jit(solution)/shard_map/ppermute | solution.py:48
  24.6 6.9 %collective-permute-start.7 = (bf16[2,16,4096]{2,1,0:T(8,128)(2,1)S(1)}, bf16[2,16,4096]{2,1,0:T(8,128)(2,1)S(1)}, u32[]{:S(2)}, u32[]{:S(2)}) collective-permute-start(bf16[2,16,4096]{2,1,0:T(8,128)(2,1)S(1)} %bitcast_dynamic-update-slice_fusion.6), channel_id=1, source_target_pairs={{0,2},{1,3},{2,0},{3,1},{4,6},{5,7},{6,4},{7,5},{8,10},{9,11},{10,... | collective-permute-start | bytes 786440 | tf_op jit(solution)/shard_map/ppermute | solution.py:48
  26.4 5.2 %copy-start.3 = (s32[8,8]{1,0:T(8,128)S(1)}, s32[8,8]{1,0:T(8,128)}, u32[]{:S(2)}) copy-start(s32[8,8]{1,0:T(8,128)} %param.11) | copy-start | bytes 772
  26.5 5.0 %collective-permute-start.10 = (f32[8320]{0:T(1024)S(1)}, f32[8320]{0:T(1024)S(1)}, u32[]{:S(2)}, u32[]{:S(2)}) collective-permute-start(f32[8320]{0:T(1024)S(1)} %add.149), channel_id=1, source_target_pairs={{0,2},{1,3},{2,0},{3,1},{4,6},{5,7},{6,4},{7,5},{8,10},{9,11},{10,... | collective-permute-start | bytes 99848 | tf_op jit(solution)/shard_map/ppermute | solution.py:79
  31.6 4.0 %collective-permute-start.11 = (bf16[64,8192]{1,0:T(8,128)(2,1)S(1)}, bf16[64,8192]{1,0:T(8,128)(2,1)}, u32[]{:S(2)}, u32[]{:S(2)}) collective-permute-start(bf16[64,8192]{1,0:T(8,128)(2,1)S(1)} %pad_maximum_fusion.1), channel_id=1, source_target_pairs={{0,1},{1,0},{2,3},{3,2},{4,5},{5,4},{6,7},{7,6},{8,9},{9,8},{10,11... | collective-permute-start | bytes 3145736 | tf_op jit(solution)/shard_map/ppermute | solution.py:112
  32.7 1.7 %collective-permute-start.12 = (f32[8320]{0:T(1024)S(1)}, f32[8320]{0:T(1024)S(1)}, u32[]{:S(2)}, u32[]{:S(2)}) collective-permute-start(f32[8320]{0:T(1024)S(1)} %add.150), channel_id=1, source_target_pairs={{0,1},{1,0},{2,3},{3,2},{4,5},{5,4},{6,7},{7,6},{8,9},{9,8},{10,11... | collective-permute-start | bytes 99848 | tf_op jit(solution)/shard_map/ppermute | solution.py:79
  35.6 2.5 %copy-start = (bf16[256,8192]{1,0:T(8,128)(2,1)S(1)}, bf16[256,8192]{1,0:T(8,128)(2,1)}, u32[]{:S(2)}) copy-start(bf16[256,8192]{1,0:T(8,128)(2,1)} %param.7) | copy-start | bytes 12582916

commit v10 on v9

--- a/solution.py
+++ b/solution.py
@@ -92,12 +92,14 @@
         while done < target:
             packed = psum_step(packed, steps[done], device_count)
             done += 1
-        parts, packed = lax.optimization_barrier((parts, packed))
+        if level + 1 < len(middle):
+            parts, packed = lax.optimization_barrier((parts, packed))
+    parts = [part.reshape(-1, size) for part, (start, size) in zip(parts, splits)]
+    joined = jnp.concatenate(parts, axis=1) if len(parts) > 1 else parts[0]
+    joined, packed = lax.optimization_barrier((joined, packed))
     while done < len(steps):
         packed = psum_step(packed, steps[done], device_count)
         done += 1
-    parts = [part.reshape(-1, size) for part, (start, size) in zip(parts, splits)]
-    joined = jnp.concatenate(parts, axis=1) if len(parts) > 1 else parts[0]
     return joined, packed, splits, orders
 
 

time: 52.3 us -> 49.6 us (0.948)
  other arithmetic: 8.46 us -> 6.94 us
  local copies, waits for them, and re-layouts: 3.94 us -> 3.13 us
  blocking collectives: 9.55 us -> 10.1 us
    concatenate x1 -> x0, other arithmetic: 1.51 us -> none  [exchange_and_score(): full = jnp.concatenate(blocks, axis=0) if size_last > 1 else joined]
    ppermute x5, starting transfers between devices: 4.16 us -> 3.1 us  [psum_step(): return values + lax.ppermute(values, AXES, pairs)]
    unnamed x9 -> x10, local copies, waits for them, and re-layouts: 1.63 us -> 0.73 us
    ppermute x5, waiting for transfers between devices: 9.75 us -> 8.98 us  [psum_step(): return values + lax.ppermute(values, AXES, pairs)]
    all_to_all x1, blocking collectives: 9.55 us -> 10.1 us  [local(): lax.all_to_all(bucket.reshape(blk_count, capacity, query_count), 'blk', s...]
  transfers between devices with their start and end apart: 13 -> 13, of which waited for: 4 -> 5; matrix products, arithmetic and copies ran while one was open for 17% -> 18% of each run, Pallas kernels for 0% -> 0%
where the time goes in v10:
time: 49.6 us; the launch traced here: 49.3 us
  starting transfers between devices  15.8 us (32%)
  blocking collectives  10.1 us (20%)
  waiting for transfers between devices  9.38 us (19%)
  other arithmetic  6.94 us (14%)
  matrix products  3.49 us (7%)
  local copies, waits for them, and re-layouts  3.13 us (6%)
  between operations  0.56 us (1%)
    ppermute x7, starting transfers between devices, gather_factor(): received = lax.ppermute(piece, AXES, shifted(factor, shift, device_count))  12.2 us
    all_to_all x1, blocking collectives, local(): lax.all_to_all(bucket.reshape(blk_count, capacity, query_count), 'blk', s...  10.1 us
    ppermute x5, waiting for transfers between devices, psum_step(): return values + lax.ppermute(values, AXES, pairs)  8.98 us
    reduce_sum x1, other arithmetic, local(): jnp.sum(row_weights[:, None] * jnp.square(grad_rows.astype(jnp.float32)),...  3.38 us
    dot_general x2, matrix products, exchange_and_score(): jnp.einsum('rk,qk->rq', grad_rows[:, start:start + size], prepared, prefe...  3.28 us
    ppermute x5, starting transfers between devices, psum_step(): return values + lax.ppermute(values, AXES, pairs)  3.1 us
    mul x1, other arithmetic, local(): weight_scale = row_weights * inv_root  1.28 us
  transfers between devices with their start and end apart: 13, of which 5 were waited for; matrix products, arithmetic and copies ran while one was open for 18% of the time, Pallas kernels for 0%

profile of v10, /device:TPU:0, one launch (start us, length us, event | category | flops | bytes accessed | tf_op | source)
XLA Modules:
  0.0 49.3 jit_solution(535706852227280916)
XLA Ops:
  0.0 3.0 %collective-permute-start = (bf16[4,8192]{1,0:T(4,128)(2,1)}, bf16[4,8192]{1,0:T(4,128)(2,1)S(1)}, u32[]{:S(2)}, u32[]{:S(2)}) collective-permute-start(bf16[4,8192]{1,0:T(4,128)(2,1)} %param.10), channel_id=1, source_target_pairs={{0,8},{1,9},{2,10},{3,11},{4,12},{5,13},{6,14},{7,15},{8,16},{9,17... | collective-permute-start | bytes 196616 | tf_op jit(solution)/shard_map/ppermute | solution.py:48
  3.0 2.6 %collective-permute-start.1 = (bf16[4,8192]{1,0:T(4,128)(2,1)}, bf16[4,8192]{1,0:T(4,128)(2,1)S(1)}, u32[]{:S(2)}, u32[]{:S(2)}) collective-permute-start(bf16[4,8192]{1,0:T(4,128)(2,1)} %param.10), channel_id=1, source_target_pairs={{0,16},{1,17},{2,18},{3,19},{4,20},{5,21},{6,22},{7,23},{8,24},{9,... | collective-permute-start | bytes 196616 | tf_op jit(solution)/shard_map/ppermute | solution.py:48
  5.6 1.3 %collective-permute-start.2 = (bf16[4,8192]{1,0:T(4,128)(2,1)}, bf16[4,8192]{1,0:T(4,128)(2,1)S(1)}, u32[]{:S(2)}, u32[]{:S(2)}) collective-permute-start(bf16[4,8192]{1,0:T(4,128)(2,1)} %param.10), channel_id=1, source_target_pairs={{0,24},{1,25},{2,26},{3,27},{4,28},{5,29},{6,30},{7,31},{8,0},{9,1... | collective-permute-start | bytes 196616 | tf_op jit(solution)/shard_map/ppermute | solution.py:48
  7.0 1.3 %broadcast_multiply_fusion = (f32[256]{0:T(256)S(1)}, f32[]{:T(128)}) fusion(f32[256]{0:T(256)} %param.8), kind=kLoop, calls=%fused_computation.56 | loop fusion | flops 511 | bytes 2052 | tf_op jit(solution)/shard_map/mul | solution.py:173
  8.2 3.4 %multiply_reduce_fusion = f32[8192]{0:T(1024)S(1)} fusion(bf16[256,8192]{1,0:T(8,128)(2,1)} %param.7, f32[256]{0:T(256)} %param.8), kind=kLoop, calls=%fused_computation.1 | loop fusion | flops 8380416 | bytes 4228096 | tf_op jit(solution)/shard_map/reduce_sum | solution.py:162
  11.8 0.7 %select_maximum_fusion = f32[8320]{0:T(1024)S(1)} fusion(f32[1]{0:T(128)} %bitcast.4, f32[8192]{0:T(1024)S(1)} %multiply_reduce_fusion), kind=kLoop, calls=%fused_computation.37 | loop fusion | flops 24960 | bytes 66052 | tf_op jit(solution)/shard_map/concatenate | solution.py:163
  12.9 0.7 %collective-permute-start.5 = (f32[8320]{0:T(1024)S(1)}, f32[8320]{0:T(1024)S(1)}, u32[]{:S(2)}, u32[]{:S(2)}) collective-permute-start(f32[8320]{0:T(1024)S(1)} %select_maximum_fusion), channel_id=1, source_target_pairs={{0,8},{1,9},{2,10},{3,11},{4,12},{5,13},{6,14},{7,15},{8,0},{9,1},... | collective-permute-start | bytes 99848 | tf_op jit(solution)/shard_map/ppermute | solution.py:79
  13.6 1.6 %collective-permute-start.4 = (bf16[16,4096]{1,0:T(8,128)(2,1)S(1)}, bf16[16,4096]{1,0:T(8,128)(2,1)S(1)}, u32[]{:S(2)}, u32[]{:S(2)}) collective-permute-start(bf16[16,4096]{1,0:T(8,128)(2,1)S(1)} %get-tuple-element.37), channel_id=1, source_target_pairs={{0,2},{1,3},{2,0},{3,1},{4,6},{5,7},{6,4},{7,5},{8,10},{9,11},{10,... | collective-permute-start | bytes 393224 | tf_op jit(solution)/shard_map/ppermute | solution.py:48
  15.2 1.5 %collective-permute-start.3 = (bf16[16,4096]{1,0:T(8,128)(2,1)S(1)}, bf16[16,4096]{1,0:T(8,128)(2,1)S(1)}, u32[]{:S(2)}, u32[]{:S(2)}) collective-permute-start(bf16[16,4096]{1,0:T(8,128)(2,1)S(1)} %get-tuple-element.38), channel_id=1, source_target_pairs={{0,4},{1,5},{2,6},{3,7},{4,0},{5,1},{6,2},{7,3},{8,12},{9,13},{10,... | collective-permute-start | bytes 393224 | tf_op jit(solution)/shard_map/ppermute | solution.py:48
  16.8 0.7 %gather_fusion = s32[256,8]{1,0:T(8,128)S(1)} fusion(s32[8,8]{1,0:T(8,128)S(1)} %bitcast.63, s32[1024]{0:T(1024)S(1)} %pad_clamp_fusion), kind=kCustom, calls=%fused_computation | custom fusion | bytes 17408 | tf_op jit(solution)/shard_map/jit(_take)/gather | solution.py:171
  17.6 0.6 %reduce-window.6 = s32[8,2,128]{2,0,1:T(8,128)S(1)} reduce-window(s32[8,2,128]{2,0,1:T(8,128)S(1)} %fusion.22, s32[]{:T(128)} %constant.191.clone.1), window={size=1x1x128 pad=0_0x0_0x127_0}, to_apply=%region_2.0 | reduce-window | flops 260096 | bytes 16388 | tf_op jit(solution)/shard_map/reduce-window
  18.7 0.8 %collective-permute-start.6 = (f32[8320]{0:T(1024)S(1)}, f32[8320]{0:T(1024)S(1)}, u32[]{:S(2)}, u32[]{:S(2)}) collective-permute-start(f32[8320]{0:T(1024)S(1)} %add.147), channel_id=1, source_target_pairs={{0,16},{1,17},{2,18},{3,19},{4,20},{5,21},{6,22},{7,23},{8,24},{9,... | collective-permute-start | bytes 99848 | tf_op jit(solution)/shard_map/ppermute | solution.py:79
  19.4 4.2 %collective-permute-done.6 = f32[8320]{0:T(1024)S(1)} collective-permute-done((f32[8320]{0:T(1024)S(1)}, f32[8320]{0:T(1024)S(1)}, u32[]{:S(2)}, u32[]{:S(2)}) %collective-permute-start.6) | collective-permute-done | bytes 33312 | tf_op jit(solution)/shard_map/ppermute | solution.py:79
  24.2 0.6 %collective-permute-start.7 = (bf16[2,16,4096]{2,1,0:T(8,128)(2,1)S(1)}, bf16[2,16,4096]{2,1,0:T(8,128)(2,1)S(1)}, u32[]{:S(2)}, u32[]{:S(2)}) collective-permute-start(bf16[2,16,4096]{2,1,0:T(8,128)(2,1)S(1)} %bitcast_dynamic-update-slice_fusion.6), channel_id=1, source_target_pairs={{0,2},{1,3},{2,0},{3,1},{4,6},{5,7},{6,4},{7,5},{8,10},{9,11},{10,... | collective-permute-start | bytes 786440 | tf_op jit(solution)/shard_map/ppermute | solution.py:48
  25.0 1.5 %collective-permute-start.8 = (bf16[2,16,4096]{2,1,0:T(8,128)(2,1)S(1)}, bf16[2,16,4096]{2,1,0:T(8,128)(2,1)S(1)}, u32[]{:S(2)}, u32[]{:S(2)}) collective-permute-start(bf16[2,16,4096]{2,1,0:T(8,128)(2,1)S(1)} %bitcast_dynamic-update-slice_fusion.4), channel_id=1, source_target_pairs={{0,4},{1,5},{2,6},{3,7},{4,0},{5,1},{6,2},{7,3},{8,12},{9,13},{10,... | collective-permute-start | bytes 786440 | tf_op jit(solution)/shard_map/ppermute | solution.py:48
  26.4 1.3 %collective-permute-done.9 = f32[8320]{0:T(1024)S(1)} collective-permute-done((f32[8320]{0:T(1024)S(1)}, f32[8320]{0:T(1024)S(1)}, u32[]{:S(2)}, u32[]{:S(2)}) %collective-permute-start.9) | collective-permute-done | bytes 33312 | tf_op jit(solution)/shard_map/ppermute | solution.py:79
  27.7 1.0 %collective-permute-start.10 = (f32[8320]{0:T(1024)S(1)}, f32[8320]{0:T(1024)S(1)}, u32[]{:S(2)}, u32[]{:S(2)}) collective-permute-start(f32[8320]{0:T(1024)S(1)} %add.149), channel_id=1, source_target_pairs={{0,2},{1,3},{2,0},{3,1},{4,6},{5,7},{6,4},{7,5},{8,10},{9,11},{10,... | collective-permute-start | bytes 99848 | tf_op jit(solution)/shard_map/ppermute | solution.py:79
  28.7 2.9 %collective-permute-done.10 = f32[8320]{0:T(1024)S(1)} collective-permute-done((f32[8320]{0:T(1024)S(1)}, f32[8320]{0:T(1024)S(1)}, u32[]{:S(2)}, u32[]{:S(2)}) %collective-permute-start.10) | collective-permute-done | bytes 33312 | tf_op jit(solution)/shard_map/ppermute | solution.py:79
  32.5 0.6 %collective-permute-done.12 = f32[8320]{0:T(1024)S(1)} collective-permute-done((f32[8320]{0:T(1024)S(1)}, f32[8320]{0:T(1024)S(1)}, u32[]{:S(2)}, u32[]{:S(2)}) %collective-permute-start.12) | collective-permute-done | bytes 33312 | tf_op jit(solution)/shard_map/ppermute | solution.py:79
  33.6 0.7 %fusion.19 = f32[8192]{0:T(1024)S(1)} fusion(f32[8320]{0:T(1024)S(1)} %add.151, f32[]{:T(128)} %bitcast.19), kind=kLoop, calls=%fused_computation.41 | loop fusion | flops 16384 | bytes 65540 | tf_op jit(solution)/shard_map/rsqrt | solution.py:168
  34.8 0.9 %fusion.4 = f32[256,128]{0,1:T(8,128)S(1)} fusion(bf16[256,8192]{1,0:T(8,128)(2,1)S(1)} %copy-done, bf16[128,8192]{1,0:T(8,128)(2,1)S(1)} %constant_dynamic-update-slice_fusion, f32[4096]{0:T(1024)S(1)} %get-tuple-element.39), kind=kOutput, calls=%fused_computation.9 | convolution fusion | flops 270008320 | bytes 3293184 | tf_op jit(solution)/shard_map/rk,qk->rq/dot_general | solution.py:120
  35.7 2.4 %fusion.7 = f32[256,128]{0,1:T(8,128)S(1)} fusion(bf16[256,8192]{1,0:T(8,128)(2,1)} %param.7, bf16[128,8192]{1,0:T(8,128)(2,1)S(1)} %constant_dynamic-update-slice_fusion, f32[4096]{0:T(1024)S(1)} %get-tuple-element.40), kind=kOutput, calls=%fused_computation.10 | convolution fusion | flops 270008320 | bytes 3293184 | tf_op jit(solution)/shard_map/rk,qk->rq/dot_general | solution.py:120
  38.6 10.1 %all_to_all.5 = bf16[8,48,128]{2,1,0:T(8,128)(2,1)S(1)} all-to-all(bf16[8,48,128]{2,1,0:T(8,128)(2,1)S(1)} %bitcast.67), channel_id=1, replica_groups=mesh['blk'=8,'harvest'=4] {'blk'}, dimensions={0} | all-to-all | bytes 196608 | tf_op jit(solution)/shard_map/all_to_all | solution.py:183
  48.7 0.6 %copy.32 = bf16[384,128]{1,0:T(8,128)(2,1)} copy(bf16[384,128]{1,0:T(8,128)(2,1)S(1)} %bitcast.66) | data formatting | bytes 196608
  (68 shorter events, 3.9 us)
Async XLA Ops:
  0.0 12.6 %collective-permute-start = (bf16[4,8192]{1,0:T(4,128)(2,1)}, bf16[4,8192]{1,0:T(4,128)(2,1)S(1)}, u32[]{:S(2)}, u32[]{:S(2)}) collective-permute-start(bf16[4,8192]{1,0:T(4,128)(2,1)} %param.10), channel_id=1, source_target_pairs={{0,8},{1,9},{2,10},{3,11},{4,12},{5,13},{6,14},{7,15},{8,16},{9,17... | collective-permute-start | bytes 196616 | tf_op jit(solution)/shard_map/ppermute | solution.py:48
  3.0 9.7 %collective-permute-start.1 = (bf16[4,8192]{1,0:T(4,128)(2,1)}, bf16[4,8192]{1,0:T(4,128)(2,1)S(1)}, u32[]{:S(2)}, u32[]{:S(2)}) collective-permute-start(bf16[4,8192]{1,0:T(4,128)(2,1)} %param.10), channel_id=1, source_target_pairs={{0,16},{1,17},{2,18},{3,19},{4,20},{5,21},{6,22},{7,23},{8,24},{9,... | collective-permute-start | bytes 196616 | tf_op jit(solution)/shard_map/ppermute | solution.py:48
  5.6 7.1 %collective-permute-start.2 = (bf16[4,8192]{1,0:T(4,128)(2,1)}, bf16[4,8192]{1,0:T(4,128)(2,1)S(1)}, u32[]{:S(2)}, u32[]{:S(2)}) collective-permute-start(bf16[4,8192]{1,0:T(4,128)(2,1)} %param.10), channel_id=1, source_target_pairs={{0,24},{1,25},{2,26},{3,27},{4,28},{5,29},{6,30},{7,31},{8,0},{9,1... | collective-permute-start | bytes 196616 | tf_op jit(solution)/shard_map/ppermute | solution.py:48
  8.2 3.5 %copy-start.1 = (bf16[4,8192]{1,0:T(4,128)(2,1)S(1)}, bf16[4,8192]{1,0:T(4,128)(2,1)}, u32[]{:S(2)}) copy-start(bf16[4,8192]{1,0:T(4,128)(2,1)} %param.10) | copy-start | bytes 196612
  11.6 5.1 %copy-start.2 = (s32[256,1]{0,1:T(1,128)S(1)}, s32[256,1]{0,1:T(1,128)}, u32[]{:S(2)}) copy-start(s32[256,1]{0,1:T(1,128)} %param.9) | copy-start | bytes 3076
  11.6 5.1 %copy-start.3 = (s32[8,8]{1,0:T(8,128)S(1)}, s32[8,8]{1,0:T(8,128)}, u32[]{:S(2)}) copy-start(s32[8,8]{1,0:T(8,128)} %param.11) | copy-start | bytes 772
  12.9 5.8 %collective-permute-start.5 = (f32[8320]{0:T(1024)S(1)}, f32[8320]{0:T(1024)S(1)}, u32[]{:S(2)}, u32[]{:S(2)}) collective-permute-start(f32[8320]{0:T(1024)S(1)} %select_maximum_fusion), channel_id=1, source_target_pairs={{0,8},{1,9},{2,10},{3,11},{4,12},{5,13},{6,14},{7,15},{8,0},{9,1},... | collective-permute-start | bytes 99848 | tf_op jit(solution)/shard_map/ppermute | solution.py:79
  13.6 10.0 %collective-permute-start.4 = (bf16[16,4096]{1,0:T(8,128)(2,1)S(1)}, bf16[16,4096]{1,0:T(8,128)(2,1)S(1)}, u32[]{:S(2)}, u32[]{:S(2)}) collective-permute-start(bf16[16,4096]{1,0:T(8,128)(2,1)S(1)} %get-tuple-element.37), channel_id=1, source_target_pairs={{0,2},{1,3},{2,0},{3,1},{4,6},{5,7},{6,4},{7,5},{8,10},{9,11},{10,... | collective-permute-start | bytes 393224 | tf_op jit(solution)/shard_map/ppermute | solution.py:48
  15.2 8.5 %collective-permute-start.3 = (bf16[16,4096]{1,0:T(8,128)(2,1)S(1)}, bf16[16,4096]{1,0:T(8,128)(2,1)S(1)}, u32[]{:S(2)}, u32[]{:S(2)}) collective-permute-start(bf16[16,4096]{1,0:T(8,128)(2,1)S(1)} %get-tuple-element.38), channel_id=1, source_target_pairs={{0,4},{1,5},{2,6},{3,7},{4,0},{5,1},{6,2},{7,3},{8,12},{9,13},{10,... | collective-permute-start | bytes 393224 | tf_op jit(solution)/shard_map/ppermute | solution.py:48
  18.7 4.9 %collective-permute-start.6 = (f32[8320]{0:T(1024)S(1)}, f32[8320]{0:T(1024)S(1)}, u32[]{:S(2)}, u32[]{:S(2)}) collective-permute-start(f32[8320]{0:T(1024)S(1)} %add.147), channel_id=1, source_target_pairs={{0,16},{1,17},{2,18},{3,19},{4,20},{5,21},{6,22},{7,23},{8,24},{9,... | collective-permute-start | bytes 99848 | tf_op jit(solution)/shard_map/ppermute | solution.py:79
  23.7 4.0 %collective-permute-start.9 = (f32[8320]{0:T(1024)S(1)}, f32[8320]{0:T(1024)S(1)}, u32[]{:S(2)}, u32[]{:S(2)}) collective-permute-start(f32[8320]{0:T(1024)S(1)} %add.148), channel_id=1, source_target_pairs={{0,4},{1,5},{2,6},{3,7},{4,0},{5,1},{6,2},{7,3},{8,12},{9,13},{10,... | collective-permute-start | bytes 99848 | tf_op jit(solution)/shard_map/ppermute | solution.py:79
  24.2 7.4 %collective-permute-start.7 = (bf16[2,16,4096]{2,1,0:T(8,128)(2,1)S(1)}, bf16[2,16,4096]{2,1,0:T(8,128)(2,1)S(1)}, u32[]{:S(2)}, u32[]{:S(2)}) collective-permute-start(bf16[2,16,4096]{2,1,0:T(8,128)(2,1)S(1)} %bitcast_dynamic-update-slice_fusion.6), channel_id=1, source_target_pairs={{0,2},{1,3},{2,0},{3,1},{4,6},{5,7},{6,4},{7,5},{8,10},{9,11},{10,... | collective-permute-start | bytes 786440 | tf_op jit(solution)/shard_map/ppermute | solution.py:48
  25.0 6.7 %collective-permute-start.8 = (bf16[2,16,4096]{2,1,0:T(8,128)(2,1)S(1)}, bf16[2,16,4096]{2,1,0:T(8,128)(2,1)S(1)}, u32[]{:S(2)}, u32[]{:S(2)}) collective-permute-start(bf16[2,16,4096]{2,1,0:T(8,128)(2,1)S(1)} %bitcast_dynamic-update-slice_fusion.4), channel_id=1, source_target_pairs={{0,4},{1,5},{2,6},{3,7},{4,0},{5,1},{6,2},{7,3},{8,12},{9,13},{10,... | collective-permute-start | bytes 786440 | tf_op jit(solution)/shard_map/ppermute | solution.py:48
  27.7 4.0 %collective-permute-start.10 = (f32[8320]{0:T(1024)S(1)}, f32[8320]{0:T(1024)S(1)}, u32[]{:S(2)}, u32[]{:S(2)}) collective-permute-start(f32[8320]{0:T(1024)S(1)} %add.149), channel_id=1, source_target_pairs={{0,2},{1,3},{2,0},{3,1},{4,6},{5,7},{6,4},{7,5},{8,10},{9,11},{10,... | collective-permute-start | bytes 99848 | tf_op jit(solution)/shard_map/ppermute | solution.py:79
  31.8 2.9 %copy-start = (bf16[256,8192]{1,0:T(8,128)(2,1)S(1)}, bf16[256,8192]{1,0:T(8,128)(2,1)}, u32[]{:S(2)}) copy-start(bf16[256,8192]{1,0:T(8,128)(2,1)} %param.7) | copy-start | bytes 12582916
  31.8 1.3 %collective-permute-start.12 = (f32[8320]{0:T(1024)S(1)}, f32[8320]{0:T(1024)S(1)}, u32[]{:S(2)}, u32[]{:S(2)}) collective-permute-start(f32[8320]{0:T(1024)S(1)} %add.150), channel_id=1, source_target_pairs={{0,1},{1,0},{2,3},{3,2},{4,5},{5,4},{6,7},{7,6},{8,9},{9,8},{10,11... | collective-permute-start | bytes 99848 | tf_op jit(solution)/shard_map/ppermute | solution.py:79
  31.9 2.8 %collective-permute-start.11 = (bf16[64,8192]{1,0:T(8,128)(2,1)S(1)}, bf16[64,8192]{1,0:T(8,128)(2,1)S(1)}, u32[]{:S(2)}, u32[]{:S(2)}) collective-permute-start(bf16[64,8192]{1,0:T(8,128)(2,1)S(1)} %pad_maximum_fusion), channel_id=1, source_target_pairs={{0,1},{1,0},{2,3},{3,2},{4,5},{5,4},{6,7},{7,6},{8,9},{9,8},{10,11... | collective-permute-start | bytes 3145736 | tf_op jit(solution)/shard_map/ppermute | solution.py:114

commit v11 on v10

--- a/solution.py
+++ b/solution.py
@@ -162,7 +162,9 @@
     squares = jnp.sum(row_weights[:, None] * jnp.square(grad_rows.astype(jnp.float32)), axis=0)
     packed = jnp.concatenate([squares, jnp.zeros((128,), jnp.float32).at[0].set(jnp.sum(row_weights))])
     first = gather_rows(queries, factors[0], device_count)
-    first, packed, destinations, tile_pattern = lax.optimization_barrier((first, packed, destinations, tile_pattern))
+    first, packed, destinations, tile_pattern, late_weights = lax.optimization_barrier(
+        (first, packed, destinations, tile_pattern, row_weights)
+    )
     joined, packed, splits, orders = gather_streams(first, packed, psum_steps(factors), factors, device_count)
     total_sq, total_weight = packed[:width], packed[width]
     scaling = lax.rsqrt(total_sq / total_weight + 1e-06)
@@ -170,7 +172,7 @@
     owner_ids = destinations[:, 0]
     pattern_rows = jnp.take(tile_pattern.T, owner_ids, axis=0).astype(jnp.float32)
     full_mask = jnp.repeat(pattern_rows, block_size, axis=1)
-    weight_scale = row_weights * inv_root
+    weight_scale = late_weights * inv_root
     value = (raw * weight_scale[:, None] * full_mask).astype(jnp.bfloat16)
 
     one_hot = (owner_ids[:, None] == jnp.arange(blk_count, dtype=jnp.int32)[None, :]).astype(jnp.int32)

time: 49.6 us -> 48.9 us (0.986)
  waiting for transfers between devices: 9.38 us -> 8.67 us
  starting transfers between devices: 15.8 us -> 16.5 us
  other arithmetic: 6.94 us -> 6.26 us
    mul x1, other arithmetic: 1.28 us -> 0.01 us  [local(): weight_scale = late_weights * inv_root]
    ppermute x5, starting transfers between devices: 3.1 us -> 3.82 us  [psum_step(): return values + lax.ppermute(values, AXES, pairs)]
    ppermute x5, waiting for transfers between devices: 8.98 us -> 8.27 us  [psum_step(): return values + lax.ppermute(values, AXES, pairs)]
    reduce_sum x0 -> x1, other arithmetic: none -> 0.6 us  [local(): jnp.sum(row_weights)]
  transfers between devices with their start and end apart: 13 -> 13, of which waited for: 5 -> 5; matrix products, arithmetic and copies ran while one was open for 18% -> 17% of each run, Pallas kernels for 0% -> 0%
where the time goes in v11:
time: 48.9 us; the launch traced here: 48.7 us
  starting transfers between devices  16.5 us (34%)
  blocking collectives  10.1 us (21%)
  waiting for transfers between devices  8.67 us (18%)
  other arithmetic  6.26 us (13%)
  matrix products  3.49 us (7%)
  local copies, waits for them, and re-layouts  3.13 us (6%)
  between operations  0.55 us (1%)
    ppermute x7, starting transfers between devices, gather_factor(): received = lax.ppermute(piece, AXES, shifted(factor, shift, device_count))  12.2 us
    all_to_all x1, blocking collectives, local(): lax.all_to_all(bucket.reshape(blk_count, capacity, query_count), 'blk', s...  10.1 us
    ppermute x5, waiting for transfers between devices, psum_step(): return values + lax.ppermute(values, AXES, pairs)  8.27 us
    ppermute x5, starting transfers between devices, psum_step(): return values + lax.ppermute(values, AXES, pairs)  3.82 us
    reduce_sum x1, other arithmetic, local(): jnp.sum(row_weights[:, None] * jnp.square(grad_rows.astype(jnp.float32)),...  3.38 us
    dot_general x2, matrix products, exchange_and_score(): jnp.einsum('rk,qk->rq', grad_rows[:, start:start + size], prepared, prefe...  3.28 us
  transfers between devices with their start and end apart: 13, of which 5 were waited for; matrix products, arithmetic and copies ran while one was open for 17% of the time, Pallas kernels for 0%

profile of v11, /device:TPU:0, one launch (start us, length us, event | category | flops | bytes accessed | tf_op | source)
XLA Modules:
  0.0 48.7 jit_solution(10938876709745023862)
XLA Ops:
  0.0 3.0 %collective-permute-start = (bf16[4,8192]{1,0:T(4,128)(2,1)}, bf16[4,8192]{1,0:T(4,128)(2,1)S(1)}, u32[]{:S(2)}, u32[]{:S(2)}) collective-permute-start(bf16[4,8192]{1,0:T(4,128)(2,1)} %param.10), channel_id=1, source_target_pairs={{0,8},{1,9},{2,10},{3,11},{4,12},{5,13},{6,14},{7,15},{8,16},{9,17... | collective-permute-start | bytes 196616 | tf_op jit(solution)/shard_map/ppermute | solution.py:48
  3.0 2.6 %collective-permute-start.1 = (bf16[4,8192]{1,0:T(4,128)(2,1)}, bf16[4,8192]{1,0:T(4,128)(2,1)S(1)}, u32[]{:S(2)}, u32[]{:S(2)}) collective-permute-start(bf16[4,8192]{1,0:T(4,128)(2,1)} %param.10), channel_id=1, source_target_pairs={{0,16},{1,17},{2,18},{3,19},{4,20},{5,21},{6,22},{7,23},{8,24},{9,... | collective-permute-start | bytes 196616 | tf_op jit(solution)/shard_map/ppermute | solution.py:48
  5.6 1.3 %collective-permute-start.2 = (bf16[4,8192]{1,0:T(4,128)(2,1)}, bf16[4,8192]{1,0:T(4,128)(2,1)S(1)}, u32[]{:S(2)}, u32[]{:S(2)}) collective-permute-start(bf16[4,8192]{1,0:T(4,128)(2,1)} %param.10), channel_id=1, source_target_pairs={{0,24},{1,25},{2,26},{3,27},{4,28},{5,29},{6,30},{7,31},{8,0},{9,1... | collective-permute-start | bytes 196616 | tf_op jit(solution)/shard_map/ppermute | solution.py:48
  7.0 3.4 %multiply_reduce_fusion = f32[8192]{0:T(1024)S(1)} fusion(bf16[256,8192]{1,0:T(8,128)(2,1)} %param.7, f32[256]{0:T(256)} %param.8), kind=kLoop, calls=%fused_computation.1 | loop fusion | flops 8380416 | bytes 4228096 | tf_op jit(solution)/shard_map/reduce_sum | solution.py:162
  10.4 0.6 %reduce_sum.28 = f32[]{:T(128)} reduce(f32[256]{0:T(256)S(1)} %copy-done.3, f32[]{:T(128)} %constant.197.clone.1), dimensions={0}, to_apply=%region_1.0 | reduce | flops 255 | bytes 1032 | tf_op jit(solution)/shard_map/reduce_sum | solution.py:163
  11.1 0.7 %select_maximum_fusion = f32[8320]{0:T(1024)S(1)} fusion(f32[1]{0:T(128)} %bitcast.4, f32[8192]{0:T(1024)S(1)} %multiply_reduce_fusion), kind=kLoop, calls=%fused_computation.37 | loop fusion | flops 24960 | bytes 66052 | tf_op jit(solution)/shard_map/concatenate | solution.py:163
  12.2 0.7 %collective-permute-start.5 = (f32[8320]{0:T(1024)S(1)}, f32[8320]{0:T(1024)S(1)}, u32[]{:S(2)}, u32[]{:S(2)}) collective-permute-start(f32[8320]{0:T(1024)S(1)} %select_maximum_fusion), channel_id=1, source_target_pairs={{0,8},{1,9},{2,10},{3,11},{4,12},{5,13},{6,14},{7,15},{8,0},{9,1},... | collective-permute-start | bytes 99848 | tf_op jit(solution)/shard_map/ppermute | solution.py:79
  12.9 1.6 %collective-permute-start.4 = (bf16[16,4096]{1,0:T(8,128)(2,1)S(1)}, bf16[16,4096]{1,0:T(8,128)(2,1)S(1)}, u32[]{:S(2)}, u32[]{:S(2)}) collective-permute-start(bf16[16,4096]{1,0:T(8,128)(2,1)S(1)} %get-tuple-element.39), channel_id=1, source_target_pairs={{0,2},{1,3},{2,0},{3,1},{4,6},{5,7},{6,4},{7,5},{8,10},{9,11},{10,... | collective-permute-start | bytes 393224 | tf_op jit(solution)/shard_map/ppermute | solution.py:48
  14.5 1.5 %collective-permute-start.3 = (bf16[16,4096]{1,0:T(8,128)(2,1)S(1)}, bf16[16,4096]{1,0:T(8,128)(2,1)S(1)}, u32[]{:S(2)}, u32[]{:S(2)}) collective-permute-start(bf16[16,4096]{1,0:T(8,128)(2,1)S(1)} %get-tuple-element.40), channel_id=1, source_target_pairs={{0,4},{1,5},{2,6},{3,7},{4,0},{5,1},{6,2},{7,3},{8,12},{9,13},{10,... | collective-permute-start | bytes 393224 | tf_op jit(solution)/shard_map/ppermute | solution.py:48
  16.1 0.7 %gather_fusion = s32[256,8]{1,0:T(8,128)S(1)} fusion(s32[8,8]{1,0:T(8,128)S(1)} %bitcast.63, s32[1024]{0:T(1024)S(1)} %pad_clamp_fusion), kind=kCustom, calls=%fused_computation | custom fusion | bytes 17408 | tf_op jit(solution)/shard_map/jit(_take)/gather | solution.py:173
  16.9 0.6 %reduce-window.6 = s32[8,2,128]{2,0,1:T(8,128)S(1)} reduce-window(s32[8,2,128]{2,0,1:T(8,128)S(1)} %fusion.22, s32[]{:T(128)} %constant.191.clone.1), window={size=1x1x128 pad=0_0x0_0x127_0}, to_apply=%region_2.0 | reduce-window | flops 260096 | bytes 16388 | tf_op jit(solution)/shard_map/reduce-window
  18.0 1.4 %collective-permute-start.6 = (f32[8320]{0:T(1024)S(1)}, f32[8320]{0:T(1024)S(1)}, u32[]{:S(2)}, u32[]{:S(2)}) collective-permute-start(f32[8320]{0:T(1024)S(1)} %add.147), channel_id=1, source_target_pairs={{0,16},{1,17},{2,18},{3,19},{4,20},{5,21},{6,22},{7,23},{8,24},{9,... | collective-permute-start | bytes 99848 | tf_op jit(solution)/shard_map/ppermute | solution.py:79
  19.5 3.5 %collective-permute-done.6 = f32[8320]{0:T(1024)S(1)} collective-permute-done((f32[8320]{0:T(1024)S(1)}, f32[8320]{0:T(1024)S(1)}, u32[]{:S(2)}, u32[]{:S(2)}) %collective-permute-start.6) | collective-permute-done | bytes 33312 | tf_op jit(solution)/shard_map/ppermute | solution.py:79
  23.6 0.6 %collective-permute-start.7 = (bf16[2,16,4096]{2,1,0:T(8,128)(2,1)S(1)}, bf16[2,16,4096]{2,1,0:T(8,128)(2,1)S(1)}, u32[]{:S(2)}, u32[]{:S(2)}) collective-permute-start(bf16[2,16,4096]{2,1,0:T(8,128)(2,1)S(1)} %bitcast_dynamic-update-slice_fusion.6), channel_id=1, source_target_pairs={{0,2},{1,3},{2,0},{3,1},{4,6},{5,7},{6,4},{7,5},{8,10},{9,11},{10,... | collective-permute-start | bytes 786440 | tf_op jit(solution)/shard_map/ppermute | solution.py:48
  24.3 1.5 %collective-permute-start.8 = (bf16[2,16,4096]{2,1,0:T(8,128)(2,1)S(1)}, bf16[2,16,4096]{2,1,0:T(8,128)(2,1)S(1)}, u32[]{:S(2)}, u32[]{:S(2)}) collective-permute-start(bf16[2,16,4096]{2,1,0:T(8,128)(2,1)S(1)} %bitcast_dynamic-update-slice_fusion.4), channel_id=1, source_target_pairs={{0,4},{1,5},{2,6},{3,7},{4,0},{5,1},{6,2},{7,3},{8,12},{9,13},{10,... | collective-permute-start | bytes 786440 | tf_op jit(solution)/shard_map/ppermute | solution.py:48
  25.8 1.3 %collective-permute-done.9 = f32[8320]{0:T(1024)S(1)} collective-permute-done((f32[8320]{0:T(1024)S(1)}, f32[8320]{0:T(1024)S(1)}, u32[]{:S(2)}, u32[]{:S(2)}) %collective-permute-start.9) | collective-permute-done | bytes 33312 | tf_op jit(solution)/shard_map/ppermute | solution.py:79
  27.0 1.0 %collective-permute-start.10 = (f32[8320]{0:T(1024)S(1)}, f32[8320]{0:T(1024)S(1)}, u32[]{:S(2)}, u32[]{:S(2)}) collective-permute-start(f32[8320]{0:T(1024)S(1)} %add.149), channel_id=1, source_target_pairs={{0,2},{1,3},{2,0},{3,1},{4,6},{5,7},{6,4},{7,5},{8,10},{9,11},{10,... | collective-permute-start | bytes 99848 | tf_op jit(solution)/shard_map/ppermute | solution.py:79
  28.1 2.9 %collective-permute-done.10 = f32[8320]{0:T(1024)S(1)} collective-permute-done((f32[8320]{0:T(1024)S(1)}, f32[8320]{0:T(1024)S(1)}, u32[]{:S(2)}, u32[]{:S(2)}) %collective-permute-start.10) | collective-permute-done | bytes 33312 | tf_op jit(solution)/shard_map/ppermute | solution.py:79
  31.8 0.6 %collective-permute-done.12 = f32[8320]{0:T(1024)S(1)} collective-permute-done((f32[8320]{0:T(1024)S(1)}, f32[8320]{0:T(1024)S(1)}, u32[]{:S(2)}, u32[]{:S(2)}) %collective-permute-start.12) | collective-permute-done | bytes 33312 | tf_op jit(solution)/shard_map/ppermute | solution.py:79
  33.0 0.7 %fusion.19 = f32[8192]{0:T(1024)S(1)} fusion(f32[8320]{0:T(1024)S(1)} %add.151, f32[]{:T(128)} %bitcast.19), kind=kLoop, calls=%fused_computation.41 | loop fusion | flops 16384 | bytes 65540 | tf_op jit(solution)/shard_map/rsqrt | solution.py:170
  34.1 0.8 %fusion.4 = f32[256,128]{0,1:T(8,128)S(1)} fusion(bf16[256,8192]{1,0:T(8,128)(2,1)S(1)} %copy-done, bf16[128,8192]{1,0:T(8,128)(2,1)S(1)} %constant_dynamic-update-slice_fusion, f32[4096]{0:T(1024)S(1)} %get-tuple-element.41), kind=kOutput, calls=%fused_computation.9 | convolution fusion | flops 270008320 | bytes 3293184 | tf_op jit(solution)/shard_map/rk,qk->rq/dot_general | solution.py:120
  35.0 2.4 %fusion.7 = f32[256,128]{0,1:T(8,128)S(1)} fusion(bf16[256,8192]{1,0:T(8,128)(2,1)} %param.7, bf16[128,8192]{1,0:T(8,128)(2,1)S(1)} %constant_dynamic-update-slice_fusion, f32[4096]{0:T(1024)S(1)} %get-tuple-element.42), kind=kOutput, calls=%fused_computation.10 | convolution fusion | flops 270008320 | bytes 3293184 | tf_op jit(solution)/shard_map/rk,qk->rq/dot_general | solution.py:120
  37.9 10.1 %all_to_all.5 = bf16[8,48,128]{2,1,0:T(8,128)(2,1)S(1)} all-to-all(bf16[8,48,128]{2,1,0:T(8,128)(2,1)S(1)} %bitcast.67), channel_id=1, replica_groups=mesh['blk'=8,'harvest'=4] {'blk'}, dimensions={0} | all-to-all | bytes 196608 | tf_op jit(solution)/shard_map/all_to_all | solution.py:185
  48.0 0.6 %copy.32 = bf16[384,128]{1,0:T(8,128)(2,1)} copy(bf16[384,128]{1,0:T(8,128)(2,1)S(1)} %bitcast.66) | data formatting | bytes 196608
  (71 shorter events, 3.9 us)
Async XLA Ops:
  0.0 11.9 %collective-permute-start = (bf16[4,8192]{1,0:T(4,128)(2,1)}, bf16[4,8192]{1,0:T(4,128)(2,1)S(1)}, u32[]{:S(2)}, u32[]{:S(2)}) collective-permute-start(bf16[4,8192]{1,0:T(4,128)(2,1)} %param.10), channel_id=1, source_target_pairs={{0,8},{1,9},{2,10},{3,11},{4,12},{5,13},{6,14},{7,15},{8,16},{9,17... | collective-permute-start | bytes 196616 | tf_op jit(solution)/shard_map/ppermute | solution.py:48
  3.0 9.0 %collective-permute-start.1 = (bf16[4,8192]{1,0:T(4,128)(2,1)}, bf16[4,8192]{1,0:T(4,128)(2,1)S(1)}, u32[]{:S(2)}, u32[]{:S(2)}) collective-permute-start(bf16[4,8192]{1,0:T(4,128)(2,1)} %param.10), channel_id=1, source_target_pairs={{0,16},{1,17},{2,18},{3,19},{4,20},{5,21},{6,22},{7,23},{8,24},{9,... | collective-permute-start | bytes 196616 | tf_op jit(solution)/shard_map/ppermute | solution.py:48
  5.6 6.4 %collective-permute-start.2 = (bf16[4,8192]{1,0:T(4,128)(2,1)}, bf16[4,8192]{1,0:T(4,128)(2,1)S(1)}, u32[]{:S(2)}, u32[]{:S(2)}) collective-permute-start(bf16[4,8192]{1,0:T(4,128)(2,1)} %param.10), channel_id=1, source_target_pairs={{0,24},{1,25},{2,26},{3,27},{4,28},{5,29},{6,30},{7,31},{8,0},{9,1... | collective-permute-start | bytes 196616 | tf_op jit(solution)/shard_map/ppermute | solution.py:48
  7.0 3.4 %copy-start.3 = (f32[256]{0:T(256)S(1)}, f32[256]{0:T(256)}, u32[]{:S(2)}) copy-start(f32[256]{0:T(256)} %param.8) | copy-start | bytes 3076
  7.0 4.1 %copy-start.1 = (bf16[4,8192]{1,0:T(4,128)(2,1)S(1)}, bf16[4,8192]{1,0:T(4,128)(2,1)}, u32[]{:S(2)}) copy-start(bf16[4,8192]{1,0:T(4,128)(2,1)} %param.10) | copy-start | bytes 196612
  10.4 5.7 %copy-start.2 = (s32[256,1]{0,1:T(1,128)S(1)}, s32[256,1]{0,1:T(1,128)}, u32[]{:S(2)}) copy-start(s32[256,1]{0,1:T(1,128)} %param.9) | copy-start | bytes 3076
  10.4 5.7 %copy-start.4 = (s32[8,8]{1,0:T(8,128)S(1)}, s32[8,8]{1,0:T(8,128)}, u32[]{:S(2)}) copy-start(s32[8,8]{1,0:T(8,128)} %param.11) | copy-start | bytes 772
  12.2 5.8 %collective-permute-start.5 = (f32[8320]{0:T(1024)S(1)}, f32[8320]{0:T(1024)S(1)}, u32[]{:S(2)}, u32[]{:S(2)}) collective-permute-start(f32[8320]{0:T(1024)S(1)} %select_maximum_fusion), channel_id=1, source_target_pairs={{0,8},{1,9},{2,10},{3,11},{4,12},{5,13},{6,14},{7,15},{8,0},{9,1},... | collective-permute-start | bytes 99848 | tf_op jit(solution)/shard_map/ppermute | solution.py:79
  12.9 10.0 %collective-permute-start.4 = (bf16[16,4096]{1,0:T(8,128)(2,1)S(1)}, bf16[16,4096]{1,0:T(8,128)(2,1)S(1)}, u32[]{:S(2)}, u32[]{:S(2)}) collective-permute-start(bf16[16,4096]{1,0:T(8,128)(2,1)S(1)} %get-tuple-element.39), channel_id=1, source_target_pairs={{0,2},{1,3},{2,0},{3,1},{4,6},{5,7},{6,4},{7,5},{8,10},{9,11},{10,... | collective-permute-start | bytes 393224 | tf_op jit(solution)/shard_map/ppermute | solution.py:48
  14.5 8.5 %collective-permute-start.3 = (bf16[16,4096]{1,0:T(8,128)(2,1)S(1)}, bf16[16,4096]{1,0:T(8,128)(2,1)S(1)}, u32[]{:S(2)}, u32[]{:S(2)}) collective-permute-start(bf16[16,4096]{1,0:T(8,128)(2,1)S(1)} %get-tuple-element.40), channel_id=1, source_target_pairs={{0,4},{1,5},{2,6},{3,7},{4,0},{5,1},{6,2},{7,3},{8,12},{9,13},{10,... | collective-permute-start | bytes 393224 | tf_op jit(solution)/shard_map/ppermute | solution.py:48
  18.0 4.9 %collective-permute-start.6 = (f32[8320]{0:T(1024)S(1)}, f32[8320]{0:T(1024)S(1)}, u32[]{:S(2)}, u32[]{:S(2)}) collective-permute-start(f32[8320]{0:T(1024)S(1)} %add.147), channel_id=1, source_target_pairs={{0,16},{1,17},{2,18},{3,19},{4,20},{5,21},{6,22},{7,23},{8,24},{9,... | collective-permute-start | bytes 99848 | tf_op jit(solution)/shard_map/ppermute | solution.py:79
  23.0 4.0 %collective-permute-start.9 = (f32[8320]{0:T(1024)S(1)}, f32[8320]{0:T(1024)S(1)}, u32[]{:S(2)}, u32[]{:S(2)}) collective-permute-start(f32[8320]{0:T(1024)S(1)} %add.148), channel_id=1, source_target_pairs={{0,4},{1,5},{2,6},{3,7},{4,0},{5,1},{6,2},{7,3},{8,12},{9,13},{10,... | collective-permute-start | bytes 99848 | tf_op jit(solution)/shard_map/ppermute | solution.py:79
  23.6 7.4 %collective-permute-start.7 = (bf16[2,16,4096]{2,1,0:T(8,128)(2,1)S(1)}, bf16[2,16,4096]{2,1,0:T(8,128)(2,1)S(1)}, u32[]{:S(2)}, u32[]{:S(2)}) collective-permute-start(bf16[2,16,4096]{2,1,0:T(8,128)(2,1)S(1)} %bitcast_dynamic-update-slice_fusion.6), channel_id=1, source_target_pairs={{0,2},{1,3},{2,0},{3,1},{4,6},{5,7},{6,4},{7,5},{8,10},{9,11},{10,... | collective-permute-start | bytes 786440 | tf_op jit(solution)/shard_map/ppermute | solution.py:48
  24.3 6.8 %collective-permute-start.8 = (bf16[2,16,4096]{2,1,0:T(8,128)(2,1)S(1)}, bf16[2,16,4096]{2,1,0:T(8,128)(2,1)S(1)}, u32[]{:S(2)}, u32[]{:S(2)}) collective-permute-start(bf16[2,16,4096]{2,1,0:T(8,128)(2,1)S(1)} %bitcast_dynamic-update-slice_fusion.4), channel_id=1, source_target_pairs={{0,4},{1,5},{2,6},{3,7},{4,0},{5,1},{6,2},{7,3},{8,12},{9,13},{10,... | collective-permute-start | bytes 786440 | tf_op jit(solution)/shard_map/ppermute | solution.py:48
  27.0 4.0 %collective-permute-start.10 = (f32[8320]{0:T(1024)S(1)}, f32[8320]{0:T(1024)S(1)}, u32[]{:S(2)}, u32[]{:S(2)}) collective-permute-start(f32[8320]{0:T(1024)S(1)} %add.149), channel_id=1, source_target_pairs={{0,2},{1,3},{2,0},{3,1},{4,6},{5,7},{6,4},{7,5},{8,10},{9,11},{10,... | collective-permute-start | bytes 99848 | tf_op jit(solution)/shard_map/ppermute | solution.py:79
  31.2 2.9 %copy-start = (bf16[256,8192]{1,0:T(8,128)(2,1)S(1)}, bf16[256,8192]{1,0:T(8,128)(2,1)}, u32[]{:S(2)}) copy-start(bf16[256,8192]{1,0:T(8,128)(2,1)} %param.7) | copy-start | bytes 12582916
  31.2 1.3 %collective-permute-start.12 = (f32[8320]{0:T(1024)S(1)}, f32[8320]{0:T(1024)S(1)}, u32[]{:S(2)}, u32[]{:S(2)}) collective-permute-start(f32[8320]{0:T(1024)S(1)} %add.150), channel_id=1, source_target_pairs={{0,1},{1,0},{2,3},{3,2},{4,5},{5,4},{6,7},{7,6},{8,9},{9,8},{10,11... | collective-permute-start | bytes 99848 | tf_op jit(solution)/shard_map/ppermute | solution.py:79
  31.2 2.8 %collective-permute-start.11 = (bf16[64,8192]{1,0:T(8,128)(2,1)S(1)}, bf16[64,8192]{1,0:T(8,128)(2,1)S(1)}, u32[]{:S(2)}, u32[]{:S(2)}) collective-permute-start(bf16[64,8192]{1,0:T(8,128)(2,1)S(1)} %pad_maximum_fusion), channel_id=1, source_target_pairs={{0,1},{1,0},{2,3},{3,2},{4,5},{5,4},{6,7},{7,6},{8,9},{9,8},{10,11... | collective-permute-start | bytes 3145736 | tf_op jit(solution)/shard_map/ppermute | solution.py:114

commit v12 on v11

--- a/solution.py
+++ b/solution.py
@@ -170,14 +170,15 @@
     scaling = lax.rsqrt(total_sq / total_weight + 1e-06)
     raw = exchange_and_score(grad_rows, joined, scaling, splits, orders, factors, queries.shape[0], device_count)
     owner_ids = destinations[:, 0]
-    pattern_rows = jnp.take(tile_pattern.T, owner_ids, axis=0).astype(jnp.float32)
+    owner_hot = (owner_ids[:, None] == jnp.arange(blk_count, dtype=jnp.int32)[None, :]).astype(jnp.float32)
+    pattern_rows = jnp.dot(owner_hot, tile_pattern.T.astype(jnp.float32), precision=lax.Precision.HIGHEST)
     full_mask = jnp.repeat(pattern_rows, block_size, axis=1)
     weight_scale = late_weights * inv_root
     value = (raw * weight_scale[:, None] * full_mask).astype(jnp.bfloat16)
 
-    one_hot = (owner_ids[:, None] == jnp.arange(blk_count, dtype=jnp.int32)[None, :]).astype(jnp.int32)
-    before = jnp.cumsum(one_hot, axis=0) - one_hot
-    slot_rank = jnp.sum(before * one_hot, axis=1)
+    earlier = (jnp.arange(row_count)[None, :] < jnp.arange(row_count)[:, None]).astype(jnp.float32)
+    before = jnp.dot(earlier, owner_hot, precision=lax.Precision.HIGHEST)
+    slot_rank = jnp.sum(before * owner_hot, axis=1).astype(jnp.int32)
     slot_index = owner_ids * capacity + slot_rank
     placement = (jnp.arange(slot_total, dtype=jnp.int32)[:, None] == slot_index[None, :]).astype(jnp.bfloat16)
     bucket = jnp.dot(placement, value, preferred_element_type=jnp.float32).astype(jnp.bfloat16)

time: 48.9 us -> 48.5 us (level)
  local copies, waits for them, and re-layouts: 3.13 us -> 2.05 us
  starting transfers between devices: 16.5 us -> 17.5 us
  other arithmetic: 6.26 us -> 5.52 us
  waiting for transfers between devices: 8.67 us -> 9.18 us
    ppermute x5, starting transfers between devices: 3.82 us -> 4.94 us  [psum_step(): return values + lax.ppermute(values, AXES, pairs)]
    ppermute x7, waiting for transfers between devices: 0.02 us -> 1.15 us  [gather_factor(): received = lax.ppermute(piece, AXES, shifted(factor, shift, device_count))]
    gather x2 -> x0, local copies, waits for them, and re-layouts: 0.79 us -> none  [local(): jnp.take(tile_pattern.T, owner_ids, axis=0).astype(jnp.float32)]
    ppermute x5, waiting for transfers between devices: 8.27 us -> 7.65 us  [psum_step(): return values + lax.ppermute(values, AXES, pairs)]
    another operation x2 -> x0, other arithmetic: 0.61 us -> none
  transfers between devices with their start and end apart: 13 -> 13, of which waited for: 5 -> 6; matrix products, arithmetic and copies ran while one was open for 17% -> 14% of each run, Pallas kernels for 0% -> 0%
where the time goes in v12:
time: 48.5 us; the launch traced here: 48.4 us
  starting transfers between devices  17.5 us (36%)
  blocking collectives  9.71 us (20%)
  waiting for transfers between devices  9.18 us (19%)
  other arithmetic  5.52 us (11%)
  matrix products  3.81 us (8%)
  local copies, waits for them, and re-layouts  2.05 us (4%)
  between operations  0.54 us (1%)
    ppermute x7, starting transfers between devices, gather_factor(): received = lax.ppermute(piece, AXES, shifted(factor, shift, device_count))  12.1 us
    all_to_all x1, blocking collectives, local(): lax.all_to_all(bucket.reshape(blk_count, capacity, query_count), 'blk', s...  9.71 us
    ppermute x5, waiting for transfers between devices, psum_step(): return values + lax.ppermute(values, AXES, pairs)  7.65 us
    ppermute x5, starting transfers between devices, psum_step(): return values + lax.ppermute(values, AXES, pairs)  4.94 us
    reduce_sum x1, other arithmetic, local(): jnp.sum(row_weights[:, None] * jnp.square(grad_rows.astype(jnp.float32)),...  3.38 us
    dot_general x2, matrix products, exchange_and_score(): jnp.einsum('rk,qk->rq', grad_rows[:, start:start + size], prepared, prefe...  3.28 us
    ppermute x7, waiting for transfers between devices, gather_factor(): received = lax.ppermute(piece, AXES, shifted(factor, shift, device_count))  1.15 us
  transfers between devices with their start and end apart: 13, of which 6 were waited for; matrix products, arithmetic and copies ran while one was open for 14% of the time, Pallas kernels for 0%

profile of v12, /device:TPU:0, one launch (start us, length us, event | category | flops | bytes accessed | tf_op | source)
XLA Modules:
  0.0 48.4 jit_solution(1478602301535550278)
XLA Ops:
  0.0 3.0 %collective-permute-start = (bf16[4,8192]{1,0:T(4,128)(2,1)}, bf16[4,8192]{1,0:T(4,128)(2,1)S(1)}, u32[]{:S(2)}, u32[]{:S(2)}) collective-permute-start(bf16[4,8192]{1,0:T(4,128)(2,1)} %param.10), channel_id=1, source_target_pairs={{0,8},{1,9},{2,10},{3,11},{4,12},{5,13},{6,14},{7,15},{8,16},{9,17... | collective-permute-start | bytes 196616 | tf_op jit(solution)/shard_map/ppermute | solution.py:48
  3.0 2.6 %collective-permute-start.1 = (bf16[4,8192]{1,0:T(4,128)(2,1)}, bf16[4,8192]{1,0:T(4,128)(2,1)S(1)}, u32[]{:S(2)}, u32[]{:S(2)}) collective-permute-start(bf16[4,8192]{1,0:T(4,128)(2,1)} %param.10), channel_id=1, source_target_pairs={{0,16},{1,17},{2,18},{3,19},{4,20},{5,21},{6,22},{7,23},{8,24},{9,... | collective-permute-start | bytes 196616 | tf_op jit(solution)/shard_map/ppermute | solution.py:48
  5.6 1.3 %collective-permute-start.2 = (bf16[4,8192]{1,0:T(4,128)(2,1)}, bf16[4,8192]{1,0:T(4,128)(2,1)S(1)}, u32[]{:S(2)}, u32[]{:S(2)}) collective-permute-start(bf16[4,8192]{1,0:T(4,128)(2,1)} %param.10), channel_id=1, source_target_pairs={{0,24},{1,25},{2,26},{3,27},{4,28},{5,29},{6,30},{7,31},{8,0},{9,1... | collective-permute-start | bytes 196616 | tf_op jit(solution)/shard_map/ppermute | solution.py:48
  7.0 3.4 %multiply_reduce_fusion = f32[8192]{0:T(1024)S(1)} fusion(bf16[256,8192]{1,0:T(8,128)(2,1)} %param.7, f32[256]{0:T(256)} %param.8), kind=kLoop, calls=%fused_computation | loop fusion | flops 8380416 | bytes 4228096 | tf_op jit(solution)/shard_map/reduce_sum | solution.py:162
  10.4 0.6 %reduce_sum.28 = f32[]{:T(128)} reduce(f32[256]{0:T(256)S(1)} %copy-done.2, f32[]{:T(128)} %constant.182.clone.1), dimensions={0}, to_apply=%region_1.0 | reduce | flops 255 | bytes 1032 | tf_op jit(solution)/shard_map/reduce_sum | solution.py:163
  11.1 0.7 %select_maximum_fusion = f32[8320]{0:T(1024)S(1)} fusion(f32[1]{0:T(128)} %bitcast.4, f32[8192]{0:T(1024)S(1)} %multiply_reduce_fusion), kind=kLoop, calls=%fused_computation.39 | loop fusion | flops 24960 | bytes 66052 | tf_op jit(solution)/shard_map/concatenate | solution.py:163
  12.2 0.7 %collective-permute-start.5 = (f32[8320]{0:T(1024)S(1)}, f32[8320]{0:T(1024)S(1)}, u32[]{:S(2)}, u32[]{:S(2)}) collective-permute-start(f32[8320]{0:T(1024)S(1)} %select_maximum_fusion), channel_id=1, source_target_pairs={{0,8},{1,9},{2,10},{3,11},{4,12},{5,13},{6,14},{7,15},{8,0},{9,1},... | collective-permute-start | bytes 99848 | tf_op jit(solution)/shard_map/ppermute | solution.py:79
  12.9 1.6 %collective-permute-start.4 = (bf16[16,4096]{1,0:T(8,128)(2,1)S(1)}, bf16[16,4096]{1,0:T(8,128)(2,1)S(1)}, u32[]{:S(2)}, u32[]{:S(2)}) collective-permute-start(bf16[16,4096]{1,0:T(8,128)(2,1)S(1)} %get-tuple-element.37), channel_id=1, source_target_pairs={{0,2},{1,3},{2,0},{3,1},{4,6},{5,7},{6,4},{7,5},{8,10},{9,11},{10,... | collective-permute-start | bytes 393224 | tf_op jit(solution)/shard_map/ppermute | solution.py:48
  14.5 1.5 %collective-permute-start.3 = (bf16[16,4096]{1,0:T(8,128)(2,1)S(1)}, bf16[16,4096]{1,0:T(8,128)(2,1)S(1)}, u32[]{:S(2)}, u32[]{:S(2)}) collective-permute-start(bf16[16,4096]{1,0:T(8,128)(2,1)S(1)} %get-tuple-element.38), channel_id=1, source_target_pairs={{0,4},{1,5},{2,6},{3,7},{4,0},{5,1},{6,2},{7,3},{8,12},{9,13},{10,... | collective-permute-start | bytes 393224 | tf_op jit(solution)/shard_map/ppermute | solution.py:48
  16.5 1.4 %collective-permute-start.6 = (f32[8320]{0:T(1024)S(1)}, f32[8320]{0:T(1024)S(1)}, u32[]{:S(2)}, u32[]{:S(2)}) collective-permute-start(f32[8320]{0:T(1024)S(1)} %add.137), channel_id=1, source_target_pairs={{0,16},{1,17},{2,18},{3,19},{4,20},{5,21},{6,22},{7,23},{8,24},{9,... | collective-permute-start | bytes 99848 | tf_op jit(solution)/shard_map/ppermute | solution.py:79
  17.9 3.5 %collective-permute-done.6 = f32[8320]{0:T(1024)S(1)} collective-permute-done((f32[8320]{0:T(1024)S(1)}, f32[8320]{0:T(1024)S(1)}, u32[]{:S(2)}, u32[]{:S(2)}) %collective-permute-start.6) | collective-permute-done | bytes 33312 | tf_op jit(solution)/shard_map/ppermute | solution.py:79
  21.5 1.6 %collective-permute-start.9 = (f32[8320]{0:T(1024)S(1)}, f32[8320]{0:T(1024)S(1)}, u32[]{:S(2)}, u32[]{:S(2)}) collective-permute-start(f32[8320]{0:T(1024)S(1)} %add.138), channel_id=1, source_target_pairs={{0,4},{1,5},{2,6},{3,7},{4,0},{5,1},{6,2},{7,3},{8,12},{9,13},{10,... | collective-permute-start | bytes 99848 | tf_op jit(solution)/shard_map/ppermute | solution.py:79
  23.1 1.5 %collective-permute-start.7 = (bf16[2,16,4096]{2,1,0:T(8,128)(2,1)S(1)}, bf16[2,16,4096]{2,1,0:T(8,128)(2,1)S(1)}, u32[]{:S(2)}, u32[]{:S(2)}) collective-permute-start(bf16[2,16,4096]{2,1,0:T(8,128)(2,1)S(1)} %bitcast_dynamic-update-slice_fusion.6), channel_id=1, source_target_pairs={{0,2},{1,3},{2,0},{3,1},{4,6},{5,7},{6,4},{7,5},{8,10},{9,11},{10,... | collective-permute-start | bytes 786440 | tf_op jit(solution)/shard_map/ppermute | solution.py:48
  24.7 0.6 %collective-permute-start.8 = (bf16[2,16,4096]{2,1,0:T(8,128)(2,1)S(1)}, bf16[2,16,4096]{2,1,0:T(8,128)(2,1)S(1)}, u32[]{:S(2)}, u32[]{:S(2)}) collective-permute-start(bf16[2,16,4096]{2,1,0:T(8,128)(2,1)S(1)} %bitcast_dynamic-update-slice_fusion.4), channel_id=1, source_target_pairs={{0,4},{1,5},{2,6},{3,7},{4,0},{5,1},{6,2},{7,3},{8,12},{9,13},{10,... | collective-permute-start | bytes 786440 | tf_op jit(solution)/shard_map/ppermute | solution.py:48
  25.3 0.7 %collective-permute-done.9 = f32[8320]{0:T(1024)S(1)} collective-permute-done((f32[8320]{0:T(1024)S(1)}, f32[8320]{0:T(1024)S(1)}, u32[]{:S(2)}, u32[]{:S(2)}) %collective-permute-start.9) | collective-permute-done | bytes 33312 | tf_op jit(solution)/shard_map/ppermute | solution.py:79
  26.0 1.1 %collective-permute-start.10 = (f32[8320]{0:T(1024)S(1)}, f32[8320]{0:T(1024)S(1)}, u32[]{:S(2)}, u32[]{:S(2)}) collective-permute-start(f32[8320]{0:T(1024)S(1)} %add.139), channel_id=1, source_target_pairs={{0,2},{1,3},{2,0},{3,1},{4,6},{5,7},{6,4},{7,5},{8,10},{9,11},{10,... | collective-permute-start | bytes 99848 | tf_op jit(solution)/shard_map/ppermute | solution.py:79
  27.1 2.8 %collective-permute-done.10 = f32[8320]{0:T(1024)S(1)} collective-permute-done((f32[8320]{0:T(1024)S(1)}, f32[8320]{0:T(1024)S(1)}, u32[]{:S(2)}, u32[]{:S(2)}) %collective-permute-start.10) | collective-permute-done | bytes 33312 | tf_op jit(solution)/shard_map/ppermute | solution.py:79
  30.0 1.1 %collective-permute-done.8 = bf16[2,16,4096]{2,1,0:T(8,128)(2,1)S(1)} collective-permute-done((bf16[2,16,4096]{2,1,0:T(8,128)(2,1)S(1)}, bf16[2,16,4096]{2,1,0:T(8,128)(2,1)S(1)}, u32[]{:S(2)}, u32[]{:S(2)}) %collective-permute-start.8) | collective-permute-done | bytes 262176 | tf_op jit(solution)/shard_map/ppermute | solution.py:48
  31.9 0.6 %collective-permute-done.12 = f32[8320]{0:T(1024)S(1)} collective-permute-done((f32[8320]{0:T(1024)S(1)}, f32[8320]{0:T(1024)S(1)}, u32[]{:S(2)}, u32[]{:S(2)}) %collective-permute-start.12) | collective-permute-done | bytes 33312 | tf_op jit(solution)/shard_map/ppermute | solution.py:79
  33.0 0.7 %fusion.20 = f32[8192]{0:T(1024)S(1)} fusion(f32[8320]{0:T(1024)S(1)} %add.141, f32[]{:T(128)} %bitcast.16), kind=kLoop, calls=%fused_computation.43 | loop fusion | flops 16384 | bytes 65540 | tf_op jit(solution)/shard_map/rsqrt | solution.py:170
  34.2 0.9 %fusion.4 = f32[256,128]{0,1:T(8,128)S(1)} fusion(bf16[256,8192]{1,0:T(8,128)(2,1)S(1)} %copy-done, bf16[128,8192]{1,0:T(8,128)(2,1)S(1)} %constant_dynamic-update-slice_fusion, f32[4096]{0:T(1024)S(1)} %get-tuple-element.39), kind=kOutput, calls=%fused_computation.8 | convolution fusion | flops 270008320 | bytes 3293184 | tf_op jit(solution)/shard_map/rk,qk->rq/dot_general | solution.py:120
  35.1 2.4 %fusion.7 = f32[256,128]{0,1:T(8,128)S(1)} fusion(bf16[256,8192]{1,0:T(8,128)(2,1)} %param.7, bf16[128,8192]{1,0:T(8,128)(2,1)S(1)} %constant_dynamic-update-slice_fusion, f32[4096]{0:T(1024)S(1)} %get-tuple-element.40), kind=kOutput, calls=%fused_computation.9 | convolution fusion | flops 270008320 | bytes 3293184 | tf_op jit(solution)/shard_map/rk,qk->rq/dot_general | solution.py:120
  38.0 9.7 %all_to_all.5 = bf16[8,48,128]{2,1,0:T(8,128)(2,1)S(1)} all-to-all(bf16[8,48,128]{2,1,0:T(8,128)(2,1)S(1)} %bitcast.55), channel_id=1, replica_groups=mesh['blk'=8,'harvest'=4] {'blk'}, dimensions={0} | all-to-all | bytes 196608 | tf_op jit(solution)/shard_map/all_to_all | solution.py:186
  47.7 0.6 %copy.28 = bf16[384,128]{1,0:T(8,128)(2,1)} copy(bf16[384,128]{1,0:T(8,128)(2,1)S(1)} %bitcast.54) | data formatting | bytes 196608
  (61 shorter events, 3.1 us)
Async XLA Ops:
  0.0 11.9 %collective-permute-start = (bf16[4,8192]{1,0:T(4,128)(2,1)}, bf16[4,8192]{1,0:T(4,128)(2,1)S(1)}, u32[]{:S(2)}, u32[]{:S(2)}) collective-permute-start(bf16[4,8192]{1,0:T(4,128)(2,1)} %param.10), channel_id=1, source_target_pairs={{0,8},{1,9},{2,10},{3,11},{4,12},{5,13},{6,14},{7,15},{8,16},{9,17... | collective-permute-start | bytes 196616 | tf_op jit(solution)/shard_map/ppermute | solution.py:48
  3.0 9.0 %collective-permute-start.1 = (bf16[4,8192]{1,0:T(4,128)(2,1)}, bf16[4,8192]{1,0:T(4,128)(2,1)S(1)}, u32[]{:S(2)}, u32[]{:S(2)}) collective-permute-start(bf16[4,8192]{1,0:T(4,128)(2,1)} %param.10), channel_id=1, source_target_pairs={{0,16},{1,17},{2,18},{3,19},{4,20},{5,21},{6,22},{7,23},{8,24},{9,... | collective-permute-start | bytes 196616 | tf_op jit(solution)/shard_map/ppermute | solution.py:48
  5.6 6.4 %collective-permute-start.2 = (bf16[4,8192]{1,0:T(4,128)(2,1)}, bf16[4,8192]{1,0:T(4,128)(2,1)S(1)}, u32[]{:S(2)}, u32[]{:S(2)}) collective-permute-start(bf16[4,8192]{1,0:T(4,128)(2,1)} %param.10), channel_id=1, source_target_pairs={{0,24},{1,25},{2,26},{3,27},{4,28},{5,29},{6,30},{7,31},{8,0},{9,1... | collective-permute-start | bytes 196616 | tf_op jit(solution)/shard_map/ppermute | solution.py:48
  7.0 3.4 %copy-start.2 = (f32[256]{0:T(256)S(1)}, f32[256]{0:T(256)}, u32[]{:S(2)}) copy-start(f32[256]{0:T(256)} %param.8) | copy-start | bytes 3076
  7.0 4.1 %copy-start.1 = (bf16[4,8192]{1,0:T(4,128)(2,1)S(1)}, bf16[4,8192]{1,0:T(4,128)(2,1)}, u32[]{:S(2)}) copy-start(bf16[4,8192]{1,0:T(4,128)(2,1)} %param.10) | copy-start | bytes 196612
  10.4 5.7 %copy-start.4 = (s32[256,1]{0,1:T(1,128)S(1)}, s32[256,1]{0,1:T(1,128)}, u32[]{:S(2)}) copy-start(s32[256,1]{0,1:T(1,128)} %param.9) | copy-start | bytes 3076
  10.4 5.8 %copy-start.3 = (s32[8,8]{1,0:T(8,128)S(1)}, s32[8,8]{1,0:T(8,128)}, u32[]{:S(2)}) copy-start(s32[8,8]{1,0:T(8,128)} %param.11) | copy-start | bytes 772
  12.2 4.3 %collective-permute-start.5 = (f32[8320]{0:T(1024)S(1)}, f32[8320]{0:T(1024)S(1)}, u32[]{:S(2)}, u32[]{:S(2)}) collective-permute-start(f32[8320]{0:T(1024)S(1)} %select_maximum_fusion), channel_id=1, source_target_pairs={{0,8},{1,9},{2,10},{3,11},{4,12},{5,13},{6,14},{7,15},{8,0},{9,1},... | collective-permute-start | bytes 99848 | tf_op jit(solution)/shard_map/ppermute | solution.py:79
  12.9 8.5 %collective-permute-start.4 = (bf16[16,4096]{1,0:T(8,128)(2,1)S(1)}, bf16[16,4096]{1,0:T(8,128)(2,1)S(1)}, u32[]{:S(2)}, u32[]{:S(2)}) collective-permute-start(bf16[16,4096]{1,0:T(8,128)(2,1)S(1)} %get-tuple-element.37), channel_id=1, source_target_pairs={{0,2},{1,3},{2,0},{3,1},{4,6},{5,7},{6,4},{7,5},{8,10},{9,11},{10,... | collective-permute-start | bytes 393224 | tf_op jit(solution)/shard_map/ppermute | solution.py:48
  14.5 7.0 %collective-permute-start.3 = (bf16[16,4096]{1,0:T(8,128)(2,1)S(1)}, bf16[16,4096]{1,0:T(8,128)(2,1)S(1)}, u32[]{:S(2)}, u32[]{:S(2)}) collective-permute-start(bf16[16,4096]{1,0:T(8,128)(2,1)S(1)} %get-tuple-element.38), channel_id=1, source_target_pairs={{0,4},{1,5},{2,6},{3,7},{4,0},{5,1},{6,2},{7,3},{8,12},{9,13},{10,... | collective-permute-start | bytes 393224 | tf_op jit(solution)/shard_map/ppermute | solution.py:48
  16.5 4.9 %collective-permute-start.6 = (f32[8320]{0:T(1024)S(1)}, f32[8320]{0:T(1024)S(1)}, u32[]{:S(2)}, u32[]{:S(2)}) collective-permute-start(f32[8320]{0:T(1024)S(1)} %add.137), channel_id=1, source_target_pairs={{0,16},{1,17},{2,18},{3,19},{4,20},{5,21},{6,22},{7,23},{8,24},{9,... | collective-permute-start | bytes 99848 | tf_op jit(solution)/shard_map/ppermute | solution.py:79
  21.5 4.5 %collective-permute-start.9 = (f32[8320]{0:T(1024)S(1)}, f32[8320]{0:T(1024)S(1)}, u32[]{:S(2)}, u32[]{:S(2)}) collective-permute-start(f32[8320]{0:T(1024)S(1)} %add.138), channel_id=1, source_target_pairs={{0,4},{1,5},{2,6},{3,7},{4,0},{5,1},{6,2},{7,3},{8,12},{9,13},{10,... | collective-permute-start | bytes 99848 | tf_op jit(solution)/shard_map/ppermute | solution.py:79
  23.1 6.8 %collective-permute-start.7 = (bf16[2,16,4096]{2,1,0:T(8,128)(2,1)S(1)}, bf16[2,16,4096]{2,1,0:T(8,128)(2,1)S(1)}, u32[]{:S(2)}, u32[]{:S(2)}) collective-permute-start(bf16[2,16,4096]{2,1,0:T(8,128)(2,1)S(1)} %bitcast_dynamic-update-slice_fusion.6), channel_id=1, source_target_pairs={{0,2},{1,3},{2,0},{3,1},{4,6},{5,7},{6,4},{7,5},{8,10},{9,11},{10,... | collective-permute-start | bytes 786440 | tf_op jit(solution)/shard_map/ppermute | solution.py:48
  24.7 6.4 %collective-permute-start.8 = (bf16[2,16,4096]{2,1,0:T(8,128)(2,1)S(1)}, bf16[2,16,4096]{2,1,0:T(8,128)(2,1)S(1)}, u32[]{:S(2)}, u32[]{:S(2)}) collective-permute-start(bf16[2,16,4096]{2,1,0:T(8,128)(2,1)S(1)} %bitcast_dynamic-update-slice_fusion.4), channel_id=1, source_target_pairs={{0,4},{1,5},{2,6},{3,7},{4,0},{5,1},{6,2},{7,3},{8,12},{9,13},{10,... | collective-permute-start | bytes 786440 | tf_op jit(solution)/shard_map/ppermute | solution.py:48
  26.0 4.0 %collective-permute-start.10 = (f32[8320]{0:T(1024)S(1)}, f32[8320]{0:T(1024)S(1)}, u32[]{:S(2)}, u32[]{:S(2)}) collective-permute-start(f32[8320]{0:T(1024)S(1)} %add.139), channel_id=1, source_target_pairs={{0,2},{1,3},{2,0},{3,1},{4,6},{5,7},{6,4},{7,5},{8,10},{9,11},{10,... | collective-permute-start | bytes 99848 | tf_op jit(solution)/shard_map/ppermute | solution.py:79
  31.2 2.9 %copy-start = (bf16[256,8192]{1,0:T(8,128)(2,1)S(1)}, bf16[256,8192]{1,0:T(8,128)(2,1)}, u32[]{:S(2)}) copy-start(bf16[256,8192]{1,0:T(8,128)(2,1)} %param.7) | copy-start | bytes 12582916
  31.2 1.3 %collective-permute-start.12 = (f32[8320]{0:T(1024)S(1)}, f32[8320]{0:T(1024)S(1)}, u32[]{:S(2)}, u32[]{:S(2)}) collective-permute-start(f32[8320]{0:T(1024)S(1)} %add.140), channel_id=1, source_target_pairs={{0,1},{1,0},{2,3},{3,2},{4,5},{5,4},{6,7},{7,6},{8,9},{9,8},{10,11... | collective-permute-start | bytes 99848 | tf_op jit(solution)/shard_map/ppermute | solution.py:79
  31.3 2.8 %collective-permute-start.11 = (bf16[64,8192]{1,0:T(8,128)(2,1)S(1)}, bf16[64,8192]{1,0:T(8,128)(2,1)S(1)}, u32[]{:S(2)}, u32[]{:S(2)}) collective-permute-start(bf16[64,8192]{1,0:T(8,128)(2,1)S(1)} %pad_maximum_fusion), channel_id=1, source_target_pairs={{0,1},{1,0},{2,3},{3,2},{4,5},{5,4},{6,7},{7,6},{8,9},{9,8},{10,11... | collective-permute-start | bytes 3145736 | tf_op jit(solution)/shard_map/ppermute | solution.py:114
